TPU v7x, 256 devices: a whole 4x4x8 slice. The times are simulated.
256 devices in a mesh: wide: 32 (over z, x), narrow: 8 (over y, core).
Axes of the slice: x: 4, y: 4, z: 8, core: 2. Of those that a mesh axis runs over, the one named last changes fastest.
Arguments:
- hidden_in: bfloat16 [64, 8192], P(None, 'wide'), may hold values from -6 to 6
- attn_gain: bfloat16 [8192], P('wide'), may hold values from 0.099609375 to 1.8984375
- qkv_weight: bfloat16 [8192, 8, 10, 128], P('wide', 'narrow'), may hold values from -2 to 2
- qkv_bias: bfloat16 [8, 10, 128], P('narrow'), may hold values from -3 to 3
- cache_keys: bfloat16 [64, 8, 4096, 128], P('wide', 'narrow'), may hold values from -256 to 256
- cache_values: bfloat16 [64, 8, 4096, 128], P('wide', 'narrow'), may hold values from -10 to 10
- positions: int32 [64, 3, 4096], P('wide'), may hold values from 0 to 4095
- lengths: int32 [64], P('wide'), may hold values from 512 to 4095, as said below
- out_weight: bfloat16 [8192, 8192], P('narrow', 'wide'), may hold values from -0.0625 to 0.0625
- mlp_gain: bfloat16 [8192], P('wide'), may hold values from 0.099609375 to 1.8984375
- gate_up_weight: bfloat16 [8192, 2, 29568], P('wide', None, 'narrow'), may hold values from -0.0625 to 0.0625
- down_weight: bfloat16 [29568, 8192], P('narrow', 'wide'), may hold values from -0.03125 to 0.03125
Outputs:
- layer_out: bfloat16 [64, 8192], P(None, 'wide')
Inputs may be any that keep to these rules, and one draw needn't show every extreme that they name: Slots 0 to lengths[b] - 1 of request b are filled, the new token takes slot lengths[b], and some request has 4095.
All inputs are finite; a program needn't handle non-finite values.
Results may differ from a plain program's by a relative error of at most 0.01115.
The roundings to bfloat16 on the way count: a program that leaves them out, or rounds other values in their place, can miss the bound.
Values may be sent and summed in bfloat16 or wider, within the bound.
No kernel may reach another device: no remote copies, remote signals or barrier semaphores. Data moves between devices by JAX's collectives and lax.ppermute only.
A program may use at most 64 MiB of HBM per device.

v0:
```python
import math

import jax
import jax.numpy as jnp
from jax import lax
from jax.sharding import PartitionSpec as P

D = 8192
DH = 128
CACHE = 4096


norm_eps = 1e-06
rope_base = 1000000.0


def mrope_tables(position):
    half_width = DH // 2
    pair_index = jnp.arange(half_width)
    inv_freq = jnp.exp(pair_index.astype(jnp.float32) * (-2.0 * math.log(rope_base) / DH))
    component = (pair_index >= DH // 8).astype(jnp.int32) + (
        pair_index >= DH // 8 + 3 * DH // 16
    ).astype(jnp.int32)
    pos_float = position.astype(jnp.float32)
    chosen = jnp.where(
        component == 0,
        pos_float[..., 0, :, None],
        jnp.where(component == 1, pos_float[..., 1, :, None], pos_float[..., 2, :, None]),
    )
    angles = chosen * inv_freq
    return (jnp.cos(angles), jnp.sin(angles))


def rotate(values, cosine, sine_table):
    half_width = values.shape[-1] // 2
    leading = values[..., :half_width]
    trailing = values[..., half_width:]
    return jnp.concatenate(
        [leading * cosine - trailing * sine_table, trailing * cosine + leading * sine_table],
        axis=-1,
    )


def local(
    hidden_in,
    attn_gain,
    qkv_weight,
    qkv_bias,
    cache_keys,
    cache_values,
    positions,
    lengths,
    out_weight,
    mlp_gain,
    gate_up_weight,
    down_weight,
):
    score_scale = 1.0 / math.sqrt(DH)
    owned = lengths.shape[0]
    local_rows = hidden_in.shape[1]
    kv_local = qkv_weight.shape[1]
    slot_count = qkv_weight.shape[2]
    group_size = slot_count - 2
    width = kv_local * slot_count * DH
    inputs = hidden_in.astype(jnp.float32)
    local_squares = jnp.sum(inputs * inputs, axis=1)
    scaled = (inputs * attn_gain.astype(jnp.float32)).astype(jnp.bfloat16)
    weight_flat = qkv_weight.reshape(local_rows, width)
    inv_rms = 1.0 / jnp.sqrt(lax.psum(local_squares, "wide") / D + norm_eps)
    row_block = scaled
    factor = inv_rms
    projected = lax.psum_scatter(
        factor[:, None] * jnp.dot(row_block, weight_flat, preferred_element_type=jnp.float32),
        "wide",
        scatter_dimension=0,
        tiled=True,
    )
    projected = projected + qkv_bias.reshape(width).astype(jnp.float32)
    projected = projected.reshape(owned, kv_local, slot_count, DH)
    cosine, sine_table = mrope_tables(positions)
    keys_rot = rotate(cache_keys.astype(jnp.float32), cosine[:, None], sine_table[:, None]).astype(
        jnp.bfloat16
    )
    new_position = jnp.take_along_axis(positions, lengths[:, None, None], axis=2)
    cos_new, sin_new = mrope_tables(new_position)
    query = rotate(projected[:, :, :group_size], cos_new[:, None], sin_new[:, None]).astype(
        jnp.bfloat16
    )
    key_new = rotate(projected[:, :, group_size], cos_new, sin_new).astype(jnp.bfloat16)
    value_new = projected[:, :, group_size + 1].astype(jnp.bfloat16)
    scores = (
        jnp.einsum("rgjd,rgsd->rgjs", query, keys_rot, preferred_element_type=jnp.float32)
        * score_scale
    )
    own_score = (
        jnp.sum(query.astype(jnp.float32) * key_new.astype(jnp.float32)[:, :, None, :], axis=3)
        * score_scale
    )
    valid_slot = jnp.arange(CACHE)[None, None, None, :] < lengths[:, None, None, None]
    row_max = jnp.maximum(jnp.max(jnp.where(valid_slot, scores, -jnp.inf), axis=3), own_score)
    probabilities = jnp.where(valid_slot, jnp.exp(scores - row_max[..., None]), 0.0)
    own_prob = jnp.exp(own_score - row_max)
    totals = jnp.sum(probabilities, axis=3) + own_prob
    probs_rounded = probabilities.astype(jnp.bfloat16)
    own_rounded = own_prob.astype(jnp.bfloat16).astype(jnp.float32)
    weighted = jnp.einsum(
        "rgjs,rgsd->rgjd", probs_rounded, cache_values, preferred_element_type=jnp.float32
    )
    weighted = weighted + own_rounded[..., None] * value_new.astype(jnp.float32)[:, :, None, :]
    attended = (
        (weighted / totals[..., None])
        .astype(jnp.bfloat16)
        .reshape(owned, kv_local * group_size * DH)
    )
    head_partial = jnp.dot(
        lax.all_gather(attended, "wide", axis=0, tiled=True),
        out_weight,
        preferred_element_type=jnp.float32,
    )
    attn_out = lax.psum(head_partial, "narrow")
    residual = (inputs + attn_out).astype(jnp.bfloat16)
    resid_float = residual.astype(jnp.float32)
    resid_squares = jnp.sum(resid_float * resid_float, axis=1)
    scaled2 = (resid_float * mlp_gain.astype(jnp.float32)).astype(jnp.bfloat16)
    hidden_local = gate_up_weight.shape[2]
    gate_up_flat = gate_up_weight.reshape(local_rows, 2 * hidden_local)
    inv_rms2 = 1.0 / jnp.sqrt(lax.psum(resid_squares, "wide") / D + norm_eps)
    row_block = scaled2
    factor = inv_rms2
    gate_up = lax.psum_scatter(
        factor[:, None] * jnp.dot(row_block, gate_up_flat, preferred_element_type=jnp.float32),
        "wide",
        scatter_dimension=0,
        tiled=True,
    )
    hidden = (jax.nn.silu(gate_up[:, :hidden_local]) * gate_up[:, hidden_local:]).astype(
        jnp.bfloat16
    )
    down_partial = jnp.dot(
        lax.all_gather(hidden, "wide", axis=0, tiled=True),
        down_weight,
        preferred_element_type=jnp.float32,
    )
    mlp_out = lax.psum(down_partial, "narrow")
    return (resid_float + mlp_out).astype(jnp.bfloat16)


def solution(mesh):
    in_specs = (
        P(None, "wide"),
        P("wide"),
        P("wide", "narrow", None, None),
        P("narrow", None, None),
        P("wide", "narrow", None, None),
        P("wide", "narrow", None, None),
        P("wide", None, None),
        P("wide"),
        P("narrow", "wide"),
        P("wide"),
        P("wide", None, "narrow"),
        P("narrow", "wide"),
    )
    out_specs = P(None, "wide")
    return jax.shard_map(local, mesh=mesh, in_specs=in_specs, out_specs=out_specs, check_vma=False)
```

profile of v0, /device:TPU:1, one launch (start us, length us, event | category | flops | bytes accessed | tf_op | source)
XLA Modules:
  0.0 690.4 jit_solution(1203411043637431055)
XLA Ops:
  6.5 1.5 copy.20
  8.0 0.9 fusion.24
  8.9 64.3 %psum.28 = f32[64]{0:T(128)S(1)} all-reduce(f32[64]{0:T(128)S(1)} %fusion.24), channel_id=1, replica_groups=mesh['wide'=32,'narrow'=8] {'wide'}, use_global_device_ids=true, to_apply=%region_1.0 | all-reduce | flops 64 | bytes 512 | tf_op jit(solution)/shard_map/psum | solution.py:69
  73.9 1.8 convolution_multiply_fusion.2
  75.8 0.9 convert_element_type.179
  76.8 3.4 copy.22
  80.3 3.8 bitcast_convert_fusion
  84.4 1.4 gather_fusion
  86.2 19.8 %fusion.7 = (bf16[2,4096,64]{2,1,0:T(8,128)(2,1)}, bf16[2,4096,64]{2,1,0:T(8,128)(2,1)}) fusion(f32[2,1,4096,128]{3,2,0,1:T(8,128)} %bitcast_convert_fusion, f32[64]{0:T(128)S(1)} %multiply_exponential_fusion, f32[2,4096]{1,0:T(2,128)S(1)} %get-tuple-element.17, f32[2,4096]{1,0:T(2,128)S(1)} %get-tuple-element.18, f32[2,4096]{1,0:T(2,128)S(1)} %get-tuple-element.16, ...), kind=kLoop, calls=%fused_computation.15 | loop fusion | flops 5767168 | bytes 6390144 | tf_op jit(solution)/shard_map/concatenate | solution.py:38
  107.5 119.1 %all-reduce.11.cloned.1.call-done = f32[64,1280]{1,0:T(8,128)} async-done(((f32[64,1280]{1,0:T(8,128)}), f32[64,1280]{1,0:T(8,128)}) %all-reduce.11.cloned.1.call-update) | async-done | bytes 327696
  226.5 0.8 dynamic-slice_add_fusion
  227.8 3.6 select_reduce_fusion
  232.1 32.4 %all-gather = bf16[32,2,1024]{2,1,0:T(2,128)(2,1)S(1)} all-gather(bf16[1,2,1024]{2,1,0:T(2,128)(2,1)S(1)} %reshape.655), channel_id=1, replica_groups=mesh['wide'=32,'narrow'=8] {'wide'}, dimensions={0}, use_global_device_ids=true | all-gather | bytes 135168 | tf_op jit(solution)/shard_map/all_gather | solution.py:116
  264.5 0.8 fusion.52
  265.4 74.6 %all-reduce.7.cloned.1.call-done = f32[64,256]{1,0:T(8,128)} async-done(((f32[64,256]{1,0:T(8,128)}), f32[64,256]{1,0:T(8,128)}) %all-reduce.7.cloned.1.call-update) | async-done | bytes 65552 | tf_op jit(solution)/shard_map/psum | solution.py:120
  340.0 0.9 fusion.27
  341.0 61.2 %psum.30 = f32[64]{0:T(128)S(1)} all-reduce(f32[64]{0:T(128)S(1)} %get-tuple-element.8), channel_id=1, replica_groups=mesh['wide'=32,'narrow'=8] {'wide'}, use_global_device_ids=true, to_apply=%region_8.9 | all-reduce | flops 64 | bytes 512 | tf_op jit(solution)/shard_map/psum | solution.py:127
  402.2 4.6 convolution_multiply_fusion
  406.8 158.8 %all-reduce.13.cloned.1.call-done = f32[64,7392]{1,0:T(8,128)} async-done(((f32[64,7392]{1,0:T(8,128)}), f32[64,7392]{1,0:T(8,128)}) %all-reduce.13.cloned.1.call-update) | async-done | bytes 1892368
  565.6 1.1 fusion.36
  566.7 36.6 %all-gather.1 = bf16[32,2,3696]{2,1,0:T(2,128)(2,1)S(1)} all-gather(bf16[1,2,3696]{2,1,0:T(2,128)(2,1)S(1)} %fusion.36), channel_id=1, replica_groups=mesh['wide'=32,'narrow'=8] {'wide'}, dimensions={0}, use_global_device_ids=true | all-gather | bytes 487872 | tf_op jit(solution)/shard_map/all_gather | solution.py:140
  603.7 2.6 fusion.53
  606.3 76.0 %all-reduce.9.cloned.1.call-done = f32[64,256]{1,0:T(8,128)} async-done(((f32[64,256]{1,0:T(8,128)}), f32[64,256]{1,0:T(8,128)}) %all-reduce.9.cloned.1.call-update) | async-done | bytes 65552 | tf_op jit(solution)/shard_map/psum | solution.py:144
  682.4 1.5 fusion.29
  (57 shorter events, 4.0 us)
Async XLA Ops:
  6.5 225.1 %copy-start = (bf16[2,1,4096,128]{3,2,1,0:T(8,128)(2,1)S(1)}, bf16[2,1,4096,128]{3,2,1,0:T(8,128)(2,1)}, u32[]{:S(2)}) copy-start(bf16[2,1,4096,128]{3,2,1,0:T(8,128)(2,1)} %param.17) | copy-start | bytes 6291460
  6.5 73.6 %copy-start.4 = (s32[2]{0:T(128)S(1)}, s32[2]{0:T(128)}, u32[]{:S(2)}) copy-start(s32[2]{0:T(128)} %param.19) | copy-start | bytes 28
  6.5 220.0 %all-reduce.11.cloned.1.call-start = ((), (), s32[]{:S(2)}) async-start(), calls=%async_computation.2 | async-start | bytes 655360
  75.7 264.3 %all-reduce.7.cloned.1.call-start = ((), (), s32[]{:S(2)}) async-start(), calls=%async_computation | async-start | bytes 131072 | tf_op jit(solution)/shard_map/psum | solution.py:120
  86.2 20.0 %copy-start.6 = (u32[256]{0:T(256)S(1)}, u32[256]{0:T(256)}, u32[]{:S(2)}) copy-start(u32[256]{0:T(256)} %constant.61) | copy-start | bytes 3076
  86.2 21.2 %copy-start.3 = (bf16[1,10,128]{2,1,0:T(8,128)(2,1)S(1)}, bf16[1,10,128]{2,1,0:T(8,128)(2,1)}, u32[]{:S(2)}) copy-start(bf16[1,10,128]{2,1,0:T(8,128)(2,1)} %param.15) | copy-start | bytes 7684
  227.7 36.8 %copy-start.1 = (bf16[1024,256]{1,0:T(8,128)(2,1)S(1)}, bf16[1024,256]{1,0:T(8,128)(2,1)}, u32[]{:S(2)}) copy-start(bf16[1024,256]{1,0:T(8,128)(2,1)} %param.20) | copy-start | bytes 1572868
  227.7 37.7 %copy-start.5 = (bf16[256]{0:T(256)(128)(2,1)S(1)}, bf16[256]{0:T(256)(128)(2,1)}, u32[]{:S(2)}) copy-start(bf16[256]{0:T(256)(128)(2,1)} %param.21) | copy-start | bytes 1540
  227.8 112.3 %copy-start.2 = (bf16[64,256]{1,0:T(8,128)(2,1)S(1)}, bf16[64,256]{1,0:T(8,128)(2,1)}, u32[]{:S(2)}) copy-start(bf16[64,256]{1,0:T(8,128)(2,1)} %param.12) | copy-start | bytes 98308
  265.4 300.3 %all-reduce.13.cloned.1.call-start = ((), (), s32[]{:S(2)}) async-start(), calls=%async_computation.3 | async-start | bytes 3801088
  406.8 275.6 %all-reduce.9.cloned.1.call-start = ((), (), s32[]{:S(2)}) async-start(), calls=%async_computation.1 | async-start | bytes 131072 | tf_op jit(solution)/shard_map/psum | solution.py:144
Sparse Core Ops, SparseCore 0:
  75.9 150.6 all-reduce.10
  265.5 74.4 all-reduce.6
  406.9 158.6 all-reduce.12
  606.5 75.8 all-reduce.8
where the time goes:
time: 692 us; the launch traced here: 690 us
  waiting for transfers between devices  429 us (62%)
  blocking collectives  194 us (28%)
  other arithmetic  31.6 us (5%)
  between operations  14 us (2%)
  matrix products  13.9 us (2%)
  local copies, waits for them, and re-layouts  7.72 us (1%)
    unnamed x6, waiting for transfers between devices  278 us
    psum x1, waiting for transfers between devices, local(): mlp_out = lax.psum(down_partial, 'narrow')  76 us
    psum x1, waiting for transfers between devices, local(): attn_out = lax.psum(head_partial, 'narrow')  74.6 us
    psum x1, blocking collectives, local(): inv_rms = 1.0 / jnp.sqrt(lax.psum(local_squares, 'wide') / D + norm_eps)  64.3 us
    psum x1, blocking collectives, local(): inv_rms2 = 1.0 / jnp.sqrt(lax.psum(resid_squares, 'wide') / D + norm_eps)  61.2 us
    all_gather x1, blocking collectives, local(): lax.all_gather(hidden, 'wide', axis=0, tiled=True)  36.6 us
    all_gather x1, blocking collectives, local(): lax.all_gather(attended, 'wide', axis=0, tiled=True)  32.4 us
    concatenate x2, other arithmetic, rotate(): jnp.concatenate([leading * cosine - trailing * sine_table, trailing * cos...  19.8 us
  transfers between devices with their start and end apart: 4, of which 4 were waited for; matrix products, arithmetic and copies ran while one was open for 4% of the time, Pallas kernels for 0%

commit v1 on v0

--- a/solution.py
+++ b/solution.py
@@ -66,16 +66,15 @@
     local_squares = jnp.sum(inputs * inputs, axis=1)
     scaled = (inputs * attn_gain.astype(jnp.float32)).astype(jnp.bfloat16)
     weight_flat = qkv_weight.reshape(local_rows, width)
-    inv_rms = 1.0 / jnp.sqrt(lax.psum(local_squares, "wide") / D + norm_eps)
-    row_block = scaled
-    factor = inv_rms
-    projected = lax.psum_scatter(
-        factor[:, None] * jnp.dot(row_block, weight_flat, preferred_element_type=jnp.float32),
+    partial = jnp.dot(scaled, weight_flat, preferred_element_type=jnp.float32)
+    summed = lax.psum_scatter(
+        jnp.concatenate([partial, local_squares[:, None]], axis=1),
         "wide",
         scatter_dimension=0,
         tiled=True,
     )
-    projected = projected + qkv_bias.reshape(width).astype(jnp.float32)
+    inv_rms = 1.0 / jnp.sqrt(summed[:, width] / D + norm_eps)
+    projected = inv_rms[:, None] * summed[:, :width] + qkv_bias.reshape(width).astype(jnp.float32)
     projected = projected.reshape(owned, kv_local, slot_count, DH)
     cosine, sine_table = mrope_tables(positions)
     keys_rot = rotate(cache_keys.astype(jnp.float32), cosine[:, None], sine_table[:, None]).astype(
@@ -124,23 +123,14 @@
     scaled2 = (resid_float * mlp_gain.astype(jnp.float32)).astype(jnp.bfloat16)
     hidden_local = gate_up_weight.shape[2]
     gate_up_flat = gate_up_weight.reshape(local_rows, 2 * hidden_local)
-    inv_rms2 = 1.0 / jnp.sqrt(lax.psum(resid_squares, "wide") / D + norm_eps)
-    row_block = scaled2
-    factor = inv_rms2
-    gate_up = lax.psum_scatter(
-        factor[:, None] * jnp.dot(row_block, gate_up_flat, preferred_element_type=jnp.float32),
-        "wide",
-        scatter_dimension=0,
-        tiled=True,
-    )
+    partial2 = jnp.dot(scaled2, gate_up_flat, preferred_element_type=jnp.float32)
+    summed2 = lax.psum(jnp.concatenate([partial2, resid_squares[:, None]], axis=1), "wide")
+    inv_rms2 = 1.0 / jnp.sqrt(summed2[:, 2 * hidden_local] / D + norm_eps)
+    gate_up = summed2[:, : 2 * hidden_local] * inv_rms2[:, None]
     hidden = (jax.nn.silu(gate_up[:, :hidden_local]) * gate_up[:, hidden_local:]).astype(
         jnp.bfloat16
     )
-    down_partial = jnp.dot(
-        lax.all_gather(hidden, "wide", axis=0, tiled=True),
-        down_weight,
-        preferred_element_type=jnp.float32,
-    )
+    down_partial = jnp.dot(hidden, down_weight, preferred_element_type=jnp.float32)
     mlp_out = lax.psum(down_partial, "narrow")
     return (resid_float + mlp_out).astype(jnp.bfloat16)
 

time: 692 us -> 507 us (0.73)
  blocking collectives: 194 us -> 31.3 us
  waiting for transfers between devices: 429 us -> 406 us
    unnamed x6 -> x5, waiting for transfers between devices: 278 us -> 116 us
    psum x0 -> x1, waiting for transfers between devices: none -> 150 us  [local(): lax.psum(jnp.concatenate([partial2, resid_squares[:, None]], axis=1), 'wi...]
    psum x2 -> x0, blocking collectives: 125 us -> none  [the longest x1 64.3 us: local(): inv_rms = 1.0 / jnp.sqrt(lax.psum(local_squares, 'wide') / D + norm_eps)]
    all_gather x1 -> x0, blocking collectives: 36.6 us -> none  [local(): lax.all_gather(hidden, 'wide', axis=0, tiled=True)]
    psum x1, waiting for transfers between devices: 76 us -> 64.5 us  [local(): mlp_out = lax.psum(down_partial, 'narrow')]
  transfers between devices with their start and end apart: 4 -> 4, of which waited for: 4 -> 4; matrix products, arithmetic and copies ran while one was open for 4% -> 6% of each run, Pallas kernels for 0% -> 0%
where the time goes in v1:
time: 507 us; the launch traced here: 505 us
  waiting for transfers between devices  406 us (80%)
  other arithmetic  35.7 us (7%)
  blocking collectives  31.3 us (6%)
  between operations  14 us (3%)
  matrix products  10.4 us (2%)
  local copies, waits for them, and re-layouts  6.65 us (1%)
    psum x1, waiting for transfers between devices, local(): lax.psum(jnp.concatenate([partial2, resid_squares[:, None]], axis=1), 'wi...  150 us
    unnamed x5, waiting for transfers between devices  116 us
    psum x1, waiting for transfers between devices, local(): attn_out = lax.psum(head_partial, 'narrow')  75.3 us
    psum x1, waiting for transfers between devices, local(): mlp_out = lax.psum(down_partial, 'narrow')  64.5 us
    all_gather x1, blocking collectives, local(): lax.all_gather(attended, 'wide', axis=0, tiled=True)  31.3 us
    concatenate x2, other arithmetic, rotate(): jnp.concatenate([leading * cosine - trailing * sine_table, trailing * cos...  19.8 us
  transfers between devices with their start and end apart: 4, of which 4 were waited for; matrix products, arithmetic and copies ran while one was open for 6% of the time, Pallas kernels for 0%

profile of v1, /device:TPU:1, one launch (start us, length us, event | category | flops | bytes accessed | tf_op | source)
XLA Modules:
  0.0 504.7 jit_solution(6786295929845901364)
XLA Ops:
  6.5 1.0 fusion.28
  7.7 1.3 copy.24
  9.7 1.1 fusion.35
  10.8 0.8 pad_maximum_fusion.1
  11.7 2.7 copy.27
  14.5 3.8 bitcast_convert_fusion
  18.6 1.4 gather_fusion
  20.4 19.8 %fusion.7 = (bf16[2,4096,64]{2,1,0:T(8,128)(2,1)}, bf16[2,4096,64]{2,1,0:T(8,128)(2,1)}) fusion(f32[2,1,4096,128]{3,2,0,1:T(8,128)} %bitcast_convert_fusion, f32[64]{0:T(128)S(1)} %multiply_exponential_fusion, f32[2,4096]{1,0:T(2,128)S(1)} %get-tuple-element.17, f32[2,4096]{1,0:T(2,128)S(1)} %get-tuple-element.18, f32[2,4096]{1,0:T(2,128)S(1)} %get-tuple-element.16, ...), kind=kLoop, calls=%fused_computation.13 | loop fusion | flops 5767168 | bytes 6390144 | tf_op jit(solution)/shard_map/concatenate | solution.py:38
  41.7 116.3 %all-reduce.12.cloned.1.call-done = f32[64,1281]{1,0:T(8,128)} async-done(((f32[64,1281]{1,0:T(8,128)}), f32[64,1281]{1,0:T(8,128)}) %all-reduce.12.cloned.1.call-update) | async-done | bytes 327952
  157.9 0.9 fusion.50
  158.8 0.9 fusion.42
  160.1 3.6 select_reduce_fusion
  164.3 31.3 %all-gather = bf16[32,2,1024]{2,1,0:T(2,128)(2,1)S(1)} all-gather(bf16[1,2,1024]{2,1,0:T(2,128)(2,1)S(1)} %reshape.653), channel_id=1, replica_groups=mesh['wide'=32,'narrow'=8] {'wide'}, dimensions={0}, use_global_device_ids=true | all-gather | bytes 135168 | tf_op jit(solution)/shard_map/all_gather | solution.py:115
  195.7 0.8 fusion.62
  196.7 75.3 %all-reduce.6.cloned.1.call-done = f32[64,256]{1,0:T(8,128)} async-done(((f32[64,256]{1,0:T(8,128)}), f32[64,256]{1,0:T(8,128)}) %all-reduce.6.cloned.1.call-update) | async-done | bytes 65552 | tf_op jit(solution)/shard_map/psum | solution.py:119
  272.0 0.9 fusion.31
  273.0 3.4 fusion.33
  276.4 1.4 pad_maximum_fusion
  277.8 150.4 %all-reduce.8.cloned.1.call-done = f32[64,7393]{1,0:T(8,128)} async-done(((f32[64,7393]{1,0:T(8,128)}), f32[64,7393]{1,0:T(8,128)}) %all-reduce.8.cloned.1.call-update) | async-done | bytes 1892624 | tf_op jit(solution)/shard_map/psum | solution.py:127
  428.2 1.1 fusion.39
  429.3 1.7 slice_multiply_fusion
  431.0 1.2 fusion.19
  432.2 64.5 %all-reduce.10.cloned.1.call-done = f32[64,256]{1,0:T(8,128)} async-done(((f32[64,256]{1,0:T(8,128)}), f32[64,256]{1,0:T(8,128)}) %all-reduce.10.cloned.1.call-update) | async-done | bytes 65552 | tf_op jit(solution)/shard_map/psum | solution.py:134
  496.7 1.5 fusion.32
  (61 shorter events, 3.8 us)
Async XLA Ops:
  6.5 157.3 %copy-start = (bf16[2,1,4096,128]{3,2,1,0:T(8,128)(2,1)S(1)}, bf16[2,1,4096,128]{3,2,1,0:T(8,128)(2,1)}, u32[]{:S(2)}) copy-start(bf16[2,1,4096,128]{3,2,1,0:T(8,128)(2,1)} %param.17) | copy-start | bytes 6291460
  6.5 5.1 %copy-start.2 = (s32[2,3,4096]{2,0,1:T(2,128)S(1)}, s32[2,3,4096]{2,0,1:T(2,128)}, u32[]{:S(2)}) copy-start(s32[2,3,4096]{2,0,1:T(2,128)} %param.18) | copy-start | bytes 294916
  6.5 151.4 %all-reduce.12.cloned.1.call-start = ((), (), s32[]{:S(2)}) async-start(), calls=%async_computation.3 | async-start | bytes 720896
  11.6 260.4 %all-reduce.6.cloned.1.call-start = ((), (), s32[]{:S(2)}) async-start(), calls=%async_computation | async-start | bytes 131072 | tf_op jit(solution)/shard_map/psum | solution.py:119
  11.7 2.7 copy-start.5
  20.4 20.0 %copy-start.8 = (u32[256]{0:T(256)S(1)}, u32[256]{0:T(256)}, u32[]{:S(2)}) copy-start(u32[256]{0:T(256)} %constant.64) | copy-start | bytes 3076
  20.4 21.2 %copy-start.4 = (bf16[1,10,128]{2,1,0:T(8,128)(2,1)S(1)}, bf16[1,10,128]{2,1,0:T(8,128)(2,1)}, u32[]{:S(2)}) copy-start(bf16[1,10,128]{2,1,0:T(8,128)(2,1)} %param.15) | copy-start | bytes 7684
  163.6 32.1 %copy-start.1 = (bf16[1024,256]{1,0:T(8,128)(2,1)S(1)}, bf16[1024,256]{1,0:T(8,128)(2,1)}, u32[]{:S(2)}) copy-start(bf16[1024,256]{1,0:T(8,128)(2,1)} %param.20) | copy-start | bytes 1572868
  163.6 33.0 %copy-start.7 = (bf16[256]{0:T(256)(128)(2,1)S(1)}, bf16[256]{0:T(256)(128)(2,1)}, u32[]{:S(2)}) copy-start(bf16[256]{0:T(256)(128)(2,1)} %param.21) | copy-start | bytes 1540
  163.6 108.3 %copy-start.3 = (bf16[64,256]{1,0:T(8,128)(2,1)S(1)}, bf16[64,256]{1,0:T(8,128)(2,1)}, u32[]{:S(2)}) copy-start(bf16[64,256]{1,0:T(8,128)(2,1)} %param.12) | copy-start | bytes 98308
  196.6 231.6 %all-reduce.8.cloned.1.call-start = ((), (), s32[]{:S(2)}) async-start(), calls=%async_computation.1 | async-start | bytes 3801088 | tf_op jit(solution)/shard_map/psum | solution.py:127
  277.8 218.9 %all-reduce.10.cloned.1.call-start = ((), (), s32[]{:S(2)}) async-start(), calls=%async_computation.2 | async-start | bytes 131072 | tf_op jit(solution)/shard_map/psum | solution.py:134
  428.2 2.8 copy-start.6
Sparse Core Ops, SparseCore 0:
  11.7 146.1 all-reduce.11
  196.7 75.2 all-reduce.5
  277.9 150.2 all-reduce.7
  432.3 64.3 all-reduce.9

commit v2 on v1

--- a/solution.py
+++ b/solution.py
@@ -41,6 +41,27 @@
     )
 
 
+def reduce_rows(x, axis):
+    n = lax.axis_size(axis)
+    blocks = x.reshape(n, x.shape[0] // n, x.shape[1])
+    return jnp.sum(lax.all_to_all(blocks, axis, 0, 0, tiled=False), axis=0)
+
+
+def gather_rows(x, axis):
+    n = lax.axis_size(axis)
+    copies = jnp.broadcast_to(x[None], (n,) + x.shape)
+    return lax.all_to_all(copies, axis, 0, 0, tiled=False).reshape(n * x.shape[0], x.shape[1])
+
+
+def sum_all(x, axis):
+    n = lax.axis_size(axis)
+    step = 1
+    while step < n:
+        x = x + lax.ppermute(x, axis, [(i, i ^ step) for i in range(n)])
+        step *= 2
+    return x
+
+
 def local(
     hidden_in,
     attn_gain,
@@ -67,12 +88,7 @@
     scaled = (inputs * attn_gain.astype(jnp.float32)).astype(jnp.bfloat16)
     weight_flat = qkv_weight.reshape(local_rows, width)
     partial = jnp.dot(scaled, weight_flat, preferred_element_type=jnp.float32)
-    summed = lax.psum_scatter(
-        jnp.concatenate([partial, local_squares[:, None]], axis=1),
-        "wide",
-        scatter_dimension=0,
-        tiled=True,
-    )
+    summed = reduce_rows(jnp.concatenate([partial, local_squares[:, None]], axis=1), "wide")
     inv_rms = 1.0 / jnp.sqrt(summed[:, width] / D + norm_eps)
     projected = inv_rms[:, None] * summed[:, :width] + qkv_bias.reshape(width).astype(jnp.float32)
     projected = projected.reshape(owned, kv_local, slot_count, DH)
@@ -112,11 +128,11 @@
         .reshape(owned, kv_local * group_size * DH)
     )
     head_partial = jnp.dot(
-        lax.all_gather(attended, "wide", axis=0, tiled=True),
+        gather_rows(attended, "wide"),
         out_weight,
         preferred_element_type=jnp.float32,
     )
-    attn_out = lax.psum(head_partial, "narrow")
+    attn_out = sum_all(head_partial, "narrow")
     residual = (inputs + attn_out).astype(jnp.bfloat16)
     resid_float = residual.astype(jnp.float32)
     resid_squares = jnp.sum(resid_float * resid_float, axis=1)
@@ -124,14 +140,14 @@
     hidden_local = gate_up_weight.shape[2]
     gate_up_flat = gate_up_weight.reshape(local_rows, 2 * hidden_local)
     partial2 = jnp.dot(scaled2, gate_up_flat, preferred_element_type=jnp.float32)
-    summed2 = lax.psum(jnp.concatenate([partial2, resid_squares[:, None]], axis=1), "wide")
+    summed2 = reduce_rows(jnp.concatenate([partial2, resid_squares[:, None]], axis=1), "wide")
     inv_rms2 = 1.0 / jnp.sqrt(summed2[:, 2 * hidden_local] / D + norm_eps)
     gate_up = summed2[:, : 2 * hidden_local] * inv_rms2[:, None]
     hidden = (jax.nn.silu(gate_up[:, :hidden_local]) * gate_up[:, hidden_local:]).astype(
         jnp.bfloat16
     )
-    down_partial = jnp.dot(hidden, down_weight, preferred_element_type=jnp.float32)
-    mlp_out = lax.psum(down_partial, "narrow")
+    down_partial = jnp.dot(gather_rows(hidden, "wide"), down_weight, preferred_element_type=jnp.float32)
+    mlp_out = sum_all(down_partial, "narrow")
     return (resid_float + mlp_out).astype(jnp.bfloat16)
 
 

time: 507 us -> 171 us (0.34)
  waiting for transfers between devices: 406 us -> 8.86 us
  blocking collectives: 31.3 us -> 85.5 us
  starting transfers between devices: 0.13 us -> 28.1 us
  between operations: 14 us -> 0.32 us
  other arithmetic: 35.7 us -> 27.1 us
    psum x3 -> x0, waiting for transfers between devices: 290 us -> none  [the longest x1 150 us: local(): lax.psum(jnp.concatenate([partial2, resid_squares[:, None]], axis=1), 'wi...]
    unnamed x5 -> x0, waiting for transfers between devices: 116 us -> none
    all_to_all x0 -> x3, blocking collectives: none -> 85.5 us  [the longest x1 47 us: reduce_rows(): return jnp.sum(lax.all_to_all(blocks, axis, 0, 0, tiled=False), axis=0)]
    all_gather x1 -> x0, blocking collectives: 31.3 us -> none  [local(): lax.all_gather(attended, 'wide', axis=0, tiled=True)]
    ppermute x0 -> x6, starting transfers between devices: none -> 16.2 us  [sum_all(): x = x + lax.ppermute(x, axis, [(i, i ^ step) for i in range(n)])]
    all_to_all x0 -> x1, starting transfers between devices: none -> 11.9 us  [reduce_rows(): return jnp.sum(lax.all_to_all(blocks, axis, 0, 0, tiled=False), axis=0)]
    ppermute x0 -> x6, waiting for transfers between devices: none -> 8.85 us  [sum_all(): x = x + lax.ppermute(x, axis, [(i, i ^ step) for i in range(n)])]
  transfers between devices with their start and end apart: 4 -> 7, of which waited for: 4 -> 6; matrix products, arithmetic and copies ran while one was open for 6% -> 15% of each run, Pallas kernels for 0% -> 0%
where the time goes in v2:
time: 171 us; the launch traced here: 170 us
  blocking collectives  85.5 us (50%)
  starting transfers between devices  28.1 us (16%)
  other arithmetic  27.1 us (16%)
  local copies, waits for them, and re-layouts  9.98 us (6%)
  matrix products  9.85 us (6%)
  waiting for transfers between devices  8.86 us (5%)
    all_to_all x1, blocking collectives, reduce_rows(): return jnp.sum(lax.all_to_all(blocks, axis, 0, 0, tiled=False), axis=0)  47 us
    all_to_all x2, blocking collectives, gather_rows(): lax.all_to_all(copies, axis, 0, 0, tiled=False)  38.5 us
    concatenate x2, other arithmetic, rotate(): jnp.concatenate([leading * cosine - trailing * sine_table, trailing * cos...  18.7 us
    ppermute x6, starting transfers between devices, sum_all(): x = x + lax.ppermute(x, axis, [(i, i ^ step) for i in range(n)])  16.2 us
    all_to_all x1, starting transfers between devices, reduce_rows(): return jnp.sum(lax.all_to_all(blocks, axis, 0, 0, tiled=False), axis=0)  11.9 us
    ppermute x6, waiting for transfers between devices, sum_all(): x = x + lax.ppermute(x, axis, [(i, i ^ step) for i in range(n)])  8.85 us
    unnamed x18, local copies, waits for them, and re-layouts  4.04 us
    dot_general x1, matrix products, local(): jnp.einsum('rgjd,rgsd->rgjs', query, keys_rot, preferred_element_type=jnp...  3.56 us
  transfers between devices with their start and end apart: 7, of which 6 were waited for; matrix products, arithmetic and copies ran while one was open for 15% of the time, Pallas kernels for 0%

profile of v2, /device:TPU:1, one launch (start us, length us, event | category | flops | bytes accessed | tf_op | source)
XLA Modules:
  0.0 169.7 jit_solution(6719630208540436073)
XLA Ops:
  2.1 1.4 copy.46
  4.9 11.9 %all-to-all-start = ((f32[32,2,1281]{2,1,0:T(2,128)}), f32[32,2,1281]{2,1,0:T(2,128)S(1)}, u32[]{:S(2)}, u32[]{:S(2)}) async-start(f32[32,2,1281]{2,1,0:T(2,128)} %copy.50), calls=%async_computation | async-start | bytes 720896 | tf_op jit(solution)/shard_map/all_to_all | solution.py:47
  16.9 2.6 %copy.53 = s32[2,3,4096]{1,2,0:T(8,128)} copy(s32[2,3,4096]{2,0,1:T(2,128)S(1)} %copy-done.2) | data formatting | bytes 196608 | tf_op args[6]
  19.8 1.5 gather_fusion
  21.8 1.9 %bitcast_convert_fusion = f32[2,1,4096,128]{3,2,0,1:T(8,128)S(1)} fusion(bf16[2,1,4096,128]{3,2,1,0:T(8,128)(2,1)} %param.16), kind=kLoop, calls=%fused_computation.12 | loop fusion | flops 1048576 | bytes 6291456 | tf_op jit(solution)/shard_map/convert_element_type | solution.py:96
  23.8 18.6 %fusion.7 = (bf16[2,4096,64]{2,1,0:T(8,128)(2,1)}, bf16[2,4096,64]{2,1,0:T(8,128)(2,1)}) fusion(f32[2,1,4096,128]{3,2,0,1:T(8,128)S(1)} %bitcast_convert_fusion, f32[64]{0:T(128)S(1)} %multiply_exponential_fusion, f32[2,4096]{1,0:T(2,128)S(1)} %get-tuple-element.17, f32[2,4096]{1,0:T(2,128)S(1)} %get-tuple-element.18, f32[2,4096]{1,0:T(2,128)S(1)} %get-tuple-element.16, ...), kind=kLoop, calls=%fused_computation.13 | loop fusion | flops 5767168 | bytes 6390144 | tf_op jit(solution)/shard_map/concatenate | solution.py:38
  43.2 3.6 %select_reduce_fusion = (f32[2,8]{1,0:T(2,128)S(1)}, f32[2,8,4096]{2,1,0:T(8,128)S(1)}) fusion(pred[2,4096]{1,0:T(4,128)(4,1)S(1)} %iota_compare_fusion, bf16[2,4096,64]{2,1,0:T(8,128)(2,1)} %get-tuple-element.15, bf16[2,4096,64]{2,1,0:T(8,128)(2,1)} %get-tuple-element.14, bf16[2,8,64]{2,1,0:T(8,128)(2,1)S(1)} %bitcast.61, bf16[2,8,64]{2,1,0:T(8,128)(2,1)S(1)} %bitcast.60), kind=kOutput, calls=%fused_computation.22 | convolution fusion | flops 21176304 | bytes 2371648 | tf_op jit(solution)/shard_map/rgjd,rgsd->rgjs/dot_general | solution.py:107
  47.6 18.4 %all_to_all.20 = bf16[32,2,1024]{2,1,0:T(2,128)(2,1)S(1)} all-to-all(bf16[32,2,1024]{2,1,0:T(2,128)(2,1)S(1)} %broadcast_in_dim.168), channel_id=1, replica_groups=mesh['wide'=32,'narrow'=8] {'wide'}, dimensions={0} | all-to-all | bytes 262144 | tf_op jit(solution)/shard_map/all_to_all | solution.py:53
  66.2 2.8 %collective-permute-start = (f32[64,256]{1,0:T(8,128)S(1)}, f32[64,256]{1,0:T(8,128)S(1)}, u32[]{:S(2)}, u32[]{:S(2)}) collective-permute-start(f32[64,256]{1,0:T(8,128)S(1)} %fusion.61), channel_id=1, source_target_pairs={{0,1},{1,0},{2,3},{3,2},{4,5},{5,4},{6,7},{7,6},{8,9},{9,8},{10,11... | collective-permute-start | bytes 196616 | tf_op jit(solution)/shard_map/ppermute | solution.py:60
  69.9 1.4 collective-permute-start.1
  71.3 1.8 %collective-permute-done.1 = f32[64,256]{1,0:T(8,128)S(1)} collective-permute-done((f32[64,256]{1,0:T(8,128)S(1)}, f32[64,256]{1,0:T(8,128)S(1)}, u32[]{:S(2)}, u32[]{:S(2)}) %collective-permute-start.1) | collective-permute-done | bytes 65568 | tf_op jit(solution)/shard_map/ppermute | solution.py:60
  73.1 3.0 %collective-permute-start.2 = (f32[64,256]{1,0:T(8,128)S(1)}, f32[64,256]{1,0:T(8,128)S(1)}, u32[]{:S(2)}, u32[]{:S(2)}) collective-permute-start(f32[64,256]{1,0:T(8,128)S(1)} %add.96), channel_id=1, source_target_pairs={{0,4},{1,5},{2,6},{3,7},{4,0},{5,1},{6,2},{7,3},{8,12},{9,13},{10,... | collective-permute-start | bytes 196616 | tf_op jit(solution)/shard_map/ppermute | solution.py:60
  76.1 1.7 %collective-permute-done.2 = f32[64,256]{1,0:T(8,128)S(1)} collective-permute-done((f32[64,256]{1,0:T(8,128)S(1)}, f32[64,256]{1,0:T(8,128)S(1)}, u32[]{:S(2)}, u32[]{:S(2)}) %collective-permute-start.2) | collective-permute-done | bytes 65568 | tf_op jit(solution)/shard_map/ppermute | solution.py:60
  78.4 3.3 %fusion.33 = f32[32,2,7392]{2,0,1:T(8,128)S(1)} fusion(bf16[256,7392,1]{0,1,2:T(8,128)(2,1)} %bitcast.58, bf16[32,2,256]{2,1,0:T(2,128)(2,1)S(1)} %dot_general.27), kind=kOutput, calls=%fused_computation.44 | convolution fusion | flops 242221056 | bytes 5709824 | tf_op jit(solution)/shard_map/dot_general | solution.py:142
  81.9 1.5 copy.57
  83.4 47.0 %all_to_all.21 = f32[32,2,7393]{2,1,0:T(2,128)} all-to-all(f32[32,2,7393]{2,1,0:T(2,128)S(1)} %copy.57), channel_id=1, replica_groups=mesh['wide'=32,'narrow'=8] {'wide'}, dimensions={0} | all-to-all | bytes 3785216 | tf_op jit(solution)/shard_map/all_to_all | solution.py:47
  130.4 2.1 %reduce_sum.59 = f32[2,7393]{1,0:T(2,128)S(1)} reduce(f32[32,2,7393]{2,1,0:T(2,128)} %all_to_all.21, f32[]{:T(128)} %constant.14.clone.1), dimensions={0}, to_apply=%region_6.7 | reduce | flops 458366 | bytes 1951756 | tf_op jit(solution)/shard_map/reduce_sum | solution.py:47
  133.1 20.2 %all_to_all.22 = bf16[32,2,3696]{2,1,0:T(2,128)(2,1)S(1)} all-to-all(bf16[32,2,3696]{2,1,0:T(2,128)(2,1)S(1)} %broadcast_in_dim.169), channel_id=1, replica_groups=mesh['wide'=32,'narrow'=8] {'wide'}, dimensions={0} | all-to-all | bytes 946176 | tf_op jit(solution)/shard_map/all_to_all | solution.py:53
  153.6 2.0 %fusion.62 = f32[64,256]{1,0:T(8,128)S(1)} fusion(bf16[64,3696]{1,0:T(8,128)(2,1)S(1)} %reshape.658, bf16[3696,256]{1,0:T(8,128)(2,1)} %param.23), kind=kOutput, calls=%fused_computation.104 | convolution fusion | flops 121110528 | bytes 2430976 | tf_op jit(solution)/shard_map/dot_general | solution.py:149
  155.6 4.7 %collective-permute-start.3 = (f32[64,256]{1,0:T(8,128)S(1)}, f32[64,256]{1,0:T(8,128)S(1)}, u32[]{:S(2)}, u32[]{:S(2)}) collective-permute-start(f32[64,256]{1,0:T(8,128)S(1)} %fusion.62), channel_id=1, source_target_pairs={{0,1},{1,0},{2,3},{3,2},{4,5},{5,4},{6,7},{7,6},{8,9},{9,8},{10,11... | collective-permute-start | bytes 196616 | tf_op jit(solution)/shard_map/ppermute | solution.py:60
  161.2 1.4 collective-permute-start.4
  162.6 1.8 %collective-permute-done.4 = f32[64,256]{1,0:T(8,128)S(1)} collective-permute-done((f32[64,256]{1,0:T(8,128)S(1)}, f32[64,256]{1,0:T(8,128)S(1)}, u32[]{:S(2)}, u32[]{:S(2)}) %collective-permute-start.4) | collective-permute-done | bytes 65568 | tf_op jit(solution)/shard_map/ppermute | solution.py:60
  164.4 3.0 %collective-permute-start.5 = (f32[64,256]{1,0:T(8,128)S(1)}, f32[64,256]{1,0:T(8,128)S(1)}, u32[]{:S(2)}, u32[]{:S(2)}) collective-permute-start(f32[64,256]{1,0:T(8,128)S(1)} %add.102), channel_id=1, source_target_pairs={{0,4},{1,5},{2,6},{3,7},{4,0},{5,1},{6,2},{7,3},{8,12},{9,13},{10,... | collective-permute-start | bytes 196616 | tf_op jit(solution)/shard_map/ppermute | solution.py:60
  167.4 1.7 %collective-permute-done.5 = f32[64,256]{1,0:T(8,128)S(1)} collective-permute-done((f32[64,256]{1,0:T(8,128)S(1)}, f32[64,256]{1,0:T(8,128)S(1)}, u32[]{:S(2)}, u32[]{:S(2)}) %collective-permute-start.5) | collective-permute-done | bytes 65568 | tf_op jit(solution)/shard_map/ppermute | solution.py:60
  (77 shorter events, 10.5 us)
Async XLA Ops:
  0.0 47.0 %copy-start = (bf16[2,1,4096,128]{3,2,1,0:T(8,128)(2,1)S(1)}, bf16[2,1,4096,128]{3,2,1,0:T(8,128)(2,1)}, u32[]{:S(2)}) copy-start(bf16[2,1,4096,128]{3,2,1,0:T(8,128)(2,1)} %param.17) | copy-start | bytes 6291460
  2.1 14.7 %copy-start.2 = (s32[2,3,4096]{2,0,1:T(2,128)S(1)}, s32[2,3,4096]{2,0,1:T(2,128)}, u32[]{:S(2)}) copy-start(s32[2,3,4096]{2,0,1:T(2,128)} %param.18) | copy-start | bytes 294916
  4.9 37.5 %all-to-all-start = ((f32[32,2,1281]{2,1,0:T(2,128)}), f32[32,2,1281]{2,1,0:T(2,128)S(1)}, u32[]{:S(2)}, u32[]{:S(2)}) async-start(f32[32,2,1281]{2,1,0:T(2,128)} %copy.50), calls=%async_computation | async-start | bytes 720896 | tf_op jit(solution)/shard_map/all_to_all | solution.py:47
  16.8 2.6 %copy-start.5 = (s32[2]{0:T(128)S(1)}, s32[2]{0:T(128)}, u32[]{:S(2)}) copy-start(s32[2]{0:T(128)} %param.19) | copy-start | bytes 28
  21.8 1.9 %copy-start.4 = (bf16[1,10,128]{2,1,0:T(8,128)(2,1)S(1)}, bf16[1,10,128]{2,1,0:T(8,128)(2,1)}, u32[]{:S(2)}) copy-start(bf16[1,10,128]{2,1,0:T(8,128)(2,1)} %param.15) | copy-start | bytes 7684
  46.8 19.2 %copy-start.1 = (bf16[1024,256]{1,0:T(8,128)(2,1)S(1)}, bf16[1024,256]{1,0:T(8,128)(2,1)}, u32[]{:S(2)}) copy-start(bf16[1024,256]{1,0:T(8,128)(2,1)} %param.20) | copy-start | bytes 1572868
  47.0 29.1 %copy-start.6 = (bf16[256]{0:T(256)(128)(2,1)S(1)}, bf16[256]{0:T(256)(128)(2,1)}, u32[]{:S(2)}) copy-start(bf16[256]{0:T(256)(128)(2,1)} %param.21) | copy-start | bytes 1540
  47.0 30.8 %copy-start.3 = (bf16[64,256]{1,0:T(8,128)(2,1)S(1)}, bf16[64,256]{1,0:T(8,128)(2,1)}, u32[]{:S(2)}) copy-start(bf16[64,256]{1,0:T(8,128)(2,1)} %param.12) | copy-start | bytes 98308
  66.2 3.7 %collective-permute-start = (f32[64,256]{1,0:T(8,128)S(1)}, f32[64,256]{1,0:T(8,128)S(1)}, u32[]{:S(2)}, u32[]{:S(2)}) collective-permute-start(f32[64,256]{1,0:T(8,128)S(1)} %fusion.61), channel_id=1, source_target_pairs={{0,1},{1,0},{2,3},{3,2},{4,5},{5,4},{6,7},{7,6},{8,9},{9,8},{10,11... | collective-permute-start | bytes 196616 | tf_op jit(solution)/shard_map/ppermute | solution.py:60
  69.9 3.2 %collective-permute-start.1 = (f32[64,256]{1,0:T(8,128)S(1)}, f32[64,256]{1,0:T(8,128)S(1)}, u32[]{:S(2)}, u32[]{:S(2)}) collective-permute-start(f32[64,256]{1,0:T(8,128)S(1)} %add.95), channel_id=1, source_target_pairs={{0,2},{1,3},{2,0},{3,1},{4,6},{5,7},{6,4},{7,5},{8,10},{9,11},{10,... | collective-permute-start | bytes 196616 | tf_op jit(solution)/shard_map/ppermute | solution.py:60
  73.1 4.7 %collective-permute-start.2 = (f32[64,256]{1,0:T(8,128)S(1)}, f32[64,256]{1,0:T(8,128)S(1)}, u32[]{:S(2)}, u32[]{:S(2)}) collective-permute-start(f32[64,256]{1,0:T(8,128)S(1)} %add.96), channel_id=1, source_target_pairs={{0,4},{1,5},{2,6},{3,7},{4,0},{5,1},{6,2},{7,3},{8,12},{9,13},{10,... | collective-permute-start | bytes 196616 | tf_op jit(solution)/shard_map/ppermute | solution.py:60
  155.6 5.6 %collective-permute-start.3 = (f32[64,256]{1,0:T(8,128)S(1)}, f32[64,256]{1,0:T(8,128)S(1)}, u32[]{:S(2)}, u32[]{:S(2)}) collective-permute-start(f32[64,256]{1,0:T(8,128)S(1)} %fusion.62), channel_id=1, source_target_pairs={{0,1},{1,0},{2,3},{3,2},{4,5},{5,4},{6,7},{7,6},{8,9},{9,8},{10,11... | collective-permute-start | bytes 196616 | tf_op jit(solution)/shard_map/ppermute | solution.py:60
  161.2 3.2 %collective-permute-start.4 = (f32[64,256]{1,0:T(8,128)S(1)}, f32[64,256]{1,0:T(8,128)S(1)}, u32[]{:S(2)}, u32[]{:S(2)}) collective-permute-start(f32[64,256]{1,0:T(8,128)S(1)} %add.101), channel_id=1, source_target_pairs={{0,2},{1,3},{2,0},{3,1},{4,6},{5,7},{6,4},{7,5},{8,10},{9,11},{10,... | collective-permute-start | bytes 196616 | tf_op jit(solution)/shard_map/ppermute | solution.py:60
  164.4 4.7 %collective-permute-start.5 = (f32[64,256]{1,0:T(8,128)S(1)}, f32[64,256]{1,0:T(8,128)S(1)}, u32[]{:S(2)}, u32[]{:S(2)}) collective-permute-start(f32[64,256]{1,0:T(8,128)S(1)} %add.102), channel_id=1, source_target_pairs={{0,4},{1,5},{2,6},{3,7},{4,0},{5,1},{6,2},{7,3},{8,12},{9,13},{10,... | collective-permute-start | bytes 196616 | tf_op jit(solution)/shard_map/ppermute | solution.py:60

commit v3 on v2

--- a/solution.py
+++ b/solution.py
@@ -140,8 +140,18 @@
     hidden_local = gate_up_weight.shape[2]
     gate_up_flat = gate_up_weight.reshape(local_rows, 2 * hidden_local)
     partial2 = jnp.dot(scaled2, gate_up_flat, preferred_element_type=jnp.float32)
-    summed2 = reduce_rows(jnp.concatenate([partial2, resid_squares[:, None]], axis=1), "wide")
-    inv_rms2 = 1.0 / jnp.sqrt(summed2[:, 2 * hidden_local] / D + norm_eps)
+    squares_hi = resid_squares.astype(jnp.bfloat16)
+    squares_lo = (resid_squares - squares_hi.astype(jnp.float32)).astype(jnp.bfloat16)
+    sent2 = jnp.concatenate(
+        [partial2.astype(jnp.bfloat16), squares_hi[:, None], squares_lo[:, None]], axis=1
+    )
+    n_wide = lax.axis_size("wide")
+    received2 = lax.all_to_all(
+        sent2.reshape(n_wide, sent2.shape[0] // n_wide, sent2.shape[1]), "wide", 0, 0, tiled=False
+    )
+    summed2 = jnp.sum(received2.astype(jnp.float32), axis=0)
+    total_squares2 = summed2[:, 2 * hidden_local] + summed2[:, 2 * hidden_local + 1]
+    inv_rms2 = 1.0 / jnp.sqrt(total_squares2 / D + norm_eps)
     gate_up = summed2[:, : 2 * hidden_local] * inv_rms2[:, None]
     hidden = (jax.nn.silu(gate_up[:, :hidden_local]) * gate_up[:, hidden_local:]).astype(
         jnp.bfloat16

time: 171 us -> 155 us (0.906)
  blocking collectives: 85.5 us -> 64.2 us
  local copies, waits for them, and re-layouts: 9.98 us -> 14.7 us
    all_to_all x1, blocking collectives: 47 us -> 26.8 us  [local(): lax.all_to_all(sent2.reshape(n_wide, sent2.shape[0] // n_wide, sent2.shap...]
    concatenate x3 -> x2, local copies, waits for them, and re-layouts: 1.89 us -> 6.22 us  [local(): jnp.concatenate([partial2.astype(jnp.bfloat16), squares_hi[:, None], squa...]
    reduce_sum x2 -> x1, other arithmetic: 2.19 us -> 0.12 us  [reduce_rows(): return jnp.sum(lax.all_to_all(blocks, axis, 0, 0, tiled=False), axis=0)]
  transfers between devices with their start and end apart: 7 -> 7, of which waited for: 6 -> 6; matrix products, arithmetic and copies ran while one was open for 15% -> 17% of each run, Pallas kernels for 0% -> 0%
where the time goes in v3:
time: 155 us; the launch traced here: 153 us
  blocking collectives  64.2 us (41%)
  starting transfers between devices  28.8 us (19%)
  other arithmetic  25.7 us (17%)
  local copies, waits for them, and re-layouts  14.7 us (9%)
  matrix products  10.9 us (7%)
  waiting for transfers between devices  8.85 us (6%)
    all_to_all x2, blocking collectives, gather_rows(): lax.all_to_all(copies, axis, 0, 0, tiled=False)  37.4 us
    all_to_all x1, blocking collectives, local(): lax.all_to_all(sent2.reshape(n_wide, sent2.shape[0] // n_wide, sent2.shap...  26.8 us
    concatenate x2, other arithmetic, rotate(): jnp.concatenate([leading * cosine - trailing * sine_table, trailing * cos...  18.7 us
    ppermute x6, starting transfers between devices, sum_all(): x = x + lax.ppermute(x, axis, [(i, i ^ step) for i in range(n)])  17 us
    all_to_all x1, starting transfers between devices, reduce_rows(): return jnp.sum(lax.all_to_all(blocks, axis, 0, 0, tiled=False), axis=0)  11.9 us
    ppermute x6, waiting for transfers between devices, sum_all(): x = x + lax.ppermute(x, axis, [(i, i ^ step) for i in range(n)])  8.85 us
    concatenate x2, local copies, waits for them, and re-layouts, local(): jnp.concatenate([partial2.astype(jnp.bfloat16), squares_hi[:, None], squa...  6.22 us
    dot_general x1, matrix products, local(): jnp.dot(scaled2, gate_up_flat, preferred_element_type=jnp.float32)  4.29 us
  transfers between devices with their start and end apart: 7, of which 6 were waited for; matrix products, arithmetic and copies ran while one was open for 17% of the time, Pallas kernels for 0%

profile of v3, /device:TPU:1, one launch (start us, length us, event | category | flops | bytes accessed | tf_op | source)
XLA Modules:
  0.0 153.4 jit_solution(5546402750807887536)
XLA Ops:
  2.1 1.3 copy.55
  4.9 11.9 %all-to-all-start = ((f32[32,2,1281]{2,1,0:T(2,128)}), f32[32,2,1281]{2,1,0:T(2,128)S(1)}, u32[]{:S(2)}, u32[]{:S(2)}) async-start(f32[32,2,1281]{2,1,0:T(2,128)} %copy.59), calls=%async_computation | async-start | bytes 720896 | tf_op jit(solution)/shard_map/all_to_all | solution.py:47
  16.8 2.6 %copy.62 = s32[2,3,4096]{1,2,0:T(8,128)} copy(s32[2,3,4096]{2,0,1:T(2,128)S(1)} %copy-done.2) | data formatting | bytes 196608 | tf_op args[6]
  19.8 1.5 gather_fusion
  21.8 1.9 %bitcast_convert_fusion = f32[2,1,4096,128]{3,2,0,1:T(8,128)S(1)} fusion(bf16[2,1,4096,128]{3,2,1,0:T(8,128)(2,1)} %param.16), kind=kLoop, calls=%fused_computation.13 | loop fusion | flops 1048576 | bytes 6291456 | tf_op jit(solution)/shard_map/convert_element_type | solution.py:96
  23.7 18.6 %fusion.7 = (bf16[2,4096,64]{2,1,0:T(8,128)(2,1)}, bf16[2,4096,64]{2,1,0:T(8,128)(2,1)}) fusion(f32[2,1,4096,128]{3,2,0,1:T(8,128)S(1)} %bitcast_convert_fusion, f32[64]{0:T(128)S(1)} %multiply_exponential_fusion, f32[2,4096]{1,0:T(2,128)S(1)} %get-tuple-element.19, f32[2,4096]{1,0:T(2,128)S(1)} %get-tuple-element.20, f32[2,4096]{1,0:T(2,128)S(1)} %get-tuple-element.18, ...), kind=kLoop, calls=%fused_computation.14 | loop fusion | flops 5767168 | bytes 6390144 | tf_op jit(solution)/shard_map/concatenate | solution.py:38
  43.2 3.6 %select_reduce_fusion = (f32[2,8]{1,0:T(2,128)S(1)}, f32[2,8,4096]{2,1,0:T(8,128)S(1)}) fusion(pred[2,4096]{1,0:T(4,128)(4,1)S(1)} %iota_compare_fusion, bf16[2,4096,64]{2,1,0:T(8,128)(2,1)} %get-tuple-element.17, bf16[2,4096,64]{2,1,0:T(8,128)(2,1)} %get-tuple-element.16, bf16[2,8,64]{2,1,0:T(8,128)(2,1)S(1)} %bitcast.59, bf16[2,8,64]{2,1,0:T(8,128)(2,1)S(1)} %bitcast.58), kind=kOutput, calls=%fused_computation.23 | convolution fusion | flops 21176304 | bytes 2371648 | tf_op jit(solution)/shard_map/rgjd,rgsd->rgjs/dot_general | solution.py:107
  47.6 18.4 %all_to_all.20 = bf16[32,2,1024]{2,1,0:T(2,128)(2,1)S(1)} all-to-all(bf16[32,2,1024]{2,1,0:T(2,128)(2,1)S(1)} %broadcast_in_dim.169), channel_id=1, replica_groups=mesh['wide'=32,'narrow'=8] {'wide'}, dimensions={0} | all-to-all | bytes 262144 | tf_op jit(solution)/shard_map/all_to_all | solution.py:53
  66.2 2.8 %collective-permute-start = (f32[64,256]{1,0:T(8,128)S(1)}, f32[64,256]{1,0:T(8,128)S(1)}, u32[]{:S(2)}, u32[]{:S(2)}) collective-permute-start(f32[64,256]{1,0:T(8,128)S(1)} %fusion.62), channel_id=1, source_target_pairs={{0,1},{1,0},{2,3},{3,2},{4,5},{5,4},{6,7},{7,6},{8,9},{9,8},{10,11... | collective-permute-start | bytes 196616 | tf_op jit(solution)/shard_map/ppermute | solution.py:60
  69.9 1.4 collective-permute-start.1
  71.3 1.8 %collective-permute-done.1 = f32[64,256]{1,0:T(8,128)S(1)} collective-permute-done((f32[64,256]{1,0:T(8,128)S(1)}, f32[64,256]{1,0:T(8,128)S(1)}, u32[]{:S(2)}, u32[]{:S(2)}) %collective-permute-start.1) | collective-permute-done | bytes 65568 | tf_op jit(solution)/shard_map/ppermute | solution.py:60
  73.2 3.0 %collective-permute-start.2 = (f32[64,256]{1,0:T(8,128)S(1)}, f32[64,256]{1,0:T(8,128)S(1)}, u32[]{:S(2)}, u32[]{:S(2)}) collective-permute-start(f32[64,256]{1,0:T(8,128)S(1)} %add.100), channel_id=1, source_target_pairs={{0,4},{1,5},{2,6},{3,7},{4,0},{5,1},{6,2},{7,3},{8,12},{9,13},{10,... | collective-permute-start | bytes 196616 | tf_op jit(solution)/shard_map/ppermute | solution.py:60
  76.2 1.7 %collective-permute-done.2 = f32[64,256]{1,0:T(8,128)S(1)} collective-permute-done((f32[64,256]{1,0:T(8,128)S(1)}, f32[64,256]{1,0:T(8,128)S(1)}, u32[]{:S(2)}, u32[]{:S(2)}) %collective-permute-start.2) | collective-permute-done | bytes 65568 | tf_op jit(solution)/shard_map/ppermute | solution.py:60
  78.0 4.3 %convolution_convert_fusion = bf16[64,7392]{1,0:T(8,128)(2,1)} fusion(bf16[256,7392]{0,1:T(8,128)(2,1)} %bitcast.56, bf16[64,256]{1,0:T(8,128)(2,1)S(1)} %get-tuple-element.11, f32[256]{0:T(256)S(1)} %convert_element_type.232), kind=kOutput, calls=%fused_computation.1 | convolution fusion | flops 242743296 | bytes 4764672 | tf_op jit(solution)/shard_map/dot_general | solution.py:142
  82.3 2.4 %concatenate.70 = bf16[32,2,7392]{2,1,0:T(2,128)(2,1)S(1)} reshape(bf16[64,7392]{1,0:T(8,128)(2,1)} %convolution_convert_fusion) | data formatting | bytes 1892352 | tf_op jit(solution)/shard_map/concatenate | solution.py:145
  85.1 3.8 %concatenate.71 = bf16[32,2,7394]{2,1,0:T(2,128)(2,1)} concatenate(bf16[32,2,7392]{2,1,0:T(2,128)(2,1)S(1)} %concatenate.70, bf16[32,2,1]{2,1,0:T(2,128)(2,1)S(1)} %copy.66, bf16[32,2,1]{2,1,0:T(2,128)(2,1)S(1)} %copy.67), dimensions={2} | concatenate | bytes 1892864 | tf_op jit(solution)/shard_map/concatenate | solution.py:145
  88.9 26.8 %all_to_all.21 = bf16[32,2,7394]{2,1,0:T(2,128)(2,1)S(1)} all-to-all(bf16[32,2,7394]{2,1,0:T(2,128)(2,1)} %concatenate.71), channel_id=1, replica_groups=mesh['wide'=32,'narrow'=8] {'wide'}, dimensions={0} | all-to-all | bytes 1892864 | tf_op jit(solution)/shard_map/all_to_all | solution.py:149
  117.2 19.0 %all_to_all.22 = bf16[32,2,3696]{2,1,0:T(2,128)(2,1)S(1)} all-to-all(bf16[32,2,3696]{2,1,0:T(2,128)(2,1)S(1)} %broadcast_in_dim.170), channel_id=1, replica_groups=mesh['wide'=32,'narrow'=8] {'wide'}, dimensions={0} | all-to-all | bytes 946176 | tf_op jit(solution)/shard_map/all_to_all | solution.py:53
  136.5 2.0 %fusion.63 = f32[64,256]{1,0:T(8,128)S(1)} fusion(bf16[64,3696]{1,0:T(8,128)(2,1)S(1)} %reshape.688, bf16[3696,256]{1,0:T(8,128)(2,1)} %param.23), kind=kOutput, calls=%fused_computation.106 | convolution fusion | flops 121110528 | bytes 2430976 | tf_op jit(solution)/shard_map/dot_general | solution.py:159
  138.5 5.4 %collective-permute-start.3 = (f32[64,256]{1,0:T(8,128)S(1)}, f32[64,256]{1,0:T(8,128)S(1)}, u32[]{:S(2)}, u32[]{:S(2)}) collective-permute-start(f32[64,256]{1,0:T(8,128)S(1)} %fusion.63), channel_id=1, source_target_pairs={{0,1},{1,0},{2,3},{3,2},{4,5},{5,4},{6,7},{7,6},{8,9},{9,8},{10,11... | collective-permute-start | bytes 196616 | tf_op jit(solution)/shard_map/ppermute | solution.py:60
  144.8 1.4 collective-permute-start.4
  146.2 1.8 %collective-permute-done.4 = f32[64,256]{1,0:T(8,128)S(1)} collective-permute-done((f32[64,256]{1,0:T(8,128)S(1)}, f32[64,256]{1,0:T(8,128)S(1)}, u32[]{:S(2)}, u32[]{:S(2)}) %collective-permute-start.4) | collective-permute-done | bytes 65568 | tf_op jit(solution)/shard_map/ppermute | solution.py:60
  148.1 3.0 %collective-permute-start.5 = (f32[64,256]{1,0:T(8,128)S(1)}, f32[64,256]{1,0:T(8,128)S(1)}, u32[]{:S(2)}, u32[]{:S(2)}) collective-permute-start(f32[64,256]{1,0:T(8,128)S(1)} %add.107), channel_id=1, source_target_pairs={{0,4},{1,5},{2,6},{3,7},{4,0},{5,1},{6,2},{7,3},{8,12},{9,13},{10,... | collective-permute-start | bytes 196616 | tf_op jit(solution)/shard_map/ppermute | solution.py:60
  151.1 1.7 %collective-permute-done.5 = f32[64,256]{1,0:T(8,128)S(1)} collective-permute-done((f32[64,256]{1,0:T(8,128)S(1)}, f32[64,256]{1,0:T(8,128)S(1)}, u32[]{:S(2)}, u32[]{:S(2)}) %collective-permute-start.5) | collective-permute-done | bytes 65568 | tf_op jit(solution)/shard_map/ppermute | solution.py:60
  (78 shorter events, 11.1 us)
Async XLA Ops:
  0.0 47.0 %copy-start = (bf16[2,1,4096,128]{3,2,1,0:T(8,128)(2,1)S(1)}, bf16[2,1,4096,128]{3,2,1,0:T(8,128)(2,1)}, u32[]{:S(2)}) copy-start(bf16[2,1,4096,128]{3,2,1,0:T(8,128)(2,1)} %param.17) | copy-start | bytes 6291460
  0.0 16.8 %copy-start.2 = (s32[2,3,4096]{2,0,1:T(2,128)S(1)}, s32[2,3,4096]{2,0,1:T(2,128)}, u32[]{:S(2)}) copy-start(s32[2,3,4096]{2,0,1:T(2,128)} %param.18) | copy-start | bytes 294916
  3.5 16.0 %copy-start.5 = (s32[2]{0:T(128)S(1)}, s32[2]{0:T(128)}, u32[]{:S(2)}) copy-start(s32[2]{0:T(128)} %param.19) | copy-start | bytes 28
  4.9 37.5 %all-to-all-start = ((f32[32,2,1281]{2,1,0:T(2,128)}), f32[32,2,1281]{2,1,0:T(2,128)S(1)}, u32[]{:S(2)}, u32[]{:S(2)}) async-start(f32[32,2,1281]{2,1,0:T(2,128)} %copy.59), calls=%async_computation | async-start | bytes 720896 | tf_op jit(solution)/shard_map/all_to_all | solution.py:47
  19.5 4.2 %copy-start.4 = (bf16[1,10,128]{2,1,0:T(8,128)(2,1)S(1)}, bf16[1,10,128]{2,1,0:T(8,128)(2,1)}, u32[]{:S(2)}) copy-start(bf16[1,10,128]{2,1,0:T(8,128)(2,1)} %param.15) | copy-start | bytes 7684
  43.2 22.8 %copy-start.1 = (bf16[1024,256]{1,0:T(8,128)(2,1)S(1)}, bf16[1024,256]{1,0:T(8,128)(2,1)}, u32[]{:S(2)}) copy-start(bf16[1024,256]{1,0:T(8,128)(2,1)} %param.20) | copy-start | bytes 1572868
  43.2 33.0 %copy-start.6 = (bf16[256]{0:T(256)(128)(2,1)S(1)}, bf16[256]{0:T(256)(128)(2,1)}, u32[]{:S(2)}) copy-start(bf16[256]{0:T(256)(128)(2,1)} %param.21) | copy-start | bytes 1540
  43.2 34.7 %copy-start.3 = (bf16[64,256]{1,0:T(8,128)(2,1)S(1)}, bf16[64,256]{1,0:T(8,128)(2,1)}, u32[]{:S(2)}) copy-start(bf16[64,256]{1,0:T(8,128)(2,1)} %param.12) | copy-start | bytes 98308
  66.2 3.7 %collective-permute-start = (f32[64,256]{1,0:T(8,128)S(1)}, f32[64,256]{1,0:T(8,128)S(1)}, u32[]{:S(2)}, u32[]{:S(2)}) collective-permute-start(f32[64,256]{1,0:T(8,128)S(1)} %fusion.62), channel_id=1, source_target_pairs={{0,1},{1,0},{2,3},{3,2},{4,5},{5,4},{6,7},{7,6},{8,9},{9,8},{10,11... | collective-permute-start | bytes 196616 | tf_op jit(solution)/shard_map/ppermute | solution.py:60
  69.9 3.2 %collective-permute-start.1 = (f32[64,256]{1,0:T(8,128)S(1)}, f32[64,256]{1,0:T(8,128)S(1)}, u32[]{:S(2)}, u32[]{:S(2)}) collective-permute-start(f32[64,256]{1,0:T(8,128)S(1)} %add.99), channel_id=1, source_target_pairs={{0,2},{1,3},{2,0},{3,1},{4,6},{5,7},{6,4},{7,5},{8,10},{9,11},{10,... | collective-permute-start | bytes 196616 | tf_op jit(solution)/shard_map/ppermute | solution.py:60
  73.2 4.7 %collective-permute-start.2 = (f32[64,256]{1,0:T(8,128)S(1)}, f32[64,256]{1,0:T(8,128)S(1)}, u32[]{:S(2)}, u32[]{:S(2)}) collective-permute-start(f32[64,256]{1,0:T(8,128)S(1)} %add.100), channel_id=1, source_target_pairs={{0,4},{1,5},{2,6},{3,7},{4,0},{5,1},{6,2},{7,3},{8,12},{9,13},{10,... | collective-permute-start | bytes 196616 | tf_op jit(solution)/shard_map/ppermute | solution.py:60
  138.5 6.3 %collective-permute-start.3 = (f32[64,256]{1,0:T(8,128)S(1)}, f32[64,256]{1,0:T(8,128)S(1)}, u32[]{:S(2)}, u32[]{:S(2)}) collective-permute-start(f32[64,256]{1,0:T(8,128)S(1)} %fusion.63), channel_id=1, source_target_pairs={{0,1},{1,0},{2,3},{3,2},{4,5},{5,4},{6,7},{7,6},{8,9},{9,8},{10,11... | collective-permute-start | bytes 196616 | tf_op jit(solution)/shard_map/ppermute | solution.py:60
  144.8 3.2 %collective-permute-start.4 = (f32[64,256]{1,0:T(8,128)S(1)}, f32[64,256]{1,0:T(8,128)S(1)}, u32[]{:S(2)}, u32[]{:S(2)}) collective-permute-start(f32[64,256]{1,0:T(8,128)S(1)} %add.106), channel_id=1, source_target_pairs={{0,2},{1,3},{2,0},{3,1},{4,6},{5,7},{6,4},{7,5},{8,10},{9,11},{10,... | collective-permute-start | bytes 196616 | tf_op jit(solution)/shard_map/ppermute | solution.py:60
  148.1 4.7 %collective-permute-start.5 = (f32[64,256]{1,0:T(8,128)S(1)}, f32[64,256]{1,0:T(8,128)S(1)}, u32[]{:S(2)}, u32[]{:S(2)}) collective-permute-start(f32[64,256]{1,0:T(8,128)S(1)} %add.107), channel_id=1, source_target_pairs={{0,4},{1,5},{2,6},{3,7},{4,0},{5,1},{6,2},{7,3},{8,12},{9,13},{10,... | collective-permute-start | bytes 196616 | tf_op jit(solution)/shard_map/ppermute | solution.py:60

commit v4 on v3

--- a/solution.py
+++ b/solution.py
@@ -14,6 +14,20 @@
 rope_base = 1000000.0
 
 
+def cos_sin(angle):
+    k = jnp.round(angle * 0.6366197723675814)
+    r = ((angle - k * 1.5703125) - k * 4.837512969970703125e-4) - k * 7.54978995489188216e-8
+    z = r * r
+    s = r + r * z * (-1.6666654611e-1 + z * (8.3321608736e-3 + z * -1.9515295891e-4))
+    c = 1.0 - 0.5 * z + z * z * (
+        4.166664568298827e-2 + z * (-1.388731625493765e-3 + z * 2.443315711809948e-5)
+    )
+    q = k.astype(jnp.int32) % 4
+    cos = jnp.where(q == 0, c, jnp.where(q == 1, -s, jnp.where(q == 2, -c, s)))
+    sin = jnp.where(q == 0, s, jnp.where(q == 1, c, jnp.where(q == 2, -s, -c)))
+    return cos, sin
+
+
 def mrope_tables(position):
     half_width = DH // 2
     pair_index = jnp.arange(half_width)
@@ -28,7 +42,7 @@
         jnp.where(component == 1, pos_float[..., 1, :, None], pos_float[..., 2, :, None]),
     )
     angles = chosen * inv_freq
-    return (jnp.cos(angles), jnp.sin(angles))
+    return cos_sin(angles)
 
 
 def rotate(values, cosine, sine_table):

time: 155 us -> 164 us (1.058)
  other arithmetic: 25.7 us -> 34.3 us
    concatenate x2 -> x3, other arithmetic: 18.7 us -> 25.5 us  [rotate(): jnp.concatenate([leading * cosine - trailing * sine_table, trailing * cos...]
    convert_element_type x1, other arithmetic: 1.87 us -> 3.79 us  [local(): cache_keys.astype(jnp.float32)]
  transfers between devices with their start and end apart: 7 -> 7, of which waited for: 6 -> 6; matrix products, arithmetic and copies ran while one was open for 17% -> 21% of each run, Pallas kernels for 0% -> 0%
where the time goes in v4:
time: 164 us; the launch traced here: 162 us
  blocking collectives  64.4 us (39%)
  other arithmetic  34.3 us (21%)
  starting transfers between devices  28.8 us (18%)
  local copies, waits for them, and re-layouts  14.6 us (9%)
  matrix products  10.8 us (7%)
  waiting for transfers between devices  8.85 us (5%)
    all_to_all x2, blocking collectives, gather_rows(): lax.all_to_all(copies, axis, 0, 0, tiled=False)  37 us
    all_to_all x1, blocking collectives, local(): lax.all_to_all(sent2.reshape(n_wide, sent2.shape[0] // n_wide, sent2.shap...  27.4 us
    concatenate x3, other arithmetic, rotate(): jnp.concatenate([leading * cosine - trailing * sine_table, trailing * cos...  25.5 us
    ppermute x6, starting transfers between devices, sum_all(): x = x + lax.ppermute(x, axis, [(i, i ^ step) for i in range(n)])  17 us
    all_to_all x1, starting transfers between devices, reduce_rows(): return jnp.sum(lax.all_to_all(blocks, axis, 0, 0, tiled=False), axis=0)  11.9 us
    ppermute x6, waiting for transfers between devices, sum_all(): x = x + lax.ppermute(x, axis, [(i, i ^ step) for i in range(n)])  8.85 us
    concatenate x2, local copies, waits for them, and re-layouts, local(): jnp.concatenate([partial2.astype(jnp.bfloat16), squares_hi[:, None], squa...  6.22 us
    dot_general x1, matrix products, local(): jnp.dot(scaled2, gate_up_flat, preferred_element_type=jnp.float32)  4.29 us
  transfers between devices with their start and end apart: 7, of which 6 were waited for; matrix products, arithmetic and copies ran while one was open for 21% of the time, Pallas kernels for 0%

profile of v4, /device:TPU:1, one launch (start us, length us, event | category | flops | bytes accessed | tf_op | source)
XLA Modules:
  0.0 162.1 jit_solution(1863863199567454429)
XLA Ops:
  2.1 1.3 copy.55
  4.9 11.9 %all-to-all-start = ((f32[32,2,1281]{2,1,0:T(2,128)}), f32[32,2,1281]{2,1,0:T(2,128)S(1)}, u32[]{:S(2)}, u32[]{:S(2)}) async-start(f32[32,2,1281]{2,1,0:T(2,128)} %copy.59), calls=%async_computation | async-start | bytes 720896 | tf_op jit(solution)/shard_map/all_to_all | solution.py:61
  16.9 2.7 %copy.62 = s32[2,3,4096]{1,2,0:T(8,128)} copy(s32[2,3,4096]{2,0,1:T(2,128)S(1)} %copy-done.2) | data formatting | bytes 196608 | tf_op args[6]
  19.6 3.8 %bitcast_convert_fusion = f32[2,1,4096,128]{3,2,0,1:T(8,128)} fusion(bf16[2,1,4096,128]{3,2,1,0:T(8,128)(2,1)} %param.16), kind=kLoop, calls=%fused_computation.37 | loop fusion | flops 1048576 | bytes 6291456 | tf_op jit(solution)/shard_map/convert_element_type | solution.py:110
  23.7 1.4 gather_fusion
  25.5 25.3 %fusion.10 = (bf16[2,4096,64]{2,1,0:T(8,128)(2,1)}, bf16[2,4096,64]{2,1,0:T(8,128)(2,1)}) fusion(f32[2,1,4096,128]{3,2,0,1:T(8,128)} %bitcast_convert_fusion, f32[64]{0:T(128)S(1)} %multiply_exponential_fusion, f32[2,4096]{1,0:T(2,128)S(1)} %get-tuple-element.20, f32[2,4096]{1,0:T(2,128)S(1)} %get-tuple-element.21, pred[64]{0:T(512)(128)(4,1)S(1)} %get-tuple-element.30, ...), kind=kLoop, calls=%fused_computation.30 | loop fusion | flops 30932992 | bytes 6390144 | tf_op jit(solution)/shard_map/concatenate | solution.py:52
  51.8 3.6 %select_reduce_fusion = (f32[2,8]{1,0:T(2,128)S(1)}, f32[2,8,4096]{2,1,0:T(8,128)S(1)}) fusion(pred[2,4096]{1,0:T(4,128)(4,1)S(1)} %iota_compare_fusion, bf16[2,4096,64]{2,1,0:T(8,128)(2,1)} %get-tuple-element.18, bf16[2,4096,64]{2,1,0:T(8,128)(2,1)} %get-tuple-element.17, bf16[2,8,64]{2,1,0:T(8,128)(2,1)S(1)} %bitcast.59, bf16[2,8,64]{2,1,0:T(8,128)(2,1)S(1)} %bitcast.58), kind=kOutput, calls=%fused_computation.48 | convolution fusion | flops 21176304 | bytes 2371648 | tf_op jit(solution)/shard_map/rgjd,rgsd->rgjs/dot_general | solution.py:121
  56.1 18.4 %all_to_all.20 = bf16[32,2,1024]{2,1,0:T(2,128)(2,1)S(1)} all-to-all(bf16[32,2,1024]{2,1,0:T(2,128)(2,1)S(1)} %broadcast_in_dim.169), channel_id=1, replica_groups=mesh['wide'=32,'narrow'=8] {'wide'}, dimensions={0} | all-to-all | bytes 262144 | tf_op jit(solution)/shard_map/all_to_all | solution.py:67
  74.8 2.8 %collective-permute-start = (f32[64,256]{1,0:T(8,128)S(1)}, f32[64,256]{1,0:T(8,128)S(1)}, u32[]{:S(2)}, u32[]{:S(2)}) collective-permute-start(f32[64,256]{1,0:T(8,128)S(1)} %fusion.72), channel_id=1, source_target_pairs={{0,1},{1,0},{2,3},{3,2},{4,5},{5,4},{6,7},{7,6},{8,9},{9,8},{10,11... | collective-permute-start | bytes 196616 | tf_op jit(solution)/shard_map/ppermute | solution.py:74
  78.5 1.4 collective-permute-start.1
  79.9 1.8 %collective-permute-done.1 = f32[64,256]{1,0:T(8,128)S(1)} collective-permute-done((f32[64,256]{1,0:T(8,128)S(1)}, f32[64,256]{1,0:T(8,128)S(1)}, u32[]{:S(2)}, u32[]{:S(2)}) %collective-permute-start.1) | collective-permute-done | bytes 65568 | tf_op jit(solution)/shard_map/ppermute | solution.py:74
  81.7 3.0 %collective-permute-start.2 = (f32[64,256]{1,0:T(8,128)S(1)}, f32[64,256]{1,0:T(8,128)S(1)}, u32[]{:S(2)}, u32[]{:S(2)}) collective-permute-start(f32[64,256]{1,0:T(8,128)S(1)} %add.437), channel_id=1, source_target_pairs={{0,4},{1,5},{2,6},{3,7},{4,0},{5,1},{6,2},{7,3},{8,12},{9,13},{10,... | collective-permute-start | bytes 196616 | tf_op jit(solution)/shard_map/ppermute | solution.py:74
  84.7 1.7 %collective-permute-done.2 = f32[64,256]{1,0:T(8,128)S(1)} collective-permute-done((f32[64,256]{1,0:T(8,128)S(1)}, f32[64,256]{1,0:T(8,128)S(1)}, u32[]{:S(2)}, u32[]{:S(2)}) %collective-permute-start.2) | collective-permute-done | bytes 65568 | tf_op jit(solution)/shard_map/ppermute | solution.py:74
  86.5 4.3 %convolution_convert_fusion = bf16[64,7392]{1,0:T(8,128)(2,1)} fusion(bf16[256,7392]{0,1:T(8,128)(2,1)} %bitcast.56, bf16[64,256]{1,0:T(8,128)(2,1)S(1)} %get-tuple-element.11, f32[256]{0:T(256)S(1)} %convert_element_type.273), kind=kOutput, calls=%fused_computation.1 | convolution fusion | flops 242743296 | bytes 4764672 | tf_op jit(solution)/shard_map/dot_general | solution.py:156
  90.8 2.4 %concatenate.70 = bf16[32,2,7392]{2,1,0:T(2,128)(2,1)S(1)} reshape(bf16[64,7392]{1,0:T(8,128)(2,1)} %convolution_convert_fusion) | data formatting | bytes 1892352 | tf_op jit(solution)/shard_map/concatenate | solution.py:159
  93.6 3.8 %concatenate.71 = bf16[32,2,7394]{2,1,0:T(2,128)(2,1)} concatenate(bf16[32,2,7392]{2,1,0:T(2,128)(2,1)S(1)} %concatenate.70, bf16[32,2,1]{2,1,0:T(2,128)(2,1)S(1)} %copy.66, bf16[32,2,1]{2,1,0:T(2,128)(2,1)S(1)} %copy.67), dimensions={2} | concatenate | bytes 1892864 | tf_op jit(solution)/shard_map/concatenate | solution.py:159
  97.5 27.4 %all_to_all.21 = bf16[32,2,7394]{2,1,0:T(2,128)(2,1)S(1)} all-to-all(bf16[32,2,7394]{2,1,0:T(2,128)(2,1)} %concatenate.71), channel_id=1, replica_groups=mesh['wide'=32,'narrow'=8] {'wide'}, dimensions={0} | all-to-all | bytes 1892864 | tf_op jit(solution)/shard_map/all_to_all | solution.py:163
  126.3 18.6 %all_to_all.22 = bf16[32,2,3696]{2,1,0:T(2,128)(2,1)S(1)} all-to-all(bf16[32,2,3696]{2,1,0:T(2,128)(2,1)S(1)} %broadcast_in_dim.170), channel_id=1, replica_groups=mesh['wide'=32,'narrow'=8] {'wide'}, dimensions={0} | all-to-all | bytes 946176 | tf_op jit(solution)/shard_map/all_to_all | solution.py:67
  145.3 2.0 %fusion.73 = f32[64,256]{1,0:T(8,128)S(1)} fusion(bf16[64,3696]{1,0:T(8,128)(2,1)S(1)} %reshape.1051, bf16[3696,256]{1,0:T(8,128)(2,1)} %param.23), kind=kOutput, calls=%fused_computation.159 | convolution fusion | flops 121110528 | bytes 2430976 | tf_op jit(solution)/shard_map/dot_general | solution.py:173
  147.2 5.4 %collective-permute-start.3 = (f32[64,256]{1,0:T(8,128)S(1)}, f32[64,256]{1,0:T(8,128)S(1)}, u32[]{:S(2)}, u32[]{:S(2)}) collective-permute-start(f32[64,256]{1,0:T(8,128)S(1)} %fusion.73), channel_id=1, source_target_pairs={{0,1},{1,0},{2,3},{3,2},{4,5},{5,4},{6,7},{7,6},{8,9},{9,8},{10,11... | collective-permute-start | bytes 196616 | tf_op jit(solution)/shard_map/ppermute | solution.py:74
  153.6 1.4 collective-permute-start.4
  154.9 1.8 %collective-permute-done.4 = f32[64,256]{1,0:T(8,128)S(1)} collective-permute-done((f32[64,256]{1,0:T(8,128)S(1)}, f32[64,256]{1,0:T(8,128)S(1)}, u32[]{:S(2)}, u32[]{:S(2)}) %collective-permute-start.4) | collective-permute-done | bytes 65568 | tf_op jit(solution)/shard_map/ppermute | solution.py:74
  156.8 3.0 %collective-permute-start.5 = (f32[64,256]{1,0:T(8,128)S(1)}, f32[64,256]{1,0:T(8,128)S(1)}, u32[]{:S(2)}, u32[]{:S(2)}) collective-permute-start(f32[64,256]{1,0:T(8,128)S(1)} %add.444), channel_id=1, source_target_pairs={{0,4},{1,5},{2,6},{3,7},{4,0},{5,1},{6,2},{7,3},{8,12},{9,13},{10,... | collective-permute-start | bytes 196616 | tf_op jit(solution)/shard_map/ppermute | solution.py:74
  159.8 1.7 %collective-permute-done.5 = f32[64,256]{1,0:T(8,128)S(1)} collective-permute-done((f32[64,256]{1,0:T(8,128)S(1)}, f32[64,256]{1,0:T(8,128)S(1)}, u32[]{:S(2)}, u32[]{:S(2)}) %collective-permute-start.5) | collective-permute-done | bytes 65568 | tf_op jit(solution)/shard_map/ppermute | solution.py:74
  (78 shorter events, 11.0 us)
Async XLA Ops:
  0.0 55.6 %copy-start = (bf16[2,1,4096,128]{3,2,1,0:T(8,128)(2,1)S(1)}, bf16[2,1,4096,128]{3,2,1,0:T(8,128)(2,1)}, u32[]{:S(2)}) copy-start(bf16[2,1,4096,128]{3,2,1,0:T(8,128)(2,1)} %param.17) | copy-start | bytes 6291460
  0.0 16.8 %copy-start.2 = (s32[2,3,4096]{2,0,1:T(2,128)S(1)}, s32[2,3,4096]{2,0,1:T(2,128)}, u32[]{:S(2)}) copy-start(s32[2,3,4096]{2,0,1:T(2,128)} %param.18) | copy-start | bytes 294916
  3.5 16.1 %copy-start.5 = (s32[2]{0:T(128)S(1)}, s32[2]{0:T(128)}, u32[]{:S(2)}) copy-start(s32[2]{0:T(128)} %param.19) | copy-start | bytes 28
  4.9 46.0 %all-to-all-start = ((f32[32,2,1281]{2,1,0:T(2,128)}), f32[32,2,1281]{2,1,0:T(2,128)S(1)}, u32[]{:S(2)}, u32[]{:S(2)}) async-start(f32[32,2,1281]{2,1,0:T(2,128)} %copy.59), calls=%async_computation | async-start | bytes 720896 | tf_op jit(solution)/shard_map/all_to_all | solution.py:61
  19.5 3.8 %copy-start.4 = (bf16[1,10,128]{2,1,0:T(8,128)(2,1)S(1)}, bf16[1,10,128]{2,1,0:T(8,128)(2,1)}, u32[]{:S(2)}) copy-start(bf16[1,10,128]{2,1,0:T(8,128)(2,1)} %param.15) | copy-start | bytes 7684
  50.8 23.8 %copy-start.1 = (bf16[1024,256]{1,0:T(8,128)(2,1)S(1)}, bf16[1024,256]{1,0:T(8,128)(2,1)}, u32[]{:S(2)}) copy-start(bf16[1024,256]{1,0:T(8,128)(2,1)} %param.20) | copy-start | bytes 1572868
  51.7 32.9 %copy-start.6 = (bf16[256]{0:T(256)(128)(2,1)S(1)}, bf16[256]{0:T(256)(128)(2,1)}, u32[]{:S(2)}) copy-start(bf16[256]{0:T(256)(128)(2,1)} %param.21) | copy-start | bytes 1540
  51.8 34.6 %copy-start.3 = (bf16[64,256]{1,0:T(8,128)(2,1)S(1)}, bf16[64,256]{1,0:T(8,128)(2,1)}, u32[]{:S(2)}) copy-start(bf16[64,256]{1,0:T(8,128)(2,1)} %param.12) | copy-start | bytes 98308
  74.8 3.7 %collective-permute-start = (f32[64,256]{1,0:T(8,128)S(1)}, f32[64,256]{1,0:T(8,128)S(1)}, u32[]{:S(2)}, u32[]{:S(2)}) collective-permute-start(f32[64,256]{1,0:T(8,128)S(1)} %fusion.72), channel_id=1, source_target_pairs={{0,1},{1,0},{2,3},{3,2},{4,5},{5,4},{6,7},{7,6},{8,9},{9,8},{10,11... | collective-permute-start | bytes 196616 | tf_op jit(solution)/shard_map/ppermute | solution.py:74
  78.5 3.2 %collective-permute-start.1 = (f32[64,256]{1,0:T(8,128)S(1)}, f32[64,256]{1,0:T(8,128)S(1)}, u32[]{:S(2)}, u32[]{:S(2)}) collective-permute-start(f32[64,256]{1,0:T(8,128)S(1)} %add.436), channel_id=1, source_target_pairs={{0,2},{1,3},{2,0},{3,1},{4,6},{5,7},{6,4},{7,5},{8,10},{9,11},{10,... | collective-permute-start | bytes 196616 | tf_op jit(solution)/shard_map/ppermute | solution.py:74
  81.7 4.7 %collective-permute-start.2 = (f32[64,256]{1,0:T(8,128)S(1)}, f32[64,256]{1,0:T(8,128)S(1)}, u32[]{:S(2)}, u32[]{:S(2)}) collective-permute-start(f32[64,256]{1,0:T(8,128)S(1)} %add.437), channel_id=1, source_target_pairs={{0,4},{1,5},{2,6},{3,7},{4,0},{5,1},{6,2},{7,3},{8,12},{9,13},{10,... | collective-permute-start | bytes 196616 | tf_op jit(solution)/shard_map/ppermute | solution.py:74
  147.2 6.3 %collective-permute-start.3 = (f32[64,256]{1,0:T(8,128)S(1)}, f32[64,256]{1,0:T(8,128)S(1)}, u32[]{:S(2)}, u32[]{:S(2)}) collective-permute-start(f32[64,256]{1,0:T(8,128)S(1)} %fusion.73), channel_id=1, source_target_pairs={{0,1},{1,0},{2,3},{3,2},{4,5},{5,4},{6,7},{7,6},{8,9},{9,8},{10,11... | collective-permute-start | bytes 196616 | tf_op jit(solution)/shard_map/ppermute | solution.py:74
  153.6 3.2 %collective-permute-start.4 = (f32[64,256]{1,0:T(8,128)S(1)}, f32[64,256]{1,0:T(8,128)S(1)}, u32[]{:S(2)}, u32[]{:S(2)}) collective-permute-start(f32[64,256]{1,0:T(8,128)S(1)} %add.443), channel_id=1, source_target_pairs={{0,2},{1,3},{2,0},{3,1},{4,6},{5,7},{6,4},{7,5},{8,10},{9,11},{10,... | collective-permute-start | bytes 196616 | tf_op jit(solution)/shard_map/ppermute | solution.py:74
  156.8 4.7 %collective-permute-start.5 = (f32[64,256]{1,0:T(8,128)S(1)}, f32[64,256]{1,0:T(8,128)S(1)}, u32[]{:S(2)}, u32[]{:S(2)}) collective-permute-start(f32[64,256]{1,0:T(8,128)S(1)} %add.444), channel_id=1, source_target_pairs={{0,4},{1,5},{2,6},{3,7},{4,0},{5,1},{6,2},{7,3},{8,12},{9,13},{10,... | collective-permute-start | bytes 196616 | tf_op jit(solution)/shard_map/ppermute | solution.py:74

commit v5 on v3

--- a/solution.py
+++ b/solution.py
@@ -55,7 +55,16 @@
 
 def sum_all(x, axis):
     n = lax.axis_size(axis)
-    step = 1
+    x = x + lax.ppermute(x, axis, [(i, i ^ 1) for i in range(n)])
+    groups = n // 2
+    if groups == 4:
+        def shifted(k):
+            return lax.ppermute(
+                x, axis, [(i, ((i // 2 + k) % groups) * 2 + i % 2) for i in range(n)]
+            )
+
+        return (x + shifted(2)) + (shifted(1) + shifted(3))
+    step = 2
     while step < n:
         x = x + lax.ppermute(x, axis, [(i, i ^ step) for i in range(n)])
         step *= 2

time: 155 us -> 154 us (level)
  starting transfers between devices: 28.8 us -> 26.7 us
  blocking collectives: 64.2 us -> 65.8 us
    ppermute x6 -> x8, starting transfers between devices: 17 us -> 14.8 us  [the longest x6 7.53 us: shifted(): lax.ppermute(x, axis, [(i, (i // 2 + k) % groups * 2 + i % 2) for i in ra...]
    ppermute x6 -> x8, waiting for transfers between devices: 8.85 us -> 9.16 us  [the longest x6 7.36 us: shifted(): lax.ppermute(x, axis, [(i, (i // 2 + k) % groups * 2 + i % 2) for i in ra...]
  transfers between devices with their start and end apart: 7 -> 9, of which waited for: 6 -> 5; matrix products, arithmetic and copies ran while one was open for 17% -> 17% of each run, Pallas kernels for 0% -> 0%
where the time goes in v5:
time: 154 us; the launch traced here: 153 us
  blocking collectives  65.8 us (43%)
  starting transfers between devices  26.7 us (17%)
  other arithmetic  25.7 us (17%)
  local copies, waits for them, and re-layouts  14.7 us (10%)
  matrix products  10.9 us (7%)
  waiting for transfers between devices  9.17 us (6%)
    all_to_all x2, blocking collectives, gather_rows(): lax.all_to_all(copies, axis, 0, 0, tiled=False)  38.4 us
    all_to_all x1, blocking collectives, local(): lax.all_to_all(sent2.reshape(n_wide, sent2.shape[0] // n_wide, sent2.shap...  27.4 us
    concatenate x2, other arithmetic, rotate(): jnp.concatenate([leading * cosine - trailing * sine_table, trailing * cos...  18.7 us
    all_to_all x1, starting transfers between devices, reduce_rows(): return jnp.sum(lax.all_to_all(blocks, axis, 0, 0, tiled=False), axis=0)  11.9 us
    ppermute x6, starting transfers between devices, shifted(): lax.ppermute(x, axis, [(i, (i // 2 + k) % groups * 2 + i % 2) for i in ra...  7.53 us
    ppermute x6, waiting for transfers between devices, shifted(): lax.ppermute(x, axis, [(i, (i // 2 + k) % groups * 2 + i % 2) for i in ra...  7.36 us
    ppermute x2, starting transfers between devices, sum_all(): x = x + lax.ppermute(x, axis, [(i, i ^ 1) for i in range(n)])  7.27 us
    concatenate x2, local copies, waits for them, and re-layouts, local(): jnp.concatenate([partial2.astype(jnp.bfloat16), squares_hi[:, None], squa...  6.22 us
  transfers between devices with their start and end apart: 9, of which 5 were waited for; matrix products, arithmetic and copies ran while one was open for 17% of the time, Pallas kernels for 0%

profile of v5, /device:TPU:1, one launch (start us, length us, event | category | flops | bytes accessed | tf_op | source)
XLA Modules:
  0.0 153.1 jit_solution(2054993436948657330)
XLA Ops:
  2.1 1.3 copy.55
  3.9 1.0 copy.59
  4.9 11.9 %all-to-all-start = ((f32[32,2,1281]{2,1,0:T(2,128)}), f32[32,2,1281]{2,1,0:T(2,128)S(1)}, u32[]{:S(2)}, u32[]{:S(2)}) async-start(f32[32,2,1281]{2,1,0:T(2,128)} %copy.59), calls=%async_computation | async-start | bytes 720896 | tf_op jit(solution)/shard_map/all_to_all | solution.py:47
  16.8 2.6 %copy.62 = s32[2,3,4096]{1,2,0:T(8,128)} copy(s32[2,3,4096]{2,0,1:T(2,128)S(1)} %copy-done.2) | data formatting | bytes 196608 | tf_op args[6]
  19.8 1.5 gather_fusion
  21.8 1.9 %bitcast_convert_fusion = f32[2,1,4096,128]{3,2,0,1:T(8,128)S(1)} fusion(bf16[2,1,4096,128]{3,2,1,0:T(8,128)(2,1)} %param.16), kind=kLoop, calls=%fused_computation.13 | loop fusion | flops 1048576 | bytes 6291456 | tf_op jit(solution)/shard_map/convert_element_type | solution.py:105
  23.7 18.6 %fusion.7 = (bf16[2,4096,64]{2,1,0:T(8,128)(2,1)}, bf16[2,4096,64]{2,1,0:T(8,128)(2,1)}) fusion(f32[2,1,4096,128]{3,2,0,1:T(8,128)S(1)} %bitcast_convert_fusion, f32[64]{0:T(128)S(1)} %multiply_exponential_fusion, f32[2,4096]{1,0:T(2,128)S(1)} %get-tuple-element.19, f32[2,4096]{1,0:T(2,128)S(1)} %get-tuple-element.20, f32[2,4096]{1,0:T(2,128)S(1)} %get-tuple-element.18, ...), kind=kLoop, calls=%fused_computation.14 | loop fusion | flops 5767168 | bytes 6390144 | tf_op jit(solution)/shard_map/concatenate | solution.py:38
  43.2 3.6 %select_reduce_fusion = (f32[2,8]{1,0:T(2,128)S(1)}, f32[2,8,4096]{2,1,0:T(8,128)S(1)}) fusion(pred[2,4096]{1,0:T(4,128)(4,1)S(1)} %iota_compare_fusion, bf16[2,4096,64]{2,1,0:T(8,128)(2,1)} %get-tuple-element.17, bf16[2,4096,64]{2,1,0:T(8,128)(2,1)} %get-tuple-element.16, bf16[2,8,64]{2,1,0:T(8,128)(2,1)S(1)} %bitcast.59, bf16[2,8,64]{2,1,0:T(8,128)(2,1)S(1)} %bitcast.58), kind=kOutput, calls=%fused_computation.23 | convolution fusion | flops 21176304 | bytes 2371648 | tf_op jit(solution)/shard_map/rgjd,rgsd->rgjs/dot_general | solution.py:116
  47.6 18.4 %all_to_all.20 = bf16[32,2,1024]{2,1,0:T(2,128)(2,1)S(1)} all-to-all(bf16[32,2,1024]{2,1,0:T(2,128)(2,1)S(1)} %broadcast_in_dim.169), channel_id=1, replica_groups=mesh['wide'=32,'narrow'=8] {'wide'}, dimensions={0} | all-to-all | bytes 262144 | tf_op jit(solution)/shard_map/all_to_all | solution.py:53
  66.2 2.8 %collective-permute-start = (f32[64,256]{1,0:T(8,128)S(1)}, f32[64,256]{1,0:T(8,128)S(1)}, u32[]{:S(2)}, u32[]{:S(2)}) collective-permute-start(f32[64,256]{1,0:T(8,128)S(1)} %fusion.62), channel_id=1, source_target_pairs={{0,1},{1,0},{2,3},{3,2},{4,5},{5,4},{6,7},{7,6},{8,9},{9,8},{10,11... | collective-permute-start | bytes 196616 | tf_op jit(solution)/shard_map/ppermute | solution.py:58
  69.9 1.4 collective-permute-start.2
  71.3 1.5 collective-permute-start.3
  72.8 1.6 %collective-permute-start.1 = (f32[64,256]{1,0:T(8,128)S(1)}, f32[64,256]{1,0:T(8,128)S(1)}, u32[]{:S(2)}, u32[]{:S(2)}) collective-permute-start(f32[64,256]{1,0:T(8,128)S(1)} %add.105), channel_id=1, source_target_pairs={{0,4},{1,5},{2,6},{3,7},{4,0},{5,1},{6,2},{7,3},{8,12},{9,13},{10,... | collective-permute-start | bytes 196616 | tf_op jit(solution)/shard_map/ppermute | solution.py:62
  74.4 3.0 %collective-permute-done.1 = f32[64,256]{1,0:T(8,128)S(1)} collective-permute-done((f32[64,256]{1,0:T(8,128)S(1)}, f32[64,256]{1,0:T(8,128)S(1)}, u32[]{:S(2)}, u32[]{:S(2)}) %collective-permute-start.1) | collective-permute-done | bytes 65568 | tf_op jit(solution)/shard_map/ppermute | solution.py:62
  77.6 4.3 %convolution_convert_fusion = bf16[64,7392]{1,0:T(8,128)(2,1)} fusion(bf16[256,7392]{0,1:T(8,128)(2,1)} %bitcast.56, bf16[64,256]{1,0:T(8,128)(2,1)S(1)} %get-tuple-element.11, f32[256]{0:T(256)S(1)} %convert_element_type.232), kind=kOutput, calls=%fused_computation.1 | convolution fusion | flops 242743296 | bytes 4764672 | tf_op jit(solution)/shard_map/dot_general | solution.py:151
  81.9 2.4 %concatenate.70 = bf16[32,2,7392]{2,1,0:T(2,128)(2,1)S(1)} reshape(bf16[64,7392]{1,0:T(8,128)(2,1)} %convolution_convert_fusion) | data formatting | bytes 1892352 | tf_op jit(solution)/shard_map/concatenate | solution.py:154
  84.7 3.8 %concatenate.71 = bf16[32,2,7394]{2,1,0:T(2,128)(2,1)} concatenate(bf16[32,2,7392]{2,1,0:T(2,128)(2,1)S(1)} %concatenate.70, bf16[32,2,1]{2,1,0:T(2,128)(2,1)S(1)} %copy.66, bf16[32,2,1]{2,1,0:T(2,128)(2,1)S(1)} %copy.67), dimensions={2} | concatenate | bytes 1892864 | tf_op jit(solution)/shard_map/concatenate | solution.py:154
  88.5 27.4 %all_to_all.21 = bf16[32,2,7394]{2,1,0:T(2,128)(2,1)S(1)} all-to-all(bf16[32,2,7394]{2,1,0:T(2,128)(2,1)} %concatenate.71), channel_id=1, replica_groups=mesh['wide'=32,'narrow'=8] {'wide'}, dimensions={0} | all-to-all | bytes 1892864 | tf_op jit(solution)/shard_map/all_to_all | solution.py:158
  117.3 20.1 %all_to_all.22 = bf16[32,2,3696]{2,1,0:T(2,128)(2,1)S(1)} all-to-all(bf16[32,2,3696]{2,1,0:T(2,128)(2,1)S(1)} %broadcast_in_dim.170), channel_id=1, replica_groups=mesh['wide'=32,'narrow'=8] {'wide'}, dimensions={0} | all-to-all | bytes 946176 | tf_op jit(solution)/shard_map/all_to_all | solution.py:53
  137.8 2.0 %fusion.63 = f32[64,256]{1,0:T(8,128)S(1)} fusion(bf16[64,3696]{1,0:T(8,128)(2,1)S(1)} %reshape.688, bf16[3696,256]{1,0:T(8,128)(2,1)} %param.23), kind=kOutput, calls=%fused_computation.106 | convolution fusion | flops 121110528 | bytes 2430976 | tf_op jit(solution)/shard_map/dot_general | solution.py:168
  139.7 4.5 %collective-permute-start.4 = (f32[64,256]{1,0:T(8,128)S(1)}, f32[64,256]{1,0:T(8,128)S(1)}, u32[]{:S(2)}, u32[]{:S(2)}) collective-permute-start(f32[64,256]{1,0:T(8,128)S(1)} %fusion.63), channel_id=1, source_target_pairs={{0,1},{1,0},{2,3},{3,2},{4,5},{5,4},{6,7},{7,6},{8,9},{9,8},{10,11... | collective-permute-start | bytes 196616 | tf_op jit(solution)/shard_map/ppermute | solution.py:58
  145.7 2.2 %collective-permute-start.7 = (f32[64,256]{1,0:T(8,128)S(1)}, f32[64,256]{1,0:T(8,128)S(1)}, u32[]{:S(2)}, u32[]{:S(2)}) collective-permute-start(f32[64,256]{1,0:T(8,128)S(1)} %add.113), channel_id=1, source_target_pairs={{0,6},{1,7},{2,0},{3,1},{4,2},{5,3},{6,4},{7,5},{8,14},{9,15},{10,... | collective-permute-start | bytes 196616 | tf_op jit(solution)/shard_map/ppermute | solution.py:62
  148.2 1.3 collective-permute-done.6
  149.5 3.0 %collective-permute-done.5 = f32[64,256]{1,0:T(8,128)S(1)} collective-permute-done((f32[64,256]{1,0:T(8,128)S(1)}, f32[64,256]{1,0:T(8,128)S(1)}, u32[]{:S(2)}, u32[]{:S(2)}) %collective-permute-start.5) | collective-permute-done | bytes 65568 | tf_op jit(solution)/shard_map/ppermute | solution.py:62
  (80 shorter events, 11.0 us)
Async XLA Ops:
  0.0 47.0 %copy-start = (bf16[2,1,4096,128]{3,2,1,0:T(8,128)(2,1)S(1)}, bf16[2,1,4096,128]{3,2,1,0:T(8,128)(2,1)}, u32[]{:S(2)}) copy-start(bf16[2,1,4096,128]{3,2,1,0:T(8,128)(2,1)} %param.17) | copy-start | bytes 6291460
  0.0 16.8 %copy-start.2 = (s32[2,3,4096]{2,0,1:T(2,128)S(1)}, s32[2,3,4096]{2,0,1:T(2,128)}, u32[]{:S(2)}) copy-start(s32[2,3,4096]{2,0,1:T(2,128)} %param.18) | copy-start | bytes 294916
  3.5 16.0 %copy-start.5 = (s32[2]{0:T(128)S(1)}, s32[2]{0:T(128)}, u32[]{:S(2)}) copy-start(s32[2]{0:T(128)} %param.19) | copy-start | bytes 28
  4.9 37.5 %all-to-all-start = ((f32[32,2,1281]{2,1,0:T(2,128)}), f32[32,2,1281]{2,1,0:T(2,128)S(1)}, u32[]{:S(2)}, u32[]{:S(2)}) async-start(f32[32,2,1281]{2,1,0:T(2,128)} %copy.59), calls=%async_computation | async-start | bytes 720896 | tf_op jit(solution)/shard_map/all_to_all | solution.py:47
  19.5 4.2 %copy-start.4 = (bf16[1,10,128]{2,1,0:T(8,128)(2,1)S(1)}, bf16[1,10,128]{2,1,0:T(8,128)(2,1)}, u32[]{:S(2)}) copy-start(bf16[1,10,128]{2,1,0:T(8,128)(2,1)} %param.15) | copy-start | bytes 7684
  43.2 22.8 %copy-start.1 = (bf16[1024,256]{1,0:T(8,128)(2,1)S(1)}, bf16[1024,256]{1,0:T(8,128)(2,1)}, u32[]{:S(2)}) copy-start(bf16[1024,256]{1,0:T(8,128)(2,1)} %param.20) | copy-start | bytes 1572868
  43.2 31.2 %copy-start.6 = (bf16[256]{0:T(256)(128)(2,1)S(1)}, bf16[256]{0:T(256)(128)(2,1)}, u32[]{:S(2)}) copy-start(bf16[256]{0:T(256)(128)(2,1)} %param.21) | copy-start | bytes 1540
  43.2 34.3 %copy-start.3 = (bf16[64,256]{1,0:T(8,128)(2,1)S(1)}, bf16[64,256]{1,0:T(8,128)(2,1)}, u32[]{:S(2)}) copy-start(bf16[64,256]{1,0:T(8,128)(2,1)} %param.12) | copy-start | bytes 98308
  66.2 3.7 %collective-permute-start = (f32[64,256]{1,0:T(8,128)S(1)}, f32[64,256]{1,0:T(8,128)S(1)}, u32[]{:S(2)}, u32[]{:S(2)}) collective-permute-start(f32[64,256]{1,0:T(8,128)S(1)} %fusion.62), channel_id=1, source_target_pairs={{0,1},{1,0},{2,3},{3,2},{4,5},{5,4},{6,7},{7,6},{8,9},{9,8},{10,11... | collective-permute-start | bytes 196616 | tf_op jit(solution)/shard_map/ppermute | solution.py:58
  69.9 4.5 %collective-permute-start.2 = (f32[64,256]{1,0:T(8,128)S(1)}, f32[64,256]{1,0:T(8,128)S(1)}, u32[]{:S(2)}, u32[]{:S(2)}) collective-permute-start(f32[64,256]{1,0:T(8,128)S(1)} %add.105), channel_id=1, source_target_pairs={{0,2},{1,3},{2,4},{3,5},{4,6},{5,7},{6,0},{7,1},{8,10},{9,11},{10,... | collective-permute-start | bytes 196616 | tf_op jit(solution)/shard_map/ppermute | solution.py:62
  71.3 3.1 %collective-permute-start.3 = (f32[64,256]{1,0:T(8,128)S(1)}, f32[64,256]{1,0:T(8,128)S(1)}, u32[]{:S(2)}, u32[]{:S(2)}) collective-permute-start(f32[64,256]{1,0:T(8,128)S(1)} %add.105), channel_id=1, source_target_pairs={{0,6},{1,7},{2,0},{3,1},{4,2},{5,3},{6,4},{7,5},{8,14},{9,15},{10,... | collective-permute-start | bytes 196616 | tf_op jit(solution)/shard_map/ppermute | solution.py:62
  72.8 4.6 %collective-permute-start.1 = (f32[64,256]{1,0:T(8,128)S(1)}, f32[64,256]{1,0:T(8,128)S(1)}, u32[]{:S(2)}, u32[]{:S(2)}) collective-permute-start(f32[64,256]{1,0:T(8,128)S(1)} %add.105), channel_id=1, source_target_pairs={{0,4},{1,5},{2,6},{3,7},{4,0},{5,1},{6,2},{7,3},{8,12},{9,13},{10,... | collective-permute-start | bytes 196616 | tf_op jit(solution)/shard_map/ppermute | solution.py:62
  139.7 5.4 %collective-permute-start.4 = (f32[64,256]{1,0:T(8,128)S(1)}, f32[64,256]{1,0:T(8,128)S(1)}, u32[]{:S(2)}, u32[]{:S(2)}) collective-permute-start(f32[64,256]{1,0:T(8,128)S(1)} %fusion.63), channel_id=1, source_target_pairs={{0,1},{1,0},{2,3},{3,2},{4,5},{5,4},{6,7},{7,6},{8,9},{9,8},{10,11... | collective-permute-start | bytes 196616 | tf_op jit(solution)/shard_map/ppermute | solution.py:58
  145.1 4.4 %collective-permute-start.6 = (f32[64,256]{1,0:T(8,128)S(1)}, f32[64,256]{1,0:T(8,128)S(1)}, u32[]{:S(2)}, u32[]{:S(2)}) collective-permute-start(f32[64,256]{1,0:T(8,128)S(1)} %add.113), channel_id=1, source_target_pairs={{0,2},{1,3},{2,4},{3,5},{4,6},{5,7},{6,0},{7,1},{8,10},{9,11},{10,... | collective-permute-start | bytes 196616 | tf_op jit(solution)/shard_map/ppermute | solution.py:62
  145.7 3.8 %collective-permute-start.7 = (f32[64,256]{1,0:T(8,128)S(1)}, f32[64,256]{1,0:T(8,128)S(1)}, u32[]{:S(2)}, u32[]{:S(2)}) collective-permute-start(f32[64,256]{1,0:T(8,128)S(1)} %add.113), channel_id=1, source_target_pairs={{0,6},{1,7},{2,0},{3,1},{4,2},{5,3},{6,4},{7,5},{8,14},{9,15},{10,... | collective-permute-start | bytes 196616 | tf_op jit(solution)/shard_map/ppermute | solution.py:62
  147.9 4.6 %collective-permute-start.5 = (f32[64,256]{1,0:T(8,128)S(1)}, f32[64,256]{1,0:T(8,128)S(1)}, u32[]{:S(2)}, u32[]{:S(2)}) collective-permute-start(f32[64,256]{1,0:T(8,128)S(1)} %add.113), channel_id=1, source_target_pairs={{0,4},{1,5},{2,6},{3,7},{4,0},{5,1},{6,2},{7,3},{8,12},{9,13},{10,... | collective-permute-start | bytes 196616 | tf_op jit(solution)/shard_map/ppermute | solution.py:62

commit v6 on v5

--- a/solution.py
+++ b/solution.py
@@ -151,9 +151,9 @@
     partial2 = jnp.dot(scaled2, gate_up_flat, preferred_element_type=jnp.float32)
     squares_hi = resid_squares.astype(jnp.bfloat16)
     squares_lo = (resid_squares - squares_hi.astype(jnp.float32)).astype(jnp.bfloat16)
-    sent2 = jnp.concatenate(
-        [partial2.astype(jnp.bfloat16), squares_hi[:, None], squares_lo[:, None]], axis=1
-    )
+    sent2 = jnp.pad(partial2.astype(jnp.bfloat16), ((0, 0), (0, 2)))
+    sent2 = sent2.at[:, 2 * hidden_local].set(squares_hi)
+    sent2 = sent2.at[:, 2 * hidden_local + 1].set(squares_lo)
     n_wide = lax.axis_size("wide")
     received2 = lax.all_to_all(
         sent2.reshape(n_wide, sent2.shape[0] // n_wide, sent2.shape[1]), "wide", 0, 0, tiled=False

time: 154 us -> 149 us (0.968)
  local copies, waits for them, and re-layouts: 14.7 us -> 9.77 us
    concatenate x2 -> x0, local copies, waits for them, and re-layouts: 6.22 us -> none  [local(): jnp.concatenate([partial2.astype(jnp.bfloat16), squares_hi[:, None], squa...]
  transfers between devices with their start and end apart: 9 -> 9, of which waited for: 5 -> 5; matrix products, arithmetic and copies ran while one was open for 17% -> 18% of each run, Pallas kernels for 0% -> 0%
where the time goes in v6:
time: 149 us; the launch traced here: 148 us
  blocking collectives  65.8 us (44%)
  other arithmetic  27 us (18%)
  starting transfers between devices  26.7 us (18%)
  matrix products  9.91 us (7%)
  local copies, waits for them, and re-layouts  9.77 us (7%)
  waiting for transfers between devices  8.53 us (6%)
    all_to_all x2, blocking collectives, gather_rows(): lax.all_to_all(copies, axis, 0, 0, tiled=False)  38.4 us
    all_to_all x1, blocking collectives, local(): lax.all_to_all(sent2.reshape(n_wide, sent2.shape[0] // n_wide, sent2.shap...  27.4 us
    concatenate x2, other arithmetic, rotate(): jnp.concatenate([leading * cosine - trailing * sine_table, trailing * cos...  18.7 us
    all_to_all x1, starting transfers between devices, reduce_rows(): return jnp.sum(lax.all_to_all(blocks, axis, 0, 0, tiled=False), axis=0)  11.9 us
    ppermute x6, starting transfers between devices, shifted(): lax.ppermute(x, axis, [(i, (i // 2 + k) % groups * 2 + i % 2) for i in ra...  7.53 us
    ppermute x2, starting transfers between devices, sum_all(): x = x + lax.ppermute(x, axis, [(i, i ^ 1) for i in range(n)])  7.27 us
    ppermute x6, waiting for transfers between devices, shifted(): lax.ppermute(x, axis, [(i, (i // 2 + k) % groups * 2 + i % 2) for i in ra...  6.72 us
    unnamed x18, local copies, waits for them, and re-layouts  4 us
  transfers between devices with their start and end apart: 9, of which 5 were waited for; matrix products, arithmetic and copies ran while one was open for 18% of the time, Pallas kernels for 0%

profile of v6, /device:TPU:1, one launch (start us, length us, event | category | flops | bytes accessed | tf_op | source)
XLA Modules:
  0.0 148.0 jit_solution(6374347293041691211)
XLA Ops:
  2.1 1.3 copy.44
  3.9 1.0 copy.48
  4.9 11.9 %all-to-all-start = ((f32[32,2,1281]{2,1,0:T(2,128)}), f32[32,2,1281]{2,1,0:T(2,128)S(1)}, u32[]{:S(2)}, u32[]{:S(2)}) async-start(f32[32,2,1281]{2,1,0:T(2,128)} %copy.48), calls=%async_computation | async-start | bytes 720896 | tf_op jit(solution)/shard_map/all_to_all | solution.py:47
  16.8 2.6 %copy.51 = s32[2,3,4096]{1,2,0:T(8,128)} copy(s32[2,3,4096]{2,0,1:T(2,128)S(1)} %copy-done.2) | data formatting | bytes 196608 | tf_op args[6]
  19.8 1.5 gather_fusion
  21.8 1.9 %bitcast_convert_fusion = f32[2,1,4096,128]{3,2,0,1:T(8,128)S(1)} fusion(bf16[2,1,4096,128]{3,2,1,0:T(8,128)(2,1)} %param.20), kind=kLoop, calls=%fused_computation.13 | loop fusion | flops 1048576 | bytes 6291456 | tf_op jit(solution)/shard_map/convert_element_type | solution.py:105
  23.7 18.6 %fusion.7 = (bf16[2,4096,64]{2,1,0:T(8,128)(2,1)}, bf16[2,4096,64]{2,1,0:T(8,128)(2,1)}) fusion(f32[2,1,4096,128]{3,2,0,1:T(8,128)S(1)} %bitcast_convert_fusion, f32[64]{0:T(128)S(1)} %multiply_exponential_fusion, f32[2,4096]{1,0:T(2,128)S(1)} %get-tuple-element.41, f32[2,4096]{1,0:T(2,128)S(1)} %get-tuple-element.42, f32[2,4096]{1,0:T(2,128)S(1)} %get-tuple-element.40, ...), kind=kLoop, calls=%fused_computation.14 | loop fusion | flops 5767168 | bytes 6390144 | tf_op jit(solution)/shard_map/concatenate | solution.py:38
  43.2 3.6 %select_reduce_fusion = (f32[2,8]{1,0:T(2,128)S(1)}, f32[2,8,4096]{2,1,0:T(8,128)S(1)}) fusion(pred[2,4096]{1,0:T(4,128)(4,1)S(1)} %iota_compare_fusion, bf16[2,4096,64]{2,1,0:T(8,128)(2,1)} %get-tuple-element.39, bf16[2,4096,64]{2,1,0:T(8,128)(2,1)} %get-tuple-element.38, bf16[2,8,64]{2,1,0:T(8,128)(2,1)S(1)} %bitcast.60, bf16[2,8,64]{2,1,0:T(8,128)(2,1)S(1)} %bitcast.59), kind=kOutput, calls=%fused_computation.23 | convolution fusion | flops 21176304 | bytes 2371648 | tf_op jit(solution)/shard_map/rgjd,rgsd->rgjs/dot_general | solution.py:116
  47.6 18.4 %all_to_all.20 = bf16[32,2,1024]{2,1,0:T(2,128)(2,1)S(1)} all-to-all(bf16[32,2,1024]{2,1,0:T(2,128)(2,1)S(1)} %broadcast_in_dim.167), channel_id=1, replica_groups=mesh['wide'=32,'narrow'=8] {'wide'}, dimensions={0} | all-to-all | bytes 262144 | tf_op jit(solution)/shard_map/all_to_all | solution.py:53
  66.2 2.8 %collective-permute-start = (f32[64,256]{1,0:T(8,128)S(1)}, f32[64,256]{1,0:T(8,128)S(1)}, u32[]{:S(2)}, u32[]{:S(2)}) collective-permute-start(f32[64,256]{1,0:T(8,128)S(1)} %fusion.62), channel_id=1, source_target_pairs={{0,1},{1,0},{2,3},{3,2},{4,5},{5,4},{6,7},{7,6},{8,9},{9,8},{10,11... | collective-permute-start | bytes 196616 | tf_op jit(solution)/shard_map/ppermute | solution.py:58
  69.0 0.9 collective-permute-done
  69.9 1.4 collective-permute-start.2
  71.3 1.5 %collective-permute-start.3 = (f32[64,256]{1,0:T(8,128)S(1)}, f32[64,256]{1,0:T(8,128)S(1)}, u32[]{:S(2)}, u32[]{:S(2)}) collective-permute-start(f32[64,256]{1,0:T(8,128)S(1)} %add.111), channel_id=1, source_target_pairs={{0,6},{1,7},{2,0},{3,1},{4,2},{5,3},{6,4},{7,5},{8,14},{9,15},{10,... | collective-permute-start | bytes 196616 | tf_op jit(solution)/shard_map/ppermute | solution.py:62
  72.8 1.6 %collective-permute-start.1 = (f32[64,256]{1,0:T(8,128)S(1)}, f32[64,256]{1,0:T(8,128)S(1)}, u32[]{:S(2)}, u32[]{:S(2)}) collective-permute-start(f32[64,256]{1,0:T(8,128)S(1)} %add.111), channel_id=1, source_target_pairs={{0,4},{1,5},{2,6},{3,7},{4,0},{5,1},{6,2},{7,3},{8,12},{9,13},{10,... | collective-permute-start | bytes 196616 | tf_op jit(solution)/shard_map/ppermute | solution.py:62
  75.0 2.4 %collective-permute-done.1 = f32[64,256]{1,0:T(8,128)S(1)} collective-permute-done((f32[64,256]{1,0:T(8,128)S(1)}, f32[64,256]{1,0:T(8,128)S(1)}, u32[]{:S(2)}, u32[]{:S(2)}) %collective-permute-start.1) | collective-permute-done | bytes 65568 | tf_op jit(solution)/shard_map/ppermute | solution.py:62
  78.4 3.3 %convolution_convert_fusion = bf16[64,7392]{1,0:T(8,128)(2,1)S(1)} fusion(bf16[256,7392]{0,1:T(8,128)(2,1)} %bitcast.57, bf16[64,256]{1,0:T(8,128)(2,1)S(1)} %get-tuple-element.33, f32[256]{0:T(256)S(1)} %convert_element_type.223), kind=kOutput, calls=%fused_computation.1 | convolution fusion | flops 242743296 | bytes 4764672 | tf_op jit(solution)/shard_map/dot_general | solution.py:151
  82.1 1.3 reshape.719
  83.4 27.4 %all_to_all.21 = bf16[32,2,7394]{2,1,0:T(2,128)(2,1)S(1)} all-to-all(bf16[32,2,7394]{2,1,0:T(2,128)(2,1)} %reshape.719), channel_id=1, replica_groups=mesh['wide'=32,'narrow'=8] {'wide'}, dimensions={0} | all-to-all | bytes 1892864 | tf_op jit(solution)/shard_map/all_to_all | solution.py:158
  112.2 20.1 %all_to_all.22 = bf16[32,2,3696]{2,1,0:T(2,128)(2,1)S(1)} all-to-all(bf16[32,2,3696]{2,1,0:T(2,128)(2,1)S(1)} %broadcast_in_dim.168), channel_id=1, replica_groups=mesh['wide'=32,'narrow'=8] {'wide'}, dimensions={0} | all-to-all | bytes 946176 | tf_op jit(solution)/shard_map/all_to_all | solution.py:53
  132.6 2.0 %fusion.63 = f32[64,256]{1,0:T(8,128)S(1)} fusion(bf16[64,3696]{1,0:T(8,128)(2,1)S(1)} %reshape.720, bf16[3696,256]{1,0:T(8,128)(2,1)} %param.27), kind=kOutput, calls=%fused_computation.108 | convolution fusion | flops 121110528 | bytes 2430976 | tf_op jit(solution)/shard_map/dot_general | solution.py:168
  134.6 4.5 %collective-permute-start.4 = (f32[64,256]{1,0:T(8,128)S(1)}, f32[64,256]{1,0:T(8,128)S(1)}, u32[]{:S(2)}, u32[]{:S(2)}) collective-permute-start(f32[64,256]{1,0:T(8,128)S(1)} %fusion.63), channel_id=1, source_target_pairs={{0,1},{1,0},{2,3},{3,2},{4,5},{5,4},{6,7},{7,6},{8,9},{9,8},{10,11... | collective-permute-start | bytes 196616 | tf_op jit(solution)/shard_map/ppermute | solution.py:58
  140.6 2.2 %collective-permute-start.7 = (f32[64,256]{1,0:T(8,128)S(1)}, f32[64,256]{1,0:T(8,128)S(1)}, u32[]{:S(2)}, u32[]{:S(2)}) collective-permute-start(f32[64,256]{1,0:T(8,128)S(1)} %add.119), channel_id=1, source_target_pairs={{0,6},{1,7},{2,0},{3,1},{4,2},{5,3},{6,4},{7,5},{8,14},{9,15},{10,... | collective-permute-start | bytes 196616 | tf_op jit(solution)/shard_map/ppermute | solution.py:62
  143.0 1.3 collective-permute-done.6
  144.4 3.0 %collective-permute-done.5 = f32[64,256]{1,0:T(8,128)S(1)} collective-permute-done((f32[64,256]{1,0:T(8,128)S(1)}, f32[64,256]{1,0:T(8,128)S(1)}, u32[]{:S(2)}, u32[]{:S(2)}) %collective-permute-start.5) | collective-permute-done | bytes 65568 | tf_op jit(solution)/shard_map/ppermute | solution.py:62
  (81 shorter events, 11.4 us)
Async XLA Ops:
  0.0 47.0 %copy-start = (bf16[2,1,4096,128]{3,2,1,0:T(8,128)(2,1)S(1)}, bf16[2,1,4096,128]{3,2,1,0:T(8,128)(2,1)}, u32[]{:S(2)}) copy-start(bf16[2,1,4096,128]{3,2,1,0:T(8,128)(2,1)} %param.21) | copy-start | bytes 6291460
  0.0 16.8 %copy-start.2 = (s32[2,3,4096]{2,0,1:T(2,128)S(1)}, s32[2,3,4096]{2,0,1:T(2,128)}, u32[]{:S(2)}) copy-start(s32[2,3,4096]{2,0,1:T(2,128)} %param.22) | copy-start | bytes 294916
  3.5 16.0 %copy-start.5 = (s32[2]{0:T(128)S(1)}, s32[2]{0:T(128)}, u32[]{:S(2)}) copy-start(s32[2]{0:T(128)} %param.23) | copy-start | bytes 28
  4.9 37.5 %all-to-all-start = ((f32[32,2,1281]{2,1,0:T(2,128)}), f32[32,2,1281]{2,1,0:T(2,128)S(1)}, u32[]{:S(2)}, u32[]{:S(2)}) async-start(f32[32,2,1281]{2,1,0:T(2,128)} %copy.48), calls=%async_computation | async-start | bytes 720896 | tf_op jit(solution)/shard_map/all_to_all | solution.py:47
  19.5 4.2 %copy-start.4 = (bf16[1,10,128]{2,1,0:T(8,128)(2,1)S(1)}, bf16[1,10,128]{2,1,0:T(8,128)(2,1)}, u32[]{:S(2)}) copy-start(bf16[1,10,128]{2,1,0:T(8,128)(2,1)} %param.19) | copy-start | bytes 7684
  43.2 22.8 %copy-start.1 = (bf16[1024,256]{1,0:T(8,128)(2,1)S(1)}, bf16[1024,256]{1,0:T(8,128)(2,1)}, u32[]{:S(2)}) copy-start(bf16[1024,256]{1,0:T(8,128)(2,1)} %param.24) | copy-start | bytes 1572868
  43.2 31.2 %copy-start.6 = (bf16[256]{0:T(256)(128)(2,1)S(1)}, bf16[256]{0:T(256)(128)(2,1)}, u32[]{:S(2)}) copy-start(bf16[256]{0:T(256)(128)(2,1)} %param.25) | copy-start | bytes 1540
  43.2 34.3 %copy-start.3 = (bf16[64,256]{1,0:T(8,128)(2,1)S(1)}, bf16[64,256]{1,0:T(8,128)(2,1)}, u32[]{:S(2)}) copy-start(bf16[64,256]{1,0:T(8,128)(2,1)} %param.16) | copy-start | bytes 98308
  66.2 3.7 %collective-permute-start = (f32[64,256]{1,0:T(8,128)S(1)}, f32[64,256]{1,0:T(8,128)S(1)}, u32[]{:S(2)}, u32[]{:S(2)}) collective-permute-start(f32[64,256]{1,0:T(8,128)S(1)} %fusion.62), channel_id=1, source_target_pairs={{0,1},{1,0},{2,3},{3,2},{4,5},{5,4},{6,7},{7,6},{8,9},{9,8},{10,11... | collective-permute-start | bytes 196616 | tf_op jit(solution)/shard_map/ppermute | solution.py:58
  69.9 5.1 %collective-permute-start.2 = (f32[64,256]{1,0:T(8,128)S(1)}, f32[64,256]{1,0:T(8,128)S(1)}, u32[]{:S(2)}, u32[]{:S(2)}) collective-permute-start(f32[64,256]{1,0:T(8,128)S(1)} %add.111), channel_id=1, source_target_pairs={{0,2},{1,3},{2,4},{3,5},{4,6},{5,7},{6,0},{7,1},{8,10},{9,11},{10,... | collective-permute-start | bytes 196616 | tf_op jit(solution)/shard_map/ppermute | solution.py:62
  71.3 3.7 %collective-permute-start.3 = (f32[64,256]{1,0:T(8,128)S(1)}, f32[64,256]{1,0:T(8,128)S(1)}, u32[]{:S(2)}, u32[]{:S(2)}) collective-permute-start(f32[64,256]{1,0:T(8,128)S(1)} %add.111), channel_id=1, source_target_pairs={{0,6},{1,7},{2,0},{3,1},{4,2},{5,3},{6,4},{7,5},{8,14},{9,15},{10,... | collective-permute-start | bytes 196616 | tf_op jit(solution)/shard_map/ppermute | solution.py:62
  72.8 4.6 %collective-permute-start.1 = (f32[64,256]{1,0:T(8,128)S(1)}, f32[64,256]{1,0:T(8,128)S(1)}, u32[]{:S(2)}, u32[]{:S(2)}) collective-permute-start(f32[64,256]{1,0:T(8,128)S(1)} %add.111), channel_id=1, source_target_pairs={{0,4},{1,5},{2,6},{3,7},{4,0},{5,1},{6,2},{7,3},{8,12},{9,13},{10,... | collective-permute-start | bytes 196616 | tf_op jit(solution)/shard_map/ppermute | solution.py:62
  134.6 5.4 %collective-permute-start.4 = (f32[64,256]{1,0:T(8,128)S(1)}, f32[64,256]{1,0:T(8,128)S(1)}, u32[]{:S(2)}, u32[]{:S(2)}) collective-permute-start(f32[64,256]{1,0:T(8,128)S(1)} %fusion.63), channel_id=1, source_target_pairs={{0,1},{1,0},{2,3},{3,2},{4,5},{5,4},{6,7},{7,6},{8,9},{9,8},{10,11... | collective-permute-start | bytes 196616 | tf_op jit(solution)/shard_map/ppermute | solution.py:58
  140.0 4.4 %collective-permute-start.6 = (f32[64,256]{1,0:T(8,128)S(1)}, f32[64,256]{1,0:T(8,128)S(1)}, u32[]{:S(2)}, u32[]{:S(2)}) collective-permute-start(f32[64,256]{1,0:T(8,128)S(1)} %add.119), channel_id=1, source_target_pairs={{0,2},{1,3},{2,4},{3,5},{4,6},{5,7},{6,0},{7,1},{8,10},{9,11},{10,... | collective-permute-start | bytes 196616 | tf_op jit(solution)/shard_map/ppermute | solution.py:62
  140.6 3.8 %collective-permute-start.7 = (f32[64,256]{1,0:T(8,128)S(1)}, f32[64,256]{1,0:T(8,128)S(1)}, u32[]{:S(2)}, u32[]{:S(2)}) collective-permute-start(f32[64,256]{1,0:T(8,128)S(1)} %add.119), channel_id=1, source_target_pairs={{0,6},{1,7},{2,0},{3,1},{4,2},{5,3},{6,4},{7,5},{8,14},{9,15},{10,... | collective-permute-start | bytes 196616 | tf_op jit(solution)/shard_map/ppermute | solution.py:62
  142.7 4.6 %collective-permute-start.5 = (f32[64,256]{1,0:T(8,128)S(1)}, f32[64,256]{1,0:T(8,128)S(1)}, u32[]{:S(2)}, u32[]{:S(2)}) collective-permute-start(f32[64,256]{1,0:T(8,128)S(1)} %add.119), channel_id=1, source_target_pairs={{0,4},{1,5},{2,6},{3,7},{4,0},{5,1},{6,2},{7,3},{8,12},{9,13},{10,... | collective-permute-start | bytes 196616 | tf_op jit(solution)/shard_map/ppermute | solution.py:62

commit v7 on v6

--- a/solution.py
+++ b/solution.py
@@ -105,7 +105,8 @@
     keys_rot = rotate(cache_keys.astype(jnp.float32), cosine[:, None], sine_table[:, None]).astype(
         jnp.bfloat16
     )
-    new_position = jnp.take_along_axis(positions, lengths[:, None, None], axis=2)
+    at_new_slot = jnp.arange(CACHE)[None, None, :] == lengths[:, None, None]
+    new_position = jnp.sum(jnp.where(at_new_slot, positions, 0), axis=2, keepdims=True)
     cos_new, sin_new = mrope_tables(new_position)
     query = rotate(projected[:, :, :group_size], cos_new[:, None], sin_new[:, None]).astype(
         jnp.bfloat16

time: 149 us -> 147 us (0.987)
  local copies, waits for them, and re-layouts: 9.77 us -> 5.72 us
  other arithmetic: 27 us -> 30 us
    unnamed x18 -> x16, local copies, waits for them, and re-layouts: 4 us -> 1.38 us
    convert_element_type x1, other arithmetic: 1.87 us -> 3.79 us  [local(): cache_keys.astype(jnp.float32)]
    gather x2 -> x0, local copies, waits for them, and re-layouts: 1.56 us -> none  [local(): jnp.take_along_axis(positions, lengths[:, None, None], axis=2)]
  transfers between devices with their start and end apart: 9 -> 9, of which waited for: 5 -> 5; matrix products, arithmetic and copies ran while one was open for 18% -> 17% of each run, Pallas kernels for 0% -> 0%
where the time goes in v7:
time: 147 us
  blocking collectives  65.8 us (45%)
  other arithmetic  30 us (20%)
  starting transfers between devices  26.7 us (18%)
  matrix products  9.91 us (7%)
  waiting for transfers between devices  8.53 us (6%)
  local copies, waits for them, and re-layouts  5.72 us (4%)
    all_to_all x2, blocking collectives, gather_rows(): lax.all_to_all(copies, axis, 0, 0, tiled=False)  38.4 us
    all_to_all x1, blocking collectives, local(): lax.all_to_all(sent2.reshape(n_wide, sent2.shape[0] // n_wide, sent2.shap...  27.4 us
    concatenate x2, other arithmetic, rotate(): jnp.concatenate([leading * cosine - trailing * sine_table, trailing * cos...  19.8 us
    all_to_all x1, starting transfers between devices, reduce_rows(): return jnp.sum(lax.all_to_all(blocks, axis, 0, 0, tiled=False), axis=0)  11.9 us
    ppermute x6, starting transfers between devices, shifted(): lax.ppermute(x, axis, [(i, (i // 2 + k) % groups * 2 + i % 2) for i in ra...  7.53 us
    ppermute x2, starting transfers between devices, sum_all(): x = x + lax.ppermute(x, axis, [(i, i ^ 1) for i in range(n)])  7.28 us
    ppermute x6, waiting for transfers between devices, shifted(): lax.ppermute(x, axis, [(i, (i // 2 + k) % groups * 2 + i % 2) for i in ra...  6.72 us
    convert_element_type x1, other arithmetic, local(): cache_keys.astype(jnp.float32)  3.79 us
  transfers between devices with their start and end apart: 9, of which 5 were waited for; matrix products, arithmetic and copies ran while one was open for 17% of the time, Pallas kernels for 0%

profile of v7, /device:TPU:1, one launch (start us, length us, event | category | flops | bytes accessed | tf_op | source)
XLA Modules:
  0.0 146.9 jit_solution(5033470225882967759)
XLA Ops:
  0.8 0.9 fusion.27
  2.1 1.3 copy.39
  3.9 1.1 copy.43
  4.9 11.9 %all-to-all-start = ((f32[32,2,1281]{2,1,0:T(2,128)}), f32[32,2,1281]{2,1,0:T(2,128)S(1)}, u32[]{:S(2)}, u32[]{:S(2)}) async-start(f32[32,2,1281]{2,1,0:T(2,128)} %copy.43), calls=%async_computation | async-start | bytes 720896 | tf_op jit(solution)/shard_map/all_to_all | solution.py:47
  16.9 3.8 %bitcast_convert_fusion = f32[2,1,4096,128]{3,2,0,1:T(8,128)} fusion(bf16[2,1,4096,128]{3,2,1,0:T(8,128)(2,1)} %param.20), kind=kLoop, calls=%fused_computation.12 | loop fusion | flops 1048576 | bytes 6291456 | tf_op jit(solution)/shard_map/convert_element_type | solution.py:105
  21.3 19.8 %fusion.7 = (bf16[2,4096,64]{2,1,0:T(8,128)(2,1)}, bf16[2,4096,64]{2,1,0:T(8,128)(2,1)}) fusion(f32[2,1,4096,128]{3,2,0,1:T(8,128)} %bitcast_convert_fusion, f32[64]{0:T(128)S(1)} %multiply_exponential_fusion, f32[2,4096]{1,0:T(2,128)S(1)} %get-tuple-element.43, f32[2,4096]{1,0:T(2,128)S(1)} %get-tuple-element.44, f32[2,4096]{1,0:T(2,128)S(1)} %get-tuple-element.42, ...), kind=kLoop, calls=%fused_computation.13 | loop fusion | flops 5767168 | bytes 6390144 | tf_op jit(solution)/shard_map/concatenate | solution.py:38
  42.1 3.6 %select_reduce_fusion = (f32[2,8]{1,0:T(2,128)S(1)}, f32[2,8,4096]{2,1,0:T(8,128)S(1)}) fusion(pred[2,4096]{1,0:T(4,128)(4,1)S(1)} %get-tuple-element.53, bf16[2,4096,64]{2,1,0:T(8,128)(2,1)} %get-tuple-element.39, bf16[2,4096,64]{2,1,0:T(8,128)(2,1)} %get-tuple-element.38, bf16[2,8,64]{2,1,0:T(8,128)(2,1)S(1)} %bitcast.54, bf16[2,8,64]{2,1,0:T(8,128)(2,1)S(1)} %bitcast.53), kind=kOutput, calls=%fused_computation.22 | convolution fusion | flops 21176304 | bytes 2371648 | tf_op jit(solution)/shard_map/rgjd,rgsd->rgjs/dot_general | solution.py:117
  46.5 18.4 %all_to_all.20 = bf16[32,2,1024]{2,1,0:T(2,128)(2,1)S(1)} all-to-all(bf16[32,2,1024]{2,1,0:T(2,128)(2,1)S(1)} %broadcast_in_dim.178), channel_id=1, replica_groups=mesh['wide'=32,'narrow'=8] {'wide'}, dimensions={0} | all-to-all | bytes 262144 | tf_op jit(solution)/shard_map/all_to_all | solution.py:53
  65.2 2.8 %collective-permute-start = (f32[64,256]{1,0:T(8,128)S(1)}, f32[64,256]{1,0:T(8,128)S(1)}, u32[]{:S(2)}, u32[]{:S(2)}) collective-permute-start(f32[64,256]{1,0:T(8,128)S(1)} %fusion.60), channel_id=1, source_target_pairs={{0,1},{1,0},{2,3},{3,2},{4,5},{5,4},{6,7},{7,6},{8,9},{9,8},{10,11... | collective-permute-start | bytes 196616 | tf_op jit(solution)/shard_map/ppermute | solution.py:58
  67.9 0.9 collective-permute-done
  68.9 1.4 collective-permute-start.2
  70.2 1.5 %collective-permute-start.3 = (f32[64,256]{1,0:T(8,128)S(1)}, f32[64,256]{1,0:T(8,128)S(1)}, u32[]{:S(2)}, u32[]{:S(2)}) collective-permute-start(f32[64,256]{1,0:T(8,128)S(1)} %add.105), channel_id=1, source_target_pairs={{0,6},{1,7},{2,0},{3,1},{4,2},{5,3},{6,4},{7,5},{8,14},{9,15},{10,... | collective-permute-start | bytes 196616 | tf_op jit(solution)/shard_map/ppermute | solution.py:62
  71.8 1.6 %collective-permute-start.1 = (f32[64,256]{1,0:T(8,128)S(1)}, f32[64,256]{1,0:T(8,128)S(1)}, u32[]{:S(2)}, u32[]{:S(2)}) collective-permute-start(f32[64,256]{1,0:T(8,128)S(1)} %add.105), channel_id=1, source_target_pairs={{0,4},{1,5},{2,6},{3,7},{4,0},{5,1},{6,2},{7,3},{8,12},{9,13},{10,... | collective-permute-start | bytes 196616 | tf_op jit(solution)/shard_map/ppermute | solution.py:62
  74.0 2.4 %collective-permute-done.1 = f32[64,256]{1,0:T(8,128)S(1)} collective-permute-done((f32[64,256]{1,0:T(8,128)S(1)}, f32[64,256]{1,0:T(8,128)S(1)}, u32[]{:S(2)}, u32[]{:S(2)}) %collective-permute-start.1) | collective-permute-done | bytes 65568 | tf_op jit(solution)/shard_map/ppermute | solution.py:62
  77.3 3.3 %convolution_convert_fusion = bf16[64,7392]{1,0:T(8,128)(2,1)S(1)} fusion(bf16[256,7392]{0,1:T(8,128)(2,1)} %bitcast.51, bf16[64,256]{1,0:T(8,128)(2,1)S(1)} %get-tuple-element.33, f32[256]{0:T(256)S(1)} %convert_element_type.227), kind=kOutput, calls=%fused_computation | convolution fusion | flops 242743296 | bytes 4764672 | tf_op jit(solution)/shard_map/dot_general | solution.py:152
  81.0 1.3 reshape.706
  82.3 27.4 %all_to_all.21 = bf16[32,2,7394]{2,1,0:T(2,128)(2,1)S(1)} all-to-all(bf16[32,2,7394]{2,1,0:T(2,128)(2,1)} %reshape.706), channel_id=1, replica_groups=mesh['wide'=32,'narrow'=8] {'wide'}, dimensions={0} | all-to-all | bytes 1892864 | tf_op jit(solution)/shard_map/all_to_all | solution.py:159
  111.1 20.1 %all_to_all.22 = bf16[32,2,3696]{2,1,0:T(2,128)(2,1)S(1)} all-to-all(bf16[32,2,3696]{2,1,0:T(2,128)(2,1)S(1)} %broadcast_in_dim.179), channel_id=1, replica_groups=mesh['wide'=32,'narrow'=8] {'wide'}, dimensions={0} | all-to-all | bytes 946176 | tf_op jit(solution)/shard_map/all_to_all | solution.py:53
  131.5 2.0 %fusion.61 = f32[64,256]{1,0:T(8,128)S(1)} fusion(bf16[64,3696]{1,0:T(8,128)(2,1)S(1)} %reshape.707, bf16[3696,256]{1,0:T(8,128)(2,1)} %param.27), kind=kOutput, calls=%fused_computation.102 | convolution fusion | flops 121110528 | bytes 2430976 | tf_op jit(solution)/shard_map/dot_general | solution.py:169
  133.5 4.5 %collective-permute-start.4 = (f32[64,256]{1,0:T(8,128)S(1)}, f32[64,256]{1,0:T(8,128)S(1)}, u32[]{:S(2)}, u32[]{:S(2)}) collective-permute-start(f32[64,256]{1,0:T(8,128)S(1)} %fusion.61), channel_id=1, source_target_pairs={{0,1},{1,0},{2,3},{3,2},{4,5},{5,4},{6,7},{7,6},{8,9},{9,8},{10,11... | collective-permute-start | bytes 196616 | tf_op jit(solution)/shard_map/ppermute | solution.py:58
  138.0 0.9 collective-permute-done.4
  139.5 2.2 %collective-permute-start.7 = (f32[64,256]{1,0:T(8,128)S(1)}, f32[64,256]{1,0:T(8,128)S(1)}, u32[]{:S(2)}, u32[]{:S(2)}) collective-permute-start(f32[64,256]{1,0:T(8,128)S(1)} %add.113), channel_id=1, source_target_pairs={{0,6},{1,7},{2,0},{3,1},{4,2},{5,3},{6,4},{7,5},{8,14},{9,15},{10,... | collective-permute-start | bytes 196616 | tf_op jit(solution)/shard_map/ppermute | solution.py:62
  142.0 1.3 collective-permute-done.6
  143.3 3.0 %collective-permute-done.5 = f32[64,256]{1,0:T(8,128)S(1)} collective-permute-done((f32[64,256]{1,0:T(8,128)S(1)}, f32[64,256]{1,0:T(8,128)S(1)}, u32[]{:S(2)}, u32[]{:S(2)}) %collective-permute-start.5) | collective-permute-done | bytes 65568 | tf_op jit(solution)/shard_map/ppermute | solution.py:62
  (74 shorter events, 9.5 us)
Async XLA Ops:
  0.0 46.0 %copy-start = (bf16[2,1,4096,128]{3,2,1,0:T(8,128)(2,1)S(1)}, bf16[2,1,4096,128]{3,2,1,0:T(8,128)(2,1)}, u32[]{:S(2)}) copy-start(bf16[2,1,4096,128]{3,2,1,0:T(8,128)(2,1)} %param.21) | copy-start | bytes 6291460
  0.0 16.8 %copy-start.5 = (s32[2]{0:T(128)S(1)}, s32[2]{0:T(128)}, u32[]{:S(2)}) copy-start(s32[2]{0:T(128)} %param.23) | copy-start | bytes 28
  3.9 16.9 %copy-start.3 = (s32[2,3,4096]{2,0,1:T(2,128)S(1)}, s32[2,3,4096]{2,0,1:T(2,128)}, u32[]{:S(2)}) copy-start(s32[2,3,4096]{2,0,1:T(2,128)} %param.22) | copy-start | bytes 294916
  4.9 36.4 %all-to-all-start = ((f32[32,2,1281]{2,1,0:T(2,128)}), f32[32,2,1281]{2,1,0:T(2,128)S(1)}, u32[]{:S(2)}, u32[]{:S(2)}) async-start(f32[32,2,1281]{2,1,0:T(2,128)} %copy.43), calls=%async_computation | async-start | bytes 720896 | tf_op jit(solution)/shard_map/all_to_all | solution.py:47
  21.3 20.1 %copy-start.4 = (bf16[1,10,128]{2,1,0:T(8,128)(2,1)S(1)}, bf16[1,10,128]{2,1,0:T(8,128)(2,1)}, u32[]{:S(2)}) copy-start(bf16[1,10,128]{2,1,0:T(8,128)(2,1)} %param.19) | copy-start | bytes 7684
  42.1 22.8 %copy-start.1 = (bf16[1024,256]{1,0:T(8,128)(2,1)S(1)}, bf16[1024,256]{1,0:T(8,128)(2,1)}, u32[]{:S(2)}) copy-start(bf16[1024,256]{1,0:T(8,128)(2,1)} %param.24) | copy-start | bytes 1572868
  42.1 31.2 %copy-start.6 = (bf16[256]{0:T(256)(128)(2,1)S(1)}, bf16[256]{0:T(256)(128)(2,1)}, u32[]{:S(2)}) copy-start(bf16[256]{0:T(256)(128)(2,1)} %param.25) | copy-start | bytes 1540
  42.1 34.3 %copy-start.2 = (bf16[64,256]{1,0:T(8,128)(2,1)S(1)}, bf16[64,256]{1,0:T(8,128)(2,1)}, u32[]{:S(2)}) copy-start(bf16[64,256]{1,0:T(8,128)(2,1)} %param.16) | copy-start | bytes 98308
  65.2 3.7 %collective-permute-start = (f32[64,256]{1,0:T(8,128)S(1)}, f32[64,256]{1,0:T(8,128)S(1)}, u32[]{:S(2)}, u32[]{:S(2)}) collective-permute-start(f32[64,256]{1,0:T(8,128)S(1)} %fusion.60), channel_id=1, source_target_pairs={{0,1},{1,0},{2,3},{3,2},{4,5},{5,4},{6,7},{7,6},{8,9},{9,8},{10,11... | collective-permute-start | bytes 196616 | tf_op jit(solution)/shard_map/ppermute | solution.py:58
  68.9 5.1 %collective-permute-start.2 = (f32[64,256]{1,0:T(8,128)S(1)}, f32[64,256]{1,0:T(8,128)S(1)}, u32[]{:S(2)}, u32[]{:S(2)}) collective-permute-start(f32[64,256]{1,0:T(8,128)S(1)} %add.105), channel_id=1, source_target_pairs={{0,2},{1,3},{2,4},{3,5},{4,6},{5,7},{6,0},{7,1},{8,10},{9,11},{10,... | collective-permute-start | bytes 196616 | tf_op jit(solution)/shard_map/ppermute | solution.py:62
  70.2 3.7 %collective-permute-start.3 = (f32[64,256]{1,0:T(8,128)S(1)}, f32[64,256]{1,0:T(8,128)S(1)}, u32[]{:S(2)}, u32[]{:S(2)}) collective-permute-start(f32[64,256]{1,0:T(8,128)S(1)} %add.105), channel_id=1, source_target_pairs={{0,6},{1,7},{2,0},{3,1},{4,2},{5,3},{6,4},{7,5},{8,14},{9,15},{10,... | collective-permute-start | bytes 196616 | tf_op jit(solution)/shard_map/ppermute | solution.py:62
  71.8 4.6 %collective-permute-start.1 = (f32[64,256]{1,0:T(8,128)S(1)}, f32[64,256]{1,0:T(8,128)S(1)}, u32[]{:S(2)}, u32[]{:S(2)}) collective-permute-start(f32[64,256]{1,0:T(8,128)S(1)} %add.105), channel_id=1, source_target_pairs={{0,4},{1,5},{2,6},{3,7},{4,0},{5,1},{6,2},{7,3},{8,12},{9,13},{10,... | collective-permute-start | bytes 196616 | tf_op jit(solution)/shard_map/ppermute | solution.py:62
  133.5 5.4 %collective-permute-start.4 = (f32[64,256]{1,0:T(8,128)S(1)}, f32[64,256]{1,0:T(8,128)S(1)}, u32[]{:S(2)}, u32[]{:S(2)}) collective-permute-start(f32[64,256]{1,0:T(8,128)S(1)} %fusion.61), channel_id=1, source_target_pairs={{0,1},{1,0},{2,3},{3,2},{4,5},{5,4},{6,7},{7,6},{8,9},{9,8},{10,11... | collective-permute-start | bytes 196616 | tf_op jit(solution)/shard_map/ppermute | solution.py:58
  138.9 4.4 %collective-permute-start.6 = (f32[64,256]{1,0:T(8,128)S(1)}, f32[64,256]{1,0:T(8,128)S(1)}, u32[]{:S(2)}, u32[]{:S(2)}) collective-permute-start(f32[64,256]{1,0:T(8,128)S(1)} %add.113), channel_id=1, source_target_pairs={{0,2},{1,3},{2,4},{3,5},{4,6},{5,7},{6,0},{7,1},{8,10},{9,11},{10,... | collective-permute-start | bytes 196616 | tf_op jit(solution)/shard_map/ppermute | solution.py:62
  139.5 3.8 %collective-permute-start.7 = (f32[64,256]{1,0:T(8,128)S(1)}, f32[64,256]{1,0:T(8,128)S(1)}, u32[]{:S(2)}, u32[]{:S(2)}) collective-permute-start(f32[64,256]{1,0:T(8,128)S(1)} %add.113), channel_id=1, source_target_pairs={{0,6},{1,7},{2,0},{3,1},{4,2},{5,3},{6,4},{7,5},{8,14},{9,15},{10,... | collective-permute-start | bytes 196616 | tf_op jit(solution)/shard_map/ppermute | solution.py:62
  141.7 4.6 %collective-permute-start.5 = (f32[64,256]{1,0:T(8,128)S(1)}, f32[64,256]{1,0:T(8,128)S(1)}, u32[]{:S(2)}, u32[]{:S(2)}) collective-permute-start(f32[64,256]{1,0:T(8,128)S(1)} %add.113), channel_id=1, source_target_pairs={{0,4},{1,5},{2,6},{3,7},{4,0},{5,1},{6,2},{7,3},{8,12},{9,13},{10,... | collective-permute-start | bytes 196616 | tf_op jit(solution)/shard_map/ppermute | solution.py:62

commit v8 on v7

--- a/solution.py
+++ b/solution.py
@@ -102,9 +102,14 @@
     projected = inv_rms[:, None] * summed[:, :width] + qkv_bias.reshape(width).astype(jnp.float32)
     projected = projected.reshape(owned, kv_local, slot_count, DH)
     cosine, sine_table = mrope_tables(positions)
-    keys_rot = rotate(cache_keys.astype(jnp.float32), cosine[:, None], sine_table[:, None]).astype(
-        jnp.bfloat16
-    )
+    half_width = DH // 2
+    keys_lead = cache_keys[..., :half_width].astype(jnp.float32)
+    keys_trail = cache_keys[..., half_width:].astype(jnp.float32)
+    cos_keys, sin_keys = cosine[:, None], sine_table[:, None]
+    keys_rot = jnp.concatenate(
+        [keys_lead * cos_keys - keys_trail * sin_keys, keys_trail * cos_keys + keys_lead * sin_keys],
+        axis=-1,
+    ).astype(jnp.bfloat16)
     at_new_slot = jnp.arange(CACHE)[None, None, :] == lengths[:, None, None]
     new_position = jnp.sum(jnp.where(at_new_slot, positions, 0), axis=2, keepdims=True)
     cos_new, sin_new = mrope_tables(new_position)

time: 147 us -> 146 us (level)
  other arithmetic: 30 us -> 26.7 us
  waiting for transfers between devices: 8.53 us -> 10 us
    concatenate x0 -> x1, other arithmetic: none -> 20.2 us  [local(): jnp.concatenate([keys_lead * cos_keys - keys_trail * sin_keys, keys_trail...]
    concatenate x2 -> x1, other arithmetic: 19.8 us -> 0.07 us  [rotate(): jnp.concatenate([leading * cosine - trailing * sine_table, trailing * cos...]
    convert_element_type x1 -> x0, other arithmetic: 3.79 us -> none  [local(): cache_keys.astype(jnp.float32)]
    ppermute x6, waiting for transfers between devices: 6.72 us -> 8.22 us  [shifted(): lax.ppermute(x, axis, [(i, (i // 2 + k) % groups * 2 + i % 2) for i in ra...]
  transfers between devices with their start and end apart: 9 -> 9, of which waited for: 5 -> 6; matrix products, arithmetic and copies ran while one was open for 17% -> 15% of each run, Pallas kernels for 0% -> 0%
where the time goes in v8:
time: 146 us; the launch traced here: 145 us
  blocking collectives  66.2 us (45%)
  other arithmetic  26.7 us (18%)
  starting transfers between devices  26.4 us (18%)
  waiting for transfers between devices  10 us (7%)
  matrix products  9.86 us (7%)
  local copies, waits for them, and re-layouts  5.71 us (4%)
    all_to_all x2, blocking collectives, gather_rows(): lax.all_to_all(copies, axis, 0, 0, tiled=False)  38.4 us
    all_to_all x1, blocking collectives, local(): lax.all_to_all(sent2.reshape(n_wide, sent2.shape[0] // n_wide, sent2.shap...  27.7 us
    concatenate x1, other arithmetic, local(): jnp.concatenate([keys_lead * cos_keys - keys_trail * sin_keys, keys_trail...  20.2 us
    all_to_all x1, starting transfers between devices, reduce_rows(): return jnp.sum(lax.all_to_all(blocks, axis, 0, 0, tiled=False), axis=0)  11.9 us
    ppermute x6, waiting for transfers between devices, shifted(): lax.ppermute(x, axis, [(i, (i // 2 + k) % groups * 2 + i % 2) for i in ra...  8.22 us
    ppermute x6, starting transfers between devices, shifted(): lax.ppermute(x, axis, [(i, (i // 2 + k) % groups * 2 + i % 2) for i in ra...  7.65 us
    ppermute x2, starting transfers between devices, sum_all(): x = x + lax.ppermute(x, axis, [(i, i ^ 1) for i in range(n)])  6.93 us
    dot_general x1, matrix products, local(): jnp.einsum('rgjd,rgsd->rgjs', query, keys_rot, preferred_element_type=jnp...  3.56 us
  transfers between devices with their start and end apart: 9, of which 6 were waited for; matrix products, arithmetic and copies ran while one was open for 15% of the time, Pallas kernels for 0%

profile of v8, /device:TPU:1, one launch (start us, length us, event | category | flops | bytes accessed | tf_op | source)
XLA Modules:
  0.0 145.1 jit_solution(7256249583132205176)
XLA Ops:
  0.0 0.8 convert_element_type.211
  0.8 0.9 fusion.31
  2.1 1.4 copy.42
  3.9 1.0 copy.46
  4.9 11.9 %all-to-all-start = ((f32[32,2,1281]{2,1,0:T(2,128)}), f32[32,2,1281]{2,1,0:T(2,128)S(1)}, u32[]{:S(2)}, u32[]{:S(2)}) async-start(f32[32,2,1281]{2,1,0:T(2,128)} %copy.46), calls=%async_computation | async-start | bytes 720896 | tf_op jit(solution)/shard_map/all_to_all | solution.py:47
  17.5 20.2 %fusion.12 = (bf16[2,4096,64]{2,1,0:T(8,128)(2,1)}, bf16[2,4096,64]{2,1,0:T(8,128)(2,1)}) fusion(f32[64]{0:T(128)S(1)} %multiply_exponential_fusion, f32[2,4096]{1,0:T(2,128)S(1)} %get-tuple-element.43, f32[2,4096]{1,0:T(2,128)S(1)} %get-tuple-element.44, f32[2,4096]{1,0:T(2,128)S(1)} %get-tuple-element.42, pred[64]{0:T(512)(128)(4,1)S(1)} %get-tuple-element.57, ...), kind=kLoop, calls=%fused_computation.19 | loop fusion | flops 6815744 | bytes 4292992 | tf_op jit(solution)/shard_map/concatenate | solution.py:109
  38.7 3.6 %select_reduce_fusion = (f32[2,8]{1,0:T(2,128)S(1)}, f32[2,8,4096]{2,1,0:T(8,128)S(1)}) fusion(pred[2,4096]{1,0:T(4,128)(4,1)S(1)} %get-tuple-element.53, bf16[2,4096,64]{2,1,0:T(8,128)(2,1)} %get-tuple-element.39, bf16[2,4096,64]{2,1,0:T(8,128)(2,1)} %get-tuple-element.38, bf16[2,8,64]{2,1,0:T(8,128)(2,1)S(1)} %bitcast.55, bf16[2,8,64]{2,1,0:T(8,128)(2,1)S(1)} %bitcast.54), kind=kOutput, calls=%fused_computation.27 | convolution fusion | flops 21176304 | bytes 2371648 | tf_op jit(solution)/shard_map/rgjd,rgsd->rgjs/dot_general | solution.py:122
  43.1 18.4 %all_to_all.20 = bf16[32,2,1024]{2,1,0:T(2,128)(2,1)S(1)} all-to-all(bf16[32,2,1024]{2,1,0:T(2,128)(2,1)S(1)} %broadcast_in_dim.178), channel_id=1, replica_groups=mesh['wide'=32,'narrow'=8] {'wide'}, dimensions={0} | all-to-all | bytes 262144 | tf_op jit(solution)/shard_map/all_to_all | solution.py:53
  61.7 2.8 %collective-permute-start = (f32[64,256]{1,0:T(8,128)S(1)}, f32[64,256]{1,0:T(8,128)S(1)}, u32[]{:S(2)}, u32[]{:S(2)}) collective-permute-start(f32[64,256]{1,0:T(8,128)S(1)} %fusion.64), channel_id=1, source_target_pairs={{0,1},{1,0},{2,3},{3,2},{4,5},{5,4},{6,7},{7,6},{8,9},{9,8},{10,11... | collective-permute-start | bytes 196616 | tf_op jit(solution)/shard_map/ppermute | solution.py:58
  64.5 0.9 collective-permute-done
  65.5 2.8 %collective-permute-start.3 = (f32[64,256]{1,0:T(8,128)S(1)}, f32[64,256]{1,0:T(8,128)S(1)}, u32[]{:S(2)}, u32[]{:S(2)}) collective-permute-start(f32[64,256]{1,0:T(8,128)S(1)} %add.105), channel_id=1, source_target_pairs={{0,6},{1,7},{2,0},{3,1},{4,2},{5,3},{6,4},{7,5},{8,14},{9,15},{10,... | collective-permute-start | bytes 196616 | tf_op jit(solution)/shard_map/ppermute | solution.py:62
  68.3 1.6 %collective-permute-start.1 = (f32[64,256]{1,0:T(8,128)S(1)}, f32[64,256]{1,0:T(8,128)S(1)}, u32[]{:S(2)}, u32[]{:S(2)}) collective-permute-start(f32[64,256]{1,0:T(8,128)S(1)} %add.105), channel_id=1, source_target_pairs={{0,4},{1,5},{2,6},{3,7},{4,0},{5,1},{6,2},{7,3},{8,12},{9,13},{10,... | collective-permute-start | bytes 196616 | tf_op jit(solution)/shard_map/ppermute | solution.py:62
  70.6 2.7 %collective-permute-done.2 = f32[64,256]{1,0:T(8,128)S(1)} collective-permute-done((f32[64,256]{1,0:T(8,128)S(1)}, f32[64,256]{1,0:T(8,128)S(1)}, u32[]{:S(2)}, u32[]{:S(2)}) %collective-permute-start.2) | collective-permute-done | bytes 65568 | tf_op jit(solution)/shard_map/ppermute | solution.py:62
  74.6 3.3 %convolution_convert_fusion = bf16[64,7392]{1,0:T(8,128)(2,1)S(1)} fusion(bf16[256,7392]{0,1:T(8,128)(2,1)} %bitcast.52, bf16[64,256]{1,0:T(8,128)(2,1)S(1)} %get-tuple-element.33, f32[256]{0:T(256)S(1)} %convert_element_type.231), kind=kOutput, calls=%fused_computation | convolution fusion | flops 242743296 | bytes 4764672 | tf_op jit(solution)/shard_map/dot_general | solution.py:157
  78.3 1.3 reshape.706
  79.6 27.7 %all_to_all.21 = bf16[32,2,7394]{2,1,0:T(2,128)(2,1)S(1)} all-to-all(bf16[32,2,7394]{2,1,0:T(2,128)(2,1)} %reshape.706), channel_id=1, replica_groups=mesh['wide'=32,'narrow'=8] {'wide'}, dimensions={0} | all-to-all | bytes 1892864 | tf_op jit(solution)/shard_map/all_to_all | solution.py:164
  107.4 0.8 convert_reduce_fusion
  108.8 20.1 %all_to_all.22 = bf16[32,2,3696]{2,1,0:T(2,128)(2,1)S(1)} all-to-all(bf16[32,2,3696]{2,1,0:T(2,128)(2,1)S(1)} %broadcast_in_dim.179), channel_id=1, replica_groups=mesh['wide'=32,'narrow'=8] {'wide'}, dimensions={0} | all-to-all | bytes 946176 | tf_op jit(solution)/shard_map/all_to_all | solution.py:53
  129.2 2.0 %fusion.65 = f32[64,256]{1,0:T(8,128)S(1)} fusion(bf16[64,3696]{1,0:T(8,128)(2,1)S(1)} %reshape.707, bf16[3696,256]{1,0:T(8,128)(2,1)} %param.27), kind=kOutput, calls=%fused_computation.107 | convolution fusion | flops 121110528 | bytes 2430976 | tf_op jit(solution)/shard_map/dot_general | solution.py:174
  131.2 4.1 %collective-permute-start.4 = (f32[64,256]{1,0:T(8,128)S(1)}, f32[64,256]{1,0:T(8,128)S(1)}, u32[]{:S(2)}, u32[]{:S(2)}) collective-permute-start(f32[64,256]{1,0:T(8,128)S(1)} %fusion.65), channel_id=1, source_target_pairs={{0,1},{1,0},{2,3},{3,2},{4,5},{5,4},{6,7},{7,6},{8,9},{9,8},{10,11... | collective-permute-start | bytes 196616 | tf_op jit(solution)/shard_map/ppermute | solution.py:58
  135.3 0.9 collective-permute-done.4
  136.3 1.9 %collective-permute-start.7 = (f32[64,256]{1,0:T(8,128)S(1)}, f32[64,256]{1,0:T(8,128)S(1)}, u32[]{:S(2)}, u32[]{:S(2)}) collective-permute-start(f32[64,256]{1,0:T(8,128)S(1)} %add.113), channel_id=1, source_target_pairs={{0,6},{1,7},{2,0},{3,1},{4,2},{5,3},{6,4},{7,5},{8,14},{9,15},{10,... | collective-permute-start | bytes 196616 | tf_op jit(solution)/shard_map/ppermute | solution.py:62
  138.2 1.3 collective-permute-start.5
  139.5 5.0 %collective-permute-done.6 = f32[64,256]{1,0:T(8,128)S(1)} collective-permute-done((f32[64,256]{1,0:T(8,128)S(1)}, f32[64,256]{1,0:T(8,128)S(1)}, u32[]{:S(2)}, u32[]{:S(2)}) %collective-permute-start.6) | collective-permute-done | bytes 65568 | tf_op jit(solution)/shard_map/ppermute | solution.py:62
  (73 shorter events, 7.5 us)
Async XLA Ops:
  0.0 42.6 %copy-start = (bf16[2,1,4096,128]{3,2,1,0:T(8,128)(2,1)S(1)}, bf16[2,1,4096,128]{3,2,1,0:T(8,128)(2,1)}, u32[]{:S(2)}) copy-start(bf16[2,1,4096,128]{3,2,1,0:T(8,128)(2,1)} %param.21) | copy-start | bytes 6291460
  2.1 14.7 %copy-start.5 = (s32[2]{0:T(128)S(1)}, s32[2]{0:T(128)}, u32[]{:S(2)}) copy-start(s32[2]{0:T(128)} %param.23) | copy-start | bytes 28
  2.1 14.8 %copy-start.3 = (s32[2,3,4096]{2,0,1:T(2,128)S(1)}, s32[2,3,4096]{2,0,1:T(2,128)}, u32[]{:S(2)}) copy-start(s32[2,3,4096]{2,0,1:T(2,128)} %param.22) | copy-start | bytes 294916
  4.9 33.1 %all-to-all-start = ((f32[32,2,1281]{2,1,0:T(2,128)}), f32[32,2,1281]{2,1,0:T(2,128)S(1)}, u32[]{:S(2)}, u32[]{:S(2)}) async-start(f32[32,2,1281]{2,1,0:T(2,128)} %copy.46), calls=%async_computation | async-start | bytes 720896 | tf_op jit(solution)/shard_map/all_to_all | solution.py:47
  17.4 20.5 %copy-start.4 = (bf16[1,10,128]{2,1,0:T(8,128)(2,1)S(1)}, bf16[1,10,128]{2,1,0:T(8,128)(2,1)}, u32[]{:S(2)}) copy-start(bf16[1,10,128]{2,1,0:T(8,128)(2,1)} %param.19) | copy-start | bytes 7684
  42.3 19.2 %copy-start.1 = (bf16[1024,256]{1,0:T(8,128)(2,1)S(1)}, bf16[1024,256]{1,0:T(8,128)(2,1)}, u32[]{:S(2)}) copy-start(bf16[1024,256]{1,0:T(8,128)(2,1)} %param.24) | copy-start | bytes 1572868
  42.3 27.6 %copy-start.6 = (bf16[256]{0:T(256)(128)(2,1)S(1)}, bf16[256]{0:T(256)(128)(2,1)}, u32[]{:S(2)}) copy-start(bf16[256]{0:T(256)(128)(2,1)} %param.25) | copy-start | bytes 1540
  42.3 31.4 %copy-start.2 = (bf16[64,256]{1,0:T(8,128)(2,1)S(1)}, bf16[64,256]{1,0:T(8,128)(2,1)}, u32[]{:S(2)}) copy-start(bf16[64,256]{1,0:T(8,128)(2,1)} %param.16) | copy-start | bytes 98308
  61.7 3.7 %collective-permute-start = (f32[64,256]{1,0:T(8,128)S(1)}, f32[64,256]{1,0:T(8,128)S(1)}, u32[]{:S(2)}, u32[]{:S(2)}) collective-permute-start(f32[64,256]{1,0:T(8,128)S(1)} %fusion.64), channel_id=1, source_target_pairs={{0,1},{1,0},{2,3},{3,2},{4,5},{5,4},{6,7},{7,6},{8,9},{9,8},{10,11... | collective-permute-start | bytes 196616 | tf_op jit(solution)/shard_map/ppermute | solution.py:58
  65.5 5.1 %collective-permute-start.3 = (f32[64,256]{1,0:T(8,128)S(1)}, f32[64,256]{1,0:T(8,128)S(1)}, u32[]{:S(2)}, u32[]{:S(2)}) collective-permute-start(f32[64,256]{1,0:T(8,128)S(1)} %add.105), channel_id=1, source_target_pairs={{0,6},{1,7},{2,0},{3,1},{4,2},{5,3},{6,4},{7,5},{8,14},{9,15},{10,... | collective-permute-start | bytes 196616 | tf_op jit(solution)/shard_map/ppermute | solution.py:62
  68.3 5.0 %collective-permute-start.2 = (f32[64,256]{1,0:T(8,128)S(1)}, f32[64,256]{1,0:T(8,128)S(1)}, u32[]{:S(2)}, u32[]{:S(2)}) collective-permute-start(f32[64,256]{1,0:T(8,128)S(1)} %add.105), channel_id=1, source_target_pairs={{0,2},{1,3},{2,4},{3,5},{4,6},{5,7},{6,0},{7,1},{8,10},{9,11},{10,... | collective-permute-start | bytes 196616 | tf_op jit(solution)/shard_map/ppermute | solution.py:62
  68.3 5.5 %collective-permute-start.1 = (f32[64,256]{1,0:T(8,128)S(1)}, f32[64,256]{1,0:T(8,128)S(1)}, u32[]{:S(2)}, u32[]{:S(2)}) collective-permute-start(f32[64,256]{1,0:T(8,128)S(1)} %add.105), channel_id=1, source_target_pairs={{0,4},{1,5},{2,6},{3,7},{4,0},{5,1},{6,2},{7,3},{8,12},{9,13},{10,... | collective-permute-start | bytes 196616 | tf_op jit(solution)/shard_map/ppermute | solution.py:62
  131.2 5.0 %collective-permute-start.4 = (f32[64,256]{1,0:T(8,128)S(1)}, f32[64,256]{1,0:T(8,128)S(1)}, u32[]{:S(2)}, u32[]{:S(2)}) collective-permute-start(f32[64,256]{1,0:T(8,128)S(1)} %fusion.65), channel_id=1, source_target_pairs={{0,1},{1,0},{2,3},{3,2},{4,5},{5,4},{6,7},{7,6},{8,9},{9,8},{10,11... | collective-permute-start | bytes 196616 | tf_op jit(solution)/shard_map/ppermute | solution.py:58
  136.3 3.3 %collective-permute-start.7 = (f32[64,256]{1,0:T(8,128)S(1)}, f32[64,256]{1,0:T(8,128)S(1)}, u32[]{:S(2)}, u32[]{:S(2)}) collective-permute-start(f32[64,256]{1,0:T(8,128)S(1)} %add.113), channel_id=1, source_target_pairs={{0,6},{1,7},{2,0},{3,1},{4,2},{5,3},{6,4},{7,5},{8,14},{9,15},{10,... | collective-permute-start | bytes 196616 | tf_op jit(solution)/shard_map/ppermute | solution.py:62
  138.2 6.3 %collective-permute-start.6 = (f32[64,256]{1,0:T(8,128)S(1)}, f32[64,256]{1,0:T(8,128)S(1)}, u32[]{:S(2)}, u32[]{:S(2)}) collective-permute-start(f32[64,256]{1,0:T(8,128)S(1)} %add.113), channel_id=1, source_target_pairs={{0,2},{1,3},{2,4},{3,5},{4,6},{5,7},{6,0},{7,1},{8,10},{9,11},{10,... | collective-permute-start | bytes 196616 | tf_op jit(solution)/shard_map/ppermute | solution.py:62
  138.2 6.3 %collective-permute-start.5 = (f32[64,256]{1,0:T(8,128)S(1)}, f32[64,256]{1,0:T(8,128)S(1)}, u32[]{:S(2)}, u32[]{:S(2)}) collective-permute-start(f32[64,256]{1,0:T(8,128)S(1)} %add.113), channel_id=1, source_target_pairs={{0,4},{1,5},{2,6},{3,7},{4,0},{5,1},{6,2},{7,3},{8,12},{9,13},{10,... | collective-permute-start | bytes 196616 | tf_op jit(solution)/shard_map/ppermute | solution.py:62

commit v9 on v8

--- a/solution.py
+++ b/solution.py
@@ -12,6 +12,21 @@
 
 norm_eps = 1e-06
 rope_base = 1000000.0
+
+
+def cos_sin(angle):
+    k = jnp.round(angle * 0.6366197723675814)
+    r = ((angle - k * 1.5703125) - k * 4.837512969970703125e-4) - k * 7.54978995489188216e-8
+    z = r * r
+    s = r + r * z * (-1.6666654611e-1 + z * (8.3321608736e-3 + z * -1.9515295891e-4))
+    c = 1.0 - 0.5 * z + z * z * (
+        4.166664568298827e-2 + z * (-1.388731625493765e-3 + z * 2.443315711809948e-5)
+    )
+    quadrant = k - 4.0 * jnp.floor(k * 0.25)
+    odd = (quadrant == 1.0) | (quadrant == 3.0)
+    cos_sign = jnp.where((quadrant == 1.0) | (quadrant == 2.0), -1.0, 1.0)
+    sin_sign = jnp.where(quadrant >= 2.0, -1.0, 1.0)
+    return cos_sign * jnp.where(odd, s, c), sin_sign * jnp.where(odd, c, s)
 
 
 def mrope_tables(position):
@@ -28,7 +43,7 @@
         jnp.where(component == 1, pos_float[..., 1, :, None], pos_float[..., 2, :, None]),
     )
     angles = chosen * inv_freq
-    return (jnp.cos(angles), jnp.sin(angles))
+    return cos_sin(angles)
 
 
 def rotate(values, cosine, sine_table):

time: 146 us -> 138 us (0.945)
  other arithmetic: 26.7 us -> 18.4 us
    concatenate x1, other arithmetic: 20.2 us -> 12 us  [local(): jnp.concatenate([keys_lead * cos_keys - keys_trail * sin_keys, keys_trail...]
  transfers between devices with their start and end apart: 9 -> 9, of which waited for: 6 -> 7; matrix products, arithmetic and copies ran while one was open for 15% -> 10% of each run, Pallas kernels for 0% -> 0%
where the time goes in v9:
time: 138 us; the launch traced here: 137 us
  blocking collectives  65.6 us (48%)
  starting transfers between devices  26.4 us (19%)
  other arithmetic  18.4 us (13%)
  waiting for transfers between devices  10.6 us (8%)
  matrix products  9.92 us (7%)
  local copies, waits for them, and re-layouts  5.63 us (4%)
    all_to_all x2, blocking collectives, gather_rows(): lax.all_to_all(copies, axis, 0, 0, tiled=False)  37.9 us
    all_to_all x1, blocking collectives, local(): lax.all_to_all(sent2.reshape(n_wide, sent2.shape[0] // n_wide, sent2.shap...  27.7 us
    concatenate x1, other arithmetic, local(): jnp.concatenate([keys_lead * cos_keys - keys_trail * sin_keys, keys_trail...  12 us
    all_to_all x1, starting transfers between devices, reduce_rows(): return jnp.sum(lax.all_to_all(blocks, axis, 0, 0, tiled=False), axis=0)  11.9 us
    ppermute x6, waiting for transfers between devices, shifted(): lax.ppermute(x, axis, [(i, (i // 2 + k) % groups * 2 + i % 2) for i in ra...  8.22 us
    ppermute x6, starting transfers between devices, shifted(): lax.ppermute(x, axis, [(i, (i // 2 + k) % groups * 2 + i % 2) for i in ra...  7.65 us
    ppermute x2, starting transfers between devices, sum_all(): x = x + lax.ppermute(x, axis, [(i, i ^ 1) for i in range(n)])  6.93 us
    dot_general x1, matrix products, local(): jnp.einsum('rgjd,rgsd->rgjs', query, keys_rot, preferred_element_type=jnp...  3.61 us
  transfers between devices with their start and end apart: 9, of which 7 were waited for; matrix products, arithmetic and copies ran while one was open for 10% of the time, Pallas kernels for 0%

profile of v9, /device:TPU:1, one launch (start us, length us, event | category | flops | bytes accessed | tf_op | source)
XLA Modules:
  0.0 136.9 jit_solution(1994645391521653652)
XLA Ops:
  0.0 0.8 convert_element_type.211
  0.8 0.9 fusion.39
  2.1 1.3 copy.42
  3.9 1.0 copy.46
  4.9 11.9 %all-to-all-start = ((f32[32,2,1281]{2,1,0:T(2,128)}), f32[32,2,1281]{2,1,0:T(2,128)S(1)}, u32[]{:S(2)}, u32[]{:S(2)}) async-start(f32[32,2,1281]{2,1,0:T(2,128)} %copy.46), calls=%async_computation | async-start | bytes 720896 | tf_op jit(solution)/shard_map/all_to_all | solution.py:62
  17.4 12.0 %fusion.15 = (bf16[2,4096,64]{2,1,0:T(8,128)(2,1)}, bf16[2,4096,64]{2,1,0:T(8,128)(2,1)}) fusion(bf16[2,1,4096,128]{3,2,0,1:T(8,128)(2,1)} %bitcast.51, f32[64]{0:T(128)S(1)} %multiply_exponential_fusion, f32[2,4096]{1,0:T(2,128)S(1)} %get-tuple-element.44, f32[2,4096]{1,0:T(2,128)S(1)} %get-tuple-element.45, pred[64]{0:T(512)(128)(4,1)S(1)} %get-tuple-element.56, ...), kind=kLoop, calls=%fused_computation.35 | loop fusion | flops 28311552 | bytes 4292992 | tf_op jit(solution)/shard_map/concatenate | solution.py:124
  31.0 3.6 %select_reduce_fusion = (f32[2,8]{1,0:T(2,128)S(1)}, f32[2,8,4096]{2,1,0:T(8,128)S(1)}) fusion(pred[2,4096]{1,0:T(4,128)(4,1)S(1)} %get-tuple-element.52, bf16[2,4096,64]{2,1,0:T(8,128)(2,1)} %get-tuple-element.40, bf16[2,4096,64]{2,1,0:T(8,128)(2,1)} %get-tuple-element.39, bf16[2,8,64]{2,1,0:T(8,128)(2,1)S(1)} %bitcast.55, bf16[2,8,64]{2,1,0:T(8,128)(2,1)S(1)} %bitcast.54), kind=kOutput, calls=%fused_computation.48 | convolution fusion | flops 21176304 | bytes 2371648 | tf_op jit(solution)/shard_map/rgjd,rgsd->rgjs/dot_general | solution.py:137
  35.4 17.8 %all_to_all.20 = bf16[32,2,1024]{2,1,0:T(2,128)(2,1)S(1)} all-to-all(bf16[32,2,1024]{2,1,0:T(2,128)(2,1)S(1)} %broadcast_in_dim.199), channel_id=1, replica_groups=mesh['wide'=32,'narrow'=8] {'wide'}, dimensions={0} | all-to-all | bytes 262144 | tf_op jit(solution)/shard_map/all_to_all | solution.py:68
  53.5 2.8 %collective-permute-start = (f32[64,256]{1,0:T(8,128)S(1)}, f32[64,256]{1,0:T(8,128)S(1)}, u32[]{:S(2)}, u32[]{:S(2)}) collective-permute-start(f32[64,256]{1,0:T(8,128)S(1)} %fusion.76), channel_id=1, source_target_pairs={{0,1},{1,0},{2,3},{3,2},{4,5},{5,4},{6,7},{7,6},{8,9},{9,8},{10,11... | collective-permute-start | bytes 196616 | tf_op jit(solution)/shard_map/ppermute | solution.py:73
  56.3 0.9 collective-permute-done
  57.2 2.8 %collective-permute-start.3 = (f32[64,256]{1,0:T(8,128)S(1)}, f32[64,256]{1,0:T(8,128)S(1)}, u32[]{:S(2)}, u32[]{:S(2)}) collective-permute-start(f32[64,256]{1,0:T(8,128)S(1)} %add.395), channel_id=1, source_target_pairs={{0,6},{1,7},{2,0},{3,1},{4,2},{5,3},{6,4},{7,5},{8,14},{9,15},{10,... | collective-permute-start | bytes 196616 | tf_op jit(solution)/shard_map/ppermute | solution.py:77
  60.0 1.6 %collective-permute-start.1 = (f32[64,256]{1,0:T(8,128)S(1)}, f32[64,256]{1,0:T(8,128)S(1)}, u32[]{:S(2)}, u32[]{:S(2)}) collective-permute-start(f32[64,256]{1,0:T(8,128)S(1)} %add.395), channel_id=1, source_target_pairs={{0,4},{1,5},{2,6},{3,7},{4,0},{5,1},{6,2},{7,3},{8,12},{9,13},{10,... | collective-permute-start | bytes 196616 | tf_op jit(solution)/shard_map/ppermute | solution.py:77
  62.3 2.7 %collective-permute-done.2 = f32[64,256]{1,0:T(8,128)S(1)} collective-permute-done((f32[64,256]{1,0:T(8,128)S(1)}, f32[64,256]{1,0:T(8,128)S(1)}, u32[]{:S(2)}, u32[]{:S(2)}) %collective-permute-start.2) | collective-permute-done | bytes 65568 | tf_op jit(solution)/shard_map/ppermute | solution.py:77
  66.3 3.3 %convolution_convert_fusion = bf16[64,7392]{1,0:T(8,128)(2,1)S(1)} fusion(bf16[256,7392]{0,1:T(8,128)(2,1)} %bitcast.52, bf16[64,256]{1,0:T(8,128)(2,1)S(1)} %get-tuple-element.33, f32[256]{0:T(256)S(1)} %convert_element_type.231), kind=kOutput, calls=%fused_computation | convolution fusion | flops 242743296 | bytes 4764672 | tf_op jit(solution)/shard_map/dot_general | solution.py:172
  70.1 1.3 reshape.1018
  71.4 27.7 %all_to_all.21 = bf16[32,2,7394]{2,1,0:T(2,128)(2,1)S(1)} all-to-all(bf16[32,2,7394]{2,1,0:T(2,128)(2,1)} %reshape.1018), channel_id=1, replica_groups=mesh['wide'=32,'narrow'=8] {'wide'}, dimensions={0} | all-to-all | bytes 1892864 | tf_op jit(solution)/shard_map/all_to_all | solution.py:179
  99.1 0.8 convert_reduce_fusion
  100.5 20.1 %all_to_all.22 = bf16[32,2,3696]{2,1,0:T(2,128)(2,1)S(1)} all-to-all(bf16[32,2,3696]{2,1,0:T(2,128)(2,1)S(1)} %broadcast_in_dim.200), channel_id=1, replica_groups=mesh['wide'=32,'narrow'=8] {'wide'}, dimensions={0} | all-to-all | bytes 946176 | tf_op jit(solution)/shard_map/all_to_all | solution.py:68
  120.9 2.0 %fusion.77 = f32[64,256]{1,0:T(8,128)S(1)} fusion(bf16[64,3696]{1,0:T(8,128)(2,1)S(1)} %reshape.1019, bf16[3696,256]{1,0:T(8,128)(2,1)} %param.27), kind=kOutput, calls=%fused_computation.148 | convolution fusion | flops 121110528 | bytes 2430976 | tf_op jit(solution)/shard_map/dot_general | solution.py:189
  122.9 4.1 %collective-permute-start.4 = (f32[64,256]{1,0:T(8,128)S(1)}, f32[64,256]{1,0:T(8,128)S(1)}, u32[]{:S(2)}, u32[]{:S(2)}) collective-permute-start(f32[64,256]{1,0:T(8,128)S(1)} %fusion.77), channel_id=1, source_target_pairs={{0,1},{1,0},{2,3},{3,2},{4,5},{5,4},{6,7},{7,6},{8,9},{9,8},{10,11... | collective-permute-start | bytes 196616 | tf_op jit(solution)/shard_map/ppermute | solution.py:73
  127.1 0.9 collective-permute-done.4
  128.0 1.9 %collective-permute-start.7 = (f32[64,256]{1,0:T(8,128)S(1)}, f32[64,256]{1,0:T(8,128)S(1)}, u32[]{:S(2)}, u32[]{:S(2)}) collective-permute-start(f32[64,256]{1,0:T(8,128)S(1)} %add.403), channel_id=1, source_target_pairs={{0,6},{1,7},{2,0},{3,1},{4,2},{5,3},{6,4},{7,5},{8,14},{9,15},{10,... | collective-permute-start | bytes 196616 | tf_op jit(solution)/shard_map/ppermute | solution.py:77
  129.9 1.3 collective-permute-start.5
  131.2 5.0 %collective-permute-done.6 = f32[64,256]{1,0:T(8,128)S(1)} collective-permute-done((f32[64,256]{1,0:T(8,128)S(1)}, f32[64,256]{1,0:T(8,128)S(1)}, u32[]{:S(2)}, u32[]{:S(2)}) %collective-permute-start.6) | collective-permute-done | bytes 65568 | tf_op jit(solution)/shard_map/ppermute | solution.py:77
  (73 shorter events, 8.0 us)
Async XLA Ops:
  0.0 34.8 %copy-start = (bf16[2,1,4096,128]{3,2,1,0:T(8,128)(2,1)S(1)}, bf16[2,1,4096,128]{3,2,1,0:T(8,128)(2,1)}, u32[]{:S(2)}) copy-start(bf16[2,1,4096,128]{3,2,1,0:T(8,128)(2,1)} %param.21) | copy-start | bytes 6291460
  0.0 16.8 %copy-start.5 = (s32[2]{0:T(128)S(1)}, s32[2]{0:T(128)}, u32[]{:S(2)}) copy-start(s32[2]{0:T(128)} %param.23) | copy-start | bytes 28
  0.0 16.9 %copy-start.3 = (s32[2,3,4096]{2,0,1:T(2,128)S(1)}, s32[2,3,4096]{2,0,1:T(2,128)}, u32[]{:S(2)}) copy-start(s32[2,3,4096]{2,0,1:T(2,128)} %param.22) | copy-start | bytes 294916
  4.9 25.2 %all-to-all-start = ((f32[32,2,1281]{2,1,0:T(2,128)}), f32[32,2,1281]{2,1,0:T(2,128)S(1)}, u32[]{:S(2)}, u32[]{:S(2)}) async-start(f32[32,2,1281]{2,1,0:T(2,128)} %copy.46), calls=%async_computation | async-start | bytes 720896 | tf_op jit(solution)/shard_map/all_to_all | solution.py:62
  17.4 12.1 %copy-start.4 = (bf16[1,10,128]{2,1,0:T(8,128)(2,1)S(1)}, bf16[1,10,128]{2,1,0:T(8,128)(2,1)}, u32[]{:S(2)}) copy-start(bf16[1,10,128]{2,1,0:T(8,128)(2,1)} %param.19) | copy-start | bytes 7684
  30.9 22.3 %copy-start.1 = (bf16[1024,256]{1,0:T(8,128)(2,1)S(1)}, bf16[1024,256]{1,0:T(8,128)(2,1)}, u32[]{:S(2)}) copy-start(bf16[1024,256]{1,0:T(8,128)(2,1)} %param.24) | copy-start | bytes 1572868
  31.0 30.7 %copy-start.6 = (bf16[256]{0:T(256)(128)(2,1)S(1)}, bf16[256]{0:T(256)(128)(2,1)}, u32[]{:S(2)}) copy-start(bf16[256]{0:T(256)(128)(2,1)} %param.25) | copy-start | bytes 1540
  31.0 34.5 %copy-start.2 = (bf16[64,256]{1,0:T(8,128)(2,1)S(1)}, bf16[64,256]{1,0:T(8,128)(2,1)}, u32[]{:S(2)}) copy-start(bf16[64,256]{1,0:T(8,128)(2,1)} %param.16) | copy-start | bytes 98308
  53.5 3.7 %collective-permute-start = (f32[64,256]{1,0:T(8,128)S(1)}, f32[64,256]{1,0:T(8,128)S(1)}, u32[]{:S(2)}, u32[]{:S(2)}) collective-permute-start(f32[64,256]{1,0:T(8,128)S(1)} %fusion.76), channel_id=1, source_target_pairs={{0,1},{1,0},{2,3},{3,2},{4,5},{5,4},{6,7},{7,6},{8,9},{9,8},{10,11... | collective-permute-start | bytes 196616 | tf_op jit(solution)/shard_map/ppermute | solution.py:73
  57.2 5.1 %collective-permute-start.3 = (f32[64,256]{1,0:T(8,128)S(1)}, f32[64,256]{1,0:T(8,128)S(1)}, u32[]{:S(2)}, u32[]{:S(2)}) collective-permute-start(f32[64,256]{1,0:T(8,128)S(1)} %add.395), channel_id=1, source_target_pairs={{0,6},{1,7},{2,0},{3,1},{4,2},{5,3},{6,4},{7,5},{8,14},{9,15},{10,... | collective-permute-start | bytes 196616 | tf_op jit(solution)/shard_map/ppermute | solution.py:77
  60.0 5.0 %collective-permute-start.2 = (f32[64,256]{1,0:T(8,128)S(1)}, f32[64,256]{1,0:T(8,128)S(1)}, u32[]{:S(2)}, u32[]{:S(2)}) collective-permute-start(f32[64,256]{1,0:T(8,128)S(1)} %add.395), channel_id=1, source_target_pairs={{0,2},{1,3},{2,4},{3,5},{4,6},{5,7},{6,0},{7,1},{8,10},{9,11},{10,... | collective-permute-start | bytes 196616 | tf_op jit(solution)/shard_map/ppermute | solution.py:77
  60.0 5.5 %collective-permute-start.1 = (f32[64,256]{1,0:T(8,128)S(1)}, f32[64,256]{1,0:T(8,128)S(1)}, u32[]{:S(2)}, u32[]{:S(2)}) collective-permute-start(f32[64,256]{1,0:T(8,128)S(1)} %add.395), channel_id=1, source_target_pairs={{0,4},{1,5},{2,6},{3,7},{4,0},{5,1},{6,2},{7,3},{8,12},{9,13},{10,... | collective-permute-start | bytes 196616 | tf_op jit(solution)/shard_map/ppermute | solution.py:77
  122.9 5.0 %collective-permute-start.4 = (f32[64,256]{1,0:T(8,128)S(1)}, f32[64,256]{1,0:T(8,128)S(1)}, u32[]{:S(2)}, u32[]{:S(2)}) collective-permute-start(f32[64,256]{1,0:T(8,128)S(1)} %fusion.77), channel_id=1, source_target_pairs={{0,1},{1,0},{2,3},{3,2},{4,5},{5,4},{6,7},{7,6},{8,9},{9,8},{10,11... | collective-permute-start | bytes 196616 | tf_op jit(solution)/shard_map/ppermute | solution.py:73
  128.0 3.3 %collective-permute-start.7 = (f32[64,256]{1,0:T(8,128)S(1)}, f32[64,256]{1,0:T(8,128)S(1)}, u32[]{:S(2)}, u32[]{:S(2)}) collective-permute-start(f32[64,256]{1,0:T(8,128)S(1)} %add.403), channel_id=1, source_target_pairs={{0,6},{1,7},{2,0},{3,1},{4,2},{5,3},{6,4},{7,5},{8,14},{9,15},{10,... | collective-permute-start | bytes 196616 | tf_op jit(solution)/shard_map/ppermute | solution.py:77
  129.9 6.3 %collective-permute-start.6 = (f32[64,256]{1,0:T(8,128)S(1)}, f32[64,256]{1,0:T(8,128)S(1)}, u32[]{:S(2)}, u32[]{:S(2)}) collective-permute-start(f32[64,256]{1,0:T(8,128)S(1)} %add.403), channel_id=1, source_target_pairs={{0,2},{1,3},{2,4},{3,5},{4,6},{5,7},{6,0},{7,1},{8,10},{9,11},{10,... | collective-permute-start | bytes 196616 | tf_op jit(solution)/shard_map/ppermute | solution.py:77
  129.9 6.3 %collective-permute-start.5 = (f32[64,256]{1,0:T(8,128)S(1)}, f32[64,256]{1,0:T(8,128)S(1)}, u32[]{:S(2)}, u32[]{:S(2)}) collective-permute-start(f32[64,256]{1,0:T(8,128)S(1)} %add.403), channel_id=1, source_target_pairs={{0,4},{1,5},{2,6},{3,7},{4,0},{5,1},{6,2},{7,3},{8,12},{9,13},{10,... | collective-permute-start | bytes 196616 | tf_op jit(solution)/shard_map/ppermute | solution.py:77

commit v10 on v9

--- a/solution.py
+++ b/solution.py
@@ -111,7 +111,14 @@
     local_squares = jnp.sum(inputs * inputs, axis=1)
     scaled = (inputs * attn_gain.astype(jnp.float32)).astype(jnp.bfloat16)
     weight_flat = qkv_weight.reshape(local_rows, width)
-    partial = jnp.dot(scaled, weight_flat, preferred_element_type=jnp.float32)
+    weight_by_slot = qkv_weight.reshape(local_rows, slot_count * kv_local, DH).transpose(1, 0, 2)
+    partial = lax.dot_general(
+        jnp.broadcast_to(scaled[None], (slot_count * kv_local,) + scaled.shape),
+        weight_by_slot,
+        (((2,), (1,)), ((0,), (0,))),
+        preferred_element_type=jnp.float32,
+    )
+    partial = partial.transpose(1, 0, 2).reshape(scaled.shape[0], width)
     summed = reduce_rows(jnp.concatenate([partial, local_squares[:, None]], axis=1), "wide")
     inv_rms = 1.0 / jnp.sqrt(summed[:, width] / D + norm_eps)
     projected = inv_rms[:, None] * summed[:, :width] + qkv_bias.reshape(width).astype(jnp.float32)

time: 138 us -> 137 us (level)
  local copies, waits for them, and re-layouts: 5.63 us -> 3.41 us
where the time goes in v10:
time: 137 us
  blocking collectives  65.6 us (48%)
  starting transfers between devices  26.4 us (19%)
  other arithmetic  19.3 us (14%)
  matrix products  10.9 us (8%)
  waiting for transfers between devices  10.6 us (8%)
  local copies, waits for them, and re-layouts  3.41 us (2%)
    all_to_all x2, blocking collectives, gather_rows(): lax.all_to_all(copies, axis, 0, 0, tiled=False)  37.9 us
    all_to_all x1, blocking collectives, local(): lax.all_to_all(sent2.reshape(n_wide, sent2.shape[0] // n_wide, sent2.shap...  27.7 us
    concatenate x1, other arithmetic, local(): jnp.concatenate([keys_lead * cos_keys - keys_trail * sin_keys, keys_trail...  12 us
    all_to_all x1, starting transfers between devices, reduce_rows(): return jnp.sum(lax.all_to_all(blocks, axis, 0, 0, tiled=False), axis=0)  11.9 us
    ppermute x6, waiting for transfers between devices, shifted(): lax.ppermute(x, axis, [(i, (i // 2 + k) % groups * 2 + i % 2) for i in ra...  8.22 us
    ppermute x6, starting transfers between devices, shifted(): lax.ppermute(x, axis, [(i, (i // 2 + k) % groups * 2 + i % 2) for i in ra...  7.65 us
    ppermute x2, starting transfers between devices, sum_all(): x = x + lax.ppermute(x, axis, [(i, i ^ 1) for i in range(n)])  6.93 us
    dot_general x1, matrix products, local(): jnp.einsum('rgjd,rgsd->rgjs', query, keys_rot, preferred_element_type=jnp...  3.61 us
  transfers between devices with their start and end apart: 9, of which 7 were waited for; matrix products, arithmetic and copies ran while one was open for 10% of the time, Pallas kernels for 0%

profile of v10, /device:TPU:1, one launch (start us, length us, event | category | flops | bytes accessed | tf_op | source)
XLA Modules:
  0.0 136.5 jit_solution(11259197812899526553)
XLA Ops:
  0.0 0.8 convert_element_type.211
  0.8 0.9 fusion.41
  1.9 1.3 convolution_bitcast_fusion
  3.6 0.9 pad_maximum_fusion
  4.5 11.9 %all-to-all-start = ((f32[32,2,1281]{2,1,0:T(2,128)}), f32[32,2,1281]{2,1,0:T(2,128)S(1)}, u32[]{:S(2)}, u32[]{:S(2)}) async-start(f32[32,2,1281]{2,1,0:T(2,128)} %pad_maximum_fusion), calls=%async_computation | async-start | bytes 720896 | tf_op jit(solution)/shard_map/all_to_all | solution.py:62
  17.1 12.0 %fusion.15 = (bf16[2,4096,64]{2,1,0:T(8,128)(2,1)}, bf16[2,4096,64]{2,1,0:T(8,128)(2,1)}) fusion(bf16[2,1,4096,128]{3,2,0,1:T(8,128)(2,1)} %bitcast.54, f32[64]{0:T(128)S(1)} %multiply_exponential_fusion, f32[2,4096]{1,0:T(2,128)S(1)} %get-tuple-element.44, f32[2,4096]{1,0:T(2,128)S(1)} %get-tuple-element.45, pred[64]{0:T(512)(128)(4,1)S(1)} %get-tuple-element.56, ...), kind=kLoop, calls=%fused_computation.35 | loop fusion | flops 28311552 | bytes 4292992 | tf_op jit(solution)/shard_map/concatenate | solution.py:131
  30.6 3.6 %select_reduce_fusion = (f32[2,8]{1,0:T(2,128)S(1)}, f32[2,8,4096]{2,1,0:T(8,128)S(1)}) fusion(pred[2,4096]{1,0:T(4,128)(4,1)S(1)} %get-tuple-element.52, bf16[2,4096,64]{2,1,0:T(8,128)(2,1)} %get-tuple-element.40, bf16[2,4096,64]{2,1,0:T(8,128)(2,1)} %get-tuple-element.39, bf16[2,8,64]{2,1,0:T(8,128)(2,1)S(1)} %bitcast.57, bf16[2,8,64]{2,1,0:T(8,128)(2,1)S(1)} %bitcast.56), kind=kOutput, calls=%fused_computation.50 | convolution fusion | flops 21176304 | bytes 2371648 | tf_op jit(solution)/shard_map/rgjd,rgsd->rgjs/dot_general | solution.py:144
  35.0 17.8 %all_to_all.20 = bf16[32,2,1024]{2,1,0:T(2,128)(2,1)S(1)} all-to-all(bf16[32,2,1024]{2,1,0:T(2,128)(2,1)S(1)} %broadcast_in_dim.206), channel_id=1, replica_groups=mesh['wide'=32,'narrow'=8] {'wide'}, dimensions={0} | all-to-all | bytes 262144 | tf_op jit(solution)/shard_map/all_to_all | solution.py:68
  53.1 2.8 %collective-permute-start = (f32[64,256]{1,0:T(8,128)S(1)}, f32[64,256]{1,0:T(8,128)S(1)}, u32[]{:S(2)}, u32[]{:S(2)}) collective-permute-start(f32[64,256]{1,0:T(8,128)S(1)} %fusion.76), channel_id=1, source_target_pairs={{0,1},{1,0},{2,3},{3,2},{4,5},{5,4},{6,7},{7,6},{8,9},{9,8},{10,11... | collective-permute-start | bytes 196616 | tf_op jit(solution)/shard_map/ppermute | solution.py:73
  55.9 0.9 collective-permute-done
  56.8 2.8 %collective-permute-start.3 = (f32[64,256]{1,0:T(8,128)S(1)}, f32[64,256]{1,0:T(8,128)S(1)}, u32[]{:S(2)}, u32[]{:S(2)}) collective-permute-start(f32[64,256]{1,0:T(8,128)S(1)} %add.395), channel_id=1, source_target_pairs={{0,6},{1,7},{2,0},{3,1},{4,2},{5,3},{6,4},{7,5},{8,14},{9,15},{10,... | collective-permute-start | bytes 196616 | tf_op jit(solution)/shard_map/ppermute | solution.py:77
  59.6 1.6 %collective-permute-start.1 = (f32[64,256]{1,0:T(8,128)S(1)}, f32[64,256]{1,0:T(8,128)S(1)}, u32[]{:S(2)}, u32[]{:S(2)}) collective-permute-start(f32[64,256]{1,0:T(8,128)S(1)} %add.395), channel_id=1, source_target_pairs={{0,4},{1,5},{2,6},{3,7},{4,0},{5,1},{6,2},{7,3},{8,12},{9,13},{10,... | collective-permute-start | bytes 196616 | tf_op jit(solution)/shard_map/ppermute | solution.py:77
  61.9 2.7 %collective-permute-done.2 = f32[64,256]{1,0:T(8,128)S(1)} collective-permute-done((f32[64,256]{1,0:T(8,128)S(1)}, f32[64,256]{1,0:T(8,128)S(1)}, u32[]{:S(2)}, u32[]{:S(2)}) %collective-permute-start.2) | collective-permute-done | bytes 65568 | tf_op jit(solution)/shard_map/ppermute | solution.py:77
  66.0 3.3 %convolution_convert_fusion = bf16[64,7392]{1,0:T(8,128)(2,1)S(1)} fusion(bf16[256,7392]{0,1:T(8,128)(2,1)} %bitcast.55, bf16[64,256]{1,0:T(8,128)(2,1)S(1)} %get-tuple-element.33, f32[256]{0:T(256)S(1)} %convert_element_type.231), kind=kOutput, calls=%fused_computation | convolution fusion | flops 242743296 | bytes 4764672 | tf_op jit(solution)/shard_map/dot_general | solution.py:179
  69.7 1.3 reshape.1020
  71.0 27.7 %all_to_all.21 = bf16[32,2,7394]{2,1,0:T(2,128)(2,1)S(1)} all-to-all(bf16[32,2,7394]{2,1,0:T(2,128)(2,1)} %reshape.1020), channel_id=1, replica_groups=mesh['wide'=32,'narrow'=8] {'wide'}, dimensions={0} | all-to-all | bytes 1892864 | tf_op jit(solution)/shard_map/all_to_all | solution.py:186
  98.7 0.8 convert_reduce_fusion
  100.2 20.1 %all_to_all.22 = bf16[32,2,3696]{2,1,0:T(2,128)(2,1)S(1)} all-to-all(bf16[32,2,3696]{2,1,0:T(2,128)(2,1)S(1)} %broadcast_in_dim.207), channel_id=1, replica_groups=mesh['wide'=32,'narrow'=8] {'wide'}, dimensions={0} | all-to-all | bytes 946176 | tf_op jit(solution)/shard_map/all_to_all | solution.py:68
  120.6 2.0 %fusion.77 = f32[64,256]{1,0:T(8,128)S(1)} fusion(bf16[64,3696]{1,0:T(8,128)(2,1)S(1)} %reshape.1021, bf16[3696,256]{1,0:T(8,128)(2,1)} %param.27), kind=kOutput, calls=%fused_computation.149 | convolution fusion | flops 121110528 | bytes 2430976 | tf_op jit(solution)/shard_map/dot_general | solution.py:196
  122.6 4.1 %collective-permute-start.4 = (f32[64,256]{1,0:T(8,128)S(1)}, f32[64,256]{1,0:T(8,128)S(1)}, u32[]{:S(2)}, u32[]{:S(2)}) collective-permute-start(f32[64,256]{1,0:T(8,128)S(1)} %fusion.77), channel_id=1, source_target_pairs={{0,1},{1,0},{2,3},{3,2},{4,5},{5,4},{6,7},{7,6},{8,9},{9,8},{10,11... | collective-permute-start | bytes 196616 | tf_op jit(solution)/shard_map/ppermute | solution.py:73
  126.7 0.9 collective-permute-done.4
  127.6 1.9 %collective-permute-start.7 = (f32[64,256]{1,0:T(8,128)S(1)}, f32[64,256]{1,0:T(8,128)S(1)}, u32[]{:S(2)}, u32[]{:S(2)}) collective-permute-start(f32[64,256]{1,0:T(8,128)S(1)} %add.403), channel_id=1, source_target_pairs={{0,6},{1,7},{2,0},{3,1},{4,2},{5,3},{6,4},{7,5},{8,14},{9,15},{10,... | collective-permute-start | bytes 196616 | tf_op jit(solution)/shard_map/ppermute | solution.py:77
  129.5 1.3 collective-permute-start.5
  130.9 5.0 %collective-permute-done.6 = f32[64,256]{1,0:T(8,128)S(1)} collective-permute-done((f32[64,256]{1,0:T(8,128)S(1)}, f32[64,256]{1,0:T(8,128)S(1)}, u32[]{:S(2)}, u32[]{:S(2)}) %collective-permute-start.6) | collective-permute-done | bytes 65568 | tf_op jit(solution)/shard_map/ppermute | solution.py:77
  (71 shorter events, 7.7 us)
Async XLA Ops:
  0.0 34.4 %copy-start = (bf16[2,1,4096,128]{3,2,1,0:T(8,128)(2,1)S(1)}, bf16[2,1,4096,128]{3,2,1,0:T(8,128)(2,1)}, u32[]{:S(2)}) copy-start(bf16[2,1,4096,128]{3,2,1,0:T(8,128)(2,1)} %param.21) | copy-start | bytes 6291460
  0.0 16.4 %copy-start.5 = (s32[2]{0:T(128)S(1)}, s32[2]{0:T(128)}, u32[]{:S(2)}) copy-start(s32[2]{0:T(128)} %param.23) | copy-start | bytes 28
  0.0 16.5 %copy-start.3 = (s32[2,3,4096]{2,0,1:T(2,128)S(1)}, s32[2,3,4096]{2,0,1:T(2,128)}, u32[]{:S(2)}) copy-start(s32[2,3,4096]{2,0,1:T(2,128)} %param.22) | copy-start | bytes 294916
  4.5 25.2 %all-to-all-start = ((f32[32,2,1281]{2,1,0:T(2,128)}), f32[32,2,1281]{2,1,0:T(2,128)S(1)}, u32[]{:S(2)}, u32[]{:S(2)}) async-start(f32[32,2,1281]{2,1,0:T(2,128)} %pad_maximum_fusion), calls=%async_computation | async-start | bytes 720896 | tf_op jit(solution)/shard_map/all_to_all | solution.py:62
  17.0 12.1 %copy-start.4 = (bf16[1,10,128]{2,1,0:T(8,128)(2,1)S(1)}, bf16[1,10,128]{2,1,0:T(8,128)(2,1)}, u32[]{:S(2)}) copy-start(bf16[1,10,128]{2,1,0:T(8,128)(2,1)} %param.19) | copy-start | bytes 7684
  30.6 22.3 %copy-start.1 = (bf16[1024,256]{1,0:T(8,128)(2,1)S(1)}, bf16[1024,256]{1,0:T(8,128)(2,1)}, u32[]{:S(2)}) copy-start(bf16[1024,256]{1,0:T(8,128)(2,1)} %param.24) | copy-start | bytes 1572868
  30.6 30.7 %copy-start.6 = (bf16[256]{0:T(256)(128)(2,1)S(1)}, bf16[256]{0:T(256)(128)(2,1)}, u32[]{:S(2)}) copy-start(bf16[256]{0:T(256)(128)(2,1)} %param.25) | copy-start | bytes 1540
  30.6 34.5 %copy-start.2 = (bf16[64,256]{1,0:T(8,128)(2,1)S(1)}, bf16[64,256]{1,0:T(8,128)(2,1)}, u32[]{:S(2)}) copy-start(bf16[64,256]{1,0:T(8,128)(2,1)} %param.16) | copy-start | bytes 98308
  53.1 3.7 %collective-permute-start = (f32[64,256]{1,0:T(8,128)S(1)}, f32[64,256]{1,0:T(8,128)S(1)}, u32[]{:S(2)}, u32[]{:S(2)}) collective-permute-start(f32[64,256]{1,0:T(8,128)S(1)} %fusion.76), channel_id=1, source_target_pairs={{0,1},{1,0},{2,3},{3,2},{4,5},{5,4},{6,7},{7,6},{8,9},{9,8},{10,11... | collective-permute-start | bytes 196616 | tf_op jit(solution)/shard_map/ppermute | solution.py:73
  56.8 5.1 %collective-permute-start.3 = (f32[64,256]{1,0:T(8,128)S(1)}, f32[64,256]{1,0:T(8,128)S(1)}, u32[]{:S(2)}, u32[]{:S(2)}) collective-permute-start(f32[64,256]{1,0:T(8,128)S(1)} %add.395), channel_id=1, source_target_pairs={{0,6},{1,7},{2,0},{3,1},{4,2},{5,3},{6,4},{7,5},{8,14},{9,15},{10,... | collective-permute-start | bytes 196616 | tf_op jit(solution)/shard_map/ppermute | solution.py:77
  59.6 5.0 %collective-permute-start.2 = (f32[64,256]{1,0:T(8,128)S(1)}, f32[64,256]{1,0:T(8,128)S(1)}, u32[]{:S(2)}, u32[]{:S(2)}) collective-permute-start(f32[64,256]{1,0:T(8,128)S(1)} %add.395), channel_id=1, source_target_pairs={{0,2},{1,3},{2,4},{3,5},{4,6},{5,7},{6,0},{7,1},{8,10},{9,11},{10,... | collective-permute-start | bytes 196616 | tf_op jit(solution)/shard_map/ppermute | solution.py:77
  59.6 5.5 %collective-permute-start.1 = (f32[64,256]{1,0:T(8,128)S(1)}, f32[64,256]{1,0:T(8,128)S(1)}, u32[]{:S(2)}, u32[]{:S(2)}) collective-permute-start(f32[64,256]{1,0:T(8,128)S(1)} %add.395), channel_id=1, source_target_pairs={{0,4},{1,5},{2,6},{3,7},{4,0},{5,1},{6,2},{7,3},{8,12},{9,13},{10,... | collective-permute-start | bytes 196616 | tf_op jit(solution)/shard_map/ppermute | solution.py:77
  122.6 5.0 %collective-permute-start.4 = (f32[64,256]{1,0:T(8,128)S(1)}, f32[64,256]{1,0:T(8,128)S(1)}, u32[]{:S(2)}, u32[]{:S(2)}) collective-permute-start(f32[64,256]{1,0:T(8,128)S(1)} %fusion.77), channel_id=1, source_target_pairs={{0,1},{1,0},{2,3},{3,2},{4,5},{5,4},{6,7},{7,6},{8,9},{9,8},{10,11... | collective-permute-start | bytes 196616 | tf_op jit(solution)/shard_map/ppermute | solution.py:73
  127.6 3.3 %collective-permute-start.7 = (f32[64,256]{1,0:T(8,128)S(1)}, f32[64,256]{1,0:T(8,128)S(1)}, u32[]{:S(2)}, u32[]{:S(2)}) collective-permute-start(f32[64,256]{1,0:T(8,128)S(1)} %add.403), channel_id=1, source_target_pairs={{0,6},{1,7},{2,0},{3,1},{4,2},{5,3},{6,4},{7,5},{8,14},{9,15},{10,... | collective-permute-start | bytes 196616 | tf_op jit(solution)/shard_map/ppermute | solution.py:77
  129.5 6.3 %collective-permute-start.6 = (f32[64,256]{1,0:T(8,128)S(1)}, f32[64,256]{1,0:T(8,128)S(1)}, u32[]{:S(2)}, u32[]{:S(2)}) collective-permute-start(f32[64,256]{1,0:T(8,128)S(1)} %add.403), channel_id=1, source_target_pairs={{0,2},{1,3},{2,4},{3,5},{4,6},{5,7},{6,0},{7,1},{8,10},{9,11},{10,... | collective-permute-start | bytes 196616 | tf_op jit(solution)/shard_map/ppermute | solution.py:77
  129.5 6.3 %collective-permute-start.5 = (f32[64,256]{1,0:T(8,128)S(1)}, f32[64,256]{1,0:T(8,128)S(1)}, u32[]{:S(2)}, u32[]{:S(2)}) collective-permute-start(f32[64,256]{1,0:T(8,128)S(1)} %add.403), channel_id=1, source_target_pairs={{0,4},{1,5},{2,6},{3,7},{4,0},{5,1},{6,2},{7,3},{8,12},{9,13},{10,... | collective-permute-start | bytes 196616 | tf_op jit(solution)/shard_map/ppermute | solution.py:77

commit v11 on v10

--- a/solution.py
+++ b/solution.py
@@ -70,18 +70,27 @@
 
 def sum_all(x, axis):
     n = lax.axis_size(axis)
-    x = x + lax.ppermute(x, axis, [(i, i ^ 1) for i in range(n)])
+
+    def sent(v):
+        return v.astype(jnp.bfloat16)
+
+    def exchange(v, pairs):
+        return lax.ppermute(v, axis, pairs).astype(jnp.float32)
+
+    own = sent(x)
+    x = own.astype(jnp.float32) + exchange(own, [(i, i ^ 1) for i in range(n)])
     groups = n // 2
     if groups == 4:
+        own = sent(x)
+
         def shifted(k):
-            return lax.ppermute(
-                x, axis, [(i, ((i // 2 + k) % groups) * 2 + i % 2) for i in range(n)]
-            )
-
-        return (x + shifted(2)) + (shifted(1) + shifted(3))
+            return exchange(own, [(i, ((i // 2 + k) % groups) * 2 + i % 2) for i in range(n)])
+
+        return (own.astype(jnp.float32) + shifted(2)) + (shifted(1) + shifted(3))
     step = 2
     while step < n:
-        x = x + lax.ppermute(x, axis, [(i, i ^ step) for i in range(n)])
+        own = sent(x)
+        x = own.astype(jnp.float32) + exchange(own, [(i, i ^ step) for i in range(n)])
         step *= 2
     return x
 

time: 137 us -> 135 us (0.985)
  waiting for transfers between devices: 10.6 us -> 7.4 us
    ppermute x8, waiting for transfers between devices: 10 us -> 6.86 us  [exchange(): return lax.ppermute(v, axis, pairs).astype(jnp.float32)]
where the time goes in v11:
time: 135 us; the launch traced here: 134 us
  blocking collectives  65.6 us (49%)
  starting transfers between devices  27.2 us (20%)
  other arithmetic  19.3 us (14%)
  matrix products  10.9 us (8%)
  waiting for transfers between devices  7.4 us (5%)
  local copies, waits for them, and re-layouts  3.41 us (3%)
    all_to_all x2, blocking collectives, gather_rows(): lax.all_to_all(copies, axis, 0, 0, tiled=False)  37.9 us
    all_to_all x1, blocking collectives, local(): lax.all_to_all(sent2.reshape(n_wide, sent2.shape[0] // n_wide, sent2.shap...  27.7 us
    ppermute x8, starting transfers between devices, exchange(): return lax.ppermute(v, axis, pairs).astype(jnp.float32)  15.3 us
    concatenate x1, other arithmetic, local(): jnp.concatenate([keys_lead * cos_keys - keys_trail * sin_keys, keys_trail...  12 us
    all_to_all x1, starting transfers between devices, reduce_rows(): return jnp.sum(lax.all_to_all(blocks, axis, 0, 0, tiled=False), axis=0)  11.9 us
    ppermute x8, waiting for transfers between devices, exchange(): return lax.ppermute(v, axis, pairs).astype(jnp.float32)  6.86 us
    dot_general x1, matrix products, local(): jnp.einsum('rgjd,rgsd->rgjs', query, keys_rot, preferred_element_type=jnp...  3.61 us
    dot_general x1, matrix products, local(): jnp.dot(scaled2, gate_up_flat, preferred_element_type=jnp.float32)  3.34 us
  transfers between devices with their start and end apart: 9, of which 7 were waited for; matrix products, arithmetic and copies ran while one was open for 10% of the time, Pallas kernels for 0%

profile of v11, /device:TPU:1, one launch (start us, length us, event | category | flops | bytes accessed | tf_op | source)
XLA Modules:
  0.0 134.1 jit_solution(9775375854051065963)
XLA Ops:
  0.0 0.8 convert_element_type.259
  0.8 0.9 fusion.41
  1.9 1.3 convolution_bitcast_fusion
  3.6 0.9 pad_maximum_fusion
  4.5 11.9 %all-to-all-start = ((f32[32,2,1281]{2,1,0:T(2,128)}), f32[32,2,1281]{2,1,0:T(2,128)S(1)}, u32[]{:S(2)}, u32[]{:S(2)}) async-start(f32[32,2,1281]{2,1,0:T(2,128)} %pad_maximum_fusion), calls=%async_computation | async-start | bytes 720896 | tf_op jit(solution)/shard_map/all_to_all | solution.py:62
  17.1 12.0 %fusion.15 = (bf16[2,4096,64]{2,1,0:T(8,128)(2,1)}, bf16[2,4096,64]{2,1,0:T(8,128)(2,1)}) fusion(bf16[2,1,4096,128]{3,2,0,1:T(8,128)(2,1)} %bitcast.54, f32[64]{0:T(128)S(1)} %multiply_exponential_fusion, f32[2,4096]{1,0:T(2,128)S(1)} %get-tuple-element.44, f32[2,4096]{1,0:T(2,128)S(1)} %get-tuple-element.45, pred[64]{0:T(512)(128)(4,1)S(1)} %get-tuple-element.56, ...), kind=kLoop, calls=%fused_computation.35 | loop fusion | flops 28311552 | bytes 4292992 | tf_op jit(solution)/shard_map/concatenate | solution.py:140
  30.6 3.6 %select_reduce_fusion = (f32[2,8]{1,0:T(2,128)S(1)}, f32[2,8,4096]{2,1,0:T(8,128)S(1)}) fusion(pred[2,4096]{1,0:T(4,128)(4,1)S(1)} %get-tuple-element.52, bf16[2,4096,64]{2,1,0:T(8,128)(2,1)} %get-tuple-element.40, bf16[2,4096,64]{2,1,0:T(8,128)(2,1)} %get-tuple-element.39, bf16[2,8,64]{2,1,0:T(8,128)(2,1)S(1)} %bitcast.57, bf16[2,8,64]{2,1,0:T(8,128)(2,1)S(1)} %bitcast.56), kind=kOutput, calls=%fused_computation.52 | convolution fusion | flops 21176304 | bytes 2371648 | tf_op jit(solution)/shard_map/rgjd,rgsd->rgjs/dot_general | solution.py:153
  35.0 17.8 %all_to_all.20 = bf16[32,2,1024]{2,1,0:T(2,128)(2,1)S(1)} all-to-all(bf16[32,2,1024]{2,1,0:T(2,128)(2,1)S(1)} %broadcast_in_dim.206), channel_id=1, replica_groups=mesh['wide'=32,'narrow'=8] {'wide'}, dimensions={0} | all-to-all | bytes 262144 | tf_op jit(solution)/shard_map/all_to_all | solution.py:68
  53.1 2.8 %collective-permute-start = (bf16[64,256]{1,0:T(8,128)(2,1)S(1)}, bf16[64,256]{1,0:T(8,128)(2,1)S(1)}, u32[]{:S(2)}, u32[]{:S(2)}) collective-permute-start(bf16[64,256]{1,0:T(8,128)(2,1)S(1)} %convolution_convert_fusion.1), channel_id=1, source_target_pairs={{0,1},{1,0},{2,3},{3,2},{4,5},{5,4},{6,7},{7,6},{8,9},{9,8},{10,11... | collective-permute-start | bytes 98312 | tf_op jit(solution)/shard_map/ppermute | solution.py:78
  55.9 0.9 collective-permute-done
  56.8 2.8 %collective-permute-start.3 = (bf16[64,256]{1,0:T(8,128)(2,1)S(1)}, bf16[64,256]{1,0:T(8,128)(2,1)S(1)}, u32[]{:S(2)}, u32[]{:S(2)}) collective-permute-start(bf16[64,256]{1,0:T(8,128)(2,1)S(1)} %add_convert_fusion.1), channel_id=1, source_target_pairs={{0,6},{1,7},{2,0},{3,1},{4,2},{5,3},{6,4},{7,5},{8,14},{9,15},{10,... | collective-permute-start | bytes 98312 | tf_op jit(solution)/shard_map/ppermute | solution.py:78
  59.6 1.6 %collective-permute-start.1 = (bf16[64,256]{1,0:T(8,128)(2,1)S(1)}, bf16[64,256]{1,0:T(8,128)(2,1)S(1)}, u32[]{:S(2)}, u32[]{:S(2)}) collective-permute-start(bf16[64,256]{1,0:T(8,128)(2,1)S(1)} %add_convert_fusion.1), channel_id=1, source_target_pairs={{0,4},{1,5},{2,6},{3,7},{4,0},{5,1},{6,2},{7,3},{8,12},{9,13},{10,... | collective-permute-start | bytes 98312 | tf_op jit(solution)/shard_map/ppermute | solution.py:78
  61.9 1.7 %collective-permute-done.2 = bf16[64,256]{1,0:T(8,128)(2,1)S(1)} collective-permute-done((bf16[64,256]{1,0:T(8,128)(2,1)S(1)}, bf16[64,256]{1,0:T(8,128)(2,1)S(1)}, u32[]{:S(2)}, u32[]{:S(2)}) %collective-permute-start.2) | collective-permute-done | bytes 32800 | tf_op jit(solution)/shard_map/ppermute | solution.py:78
  64.9 3.3 %convolution_convert_fusion = bf16[64,7392]{1,0:T(8,128)(2,1)S(1)} fusion(bf16[256,7392]{0,1:T(8,128)(2,1)} %bitcast.55, bf16[64,256]{1,0:T(8,128)(2,1)S(1)} %get-tuple-element.33, f32[256]{0:T(256)S(1)} %convert_element_type.287), kind=kOutput, calls=%fused_computation | convolution fusion | flops 242743296 | bytes 4764672 | tf_op jit(solution)/shard_map/dot_general | solution.py:188
  68.6 1.3 reshape.1020
  69.9 27.7 %all_to_all.21 = bf16[32,2,7394]{2,1,0:T(2,128)(2,1)S(1)} all-to-all(bf16[32,2,7394]{2,1,0:T(2,128)(2,1)} %reshape.1020), channel_id=1, replica_groups=mesh['wide'=32,'narrow'=8] {'wide'}, dimensions={0} | all-to-all | bytes 1892864 | tf_op jit(solution)/shard_map/all_to_all | solution.py:195
  97.6 0.8 convert_reduce_fusion
  99.0 20.1 %all_to_all.22 = bf16[32,2,3696]{2,1,0:T(2,128)(2,1)S(1)} all-to-all(bf16[32,2,3696]{2,1,0:T(2,128)(2,1)S(1)} %broadcast_in_dim.207), channel_id=1, replica_groups=mesh['wide'=32,'narrow'=8] {'wide'}, dimensions={0} | all-to-all | bytes 946176 | tf_op jit(solution)/shard_map/all_to_all | solution.py:68
  119.5 2.0 %convolution_convert_fusion.2 = bf16[64,256]{1,0:T(8,128)(2,1)S(1)} fusion(bf16[64,3696]{1,0:T(8,128)(2,1)S(1)} %reshape.1021, bf16[3696,256]{1,0:T(8,128)(2,1)} %param.27), kind=kOutput, calls=%fused_computation.44 | convolution fusion | flops 121126912 | bytes 2398208 | tf_op jit(solution)/shard_map/dot_general | solution.py:205
  121.4 4.1 %collective-permute-start.4 = (bf16[64,256]{1,0:T(8,128)(2,1)S(1)}, bf16[64,256]{1,0:T(8,128)(2,1)S(1)}, u32[]{:S(2)}, u32[]{:S(2)}) collective-permute-start(bf16[64,256]{1,0:T(8,128)(2,1)S(1)} %convolution_convert_fusion.2), channel_id=1, source_target_pairs={{0,1},{1,0},{2,3},{3,2},{4,5},{5,4},{6,7},{7,6},{8,9},{9,8},{10,11... | collective-permute-start | bytes 98312 | tf_op jit(solution)/shard_map/ppermute | solution.py:78
  125.6 0.9 collective-permute-done.4
  126.5 2.6 %collective-permute-start.7 = (bf16[64,256]{1,0:T(8,128)(2,1)S(1)}, bf16[64,256]{1,0:T(8,128)(2,1)S(1)}, u32[]{:S(2)}, u32[]{:S(2)}) collective-permute-start(bf16[64,256]{1,0:T(8,128)(2,1)S(1)} %add_convert_fusion), channel_id=1, source_target_pairs={{0,6},{1,7},{2,0},{3,1},{4,2},{5,3},{6,4},{7,5},{8,14},{9,15},{10,... | collective-permute-start | bytes 98312 | tf_op jit(solution)/shard_map/ppermute | solution.py:78
  129.1 1.3 collective-permute-start.5
  130.4 2.7 %collective-permute-done.6 = bf16[64,256]{1,0:T(8,128)(2,1)S(1)} collective-permute-done((bf16[64,256]{1,0:T(8,128)(2,1)S(1)}, bf16[64,256]{1,0:T(8,128)(2,1)S(1)}, u32[]{:S(2)}, u32[]{:S(2)}) %collective-permute-start.6) | collective-permute-done | bytes 32800 | tf_op jit(solution)/shard_map/ppermute | solution.py:78
  (71 shorter events, 8.0 us)
Async XLA Ops:
  0.0 34.4 %copy-start = (bf16[2,1,4096,128]{3,2,1,0:T(8,128)(2,1)S(1)}, bf16[2,1,4096,128]{3,2,1,0:T(8,128)(2,1)}, u32[]{:S(2)}) copy-start(bf16[2,1,4096,128]{3,2,1,0:T(8,128)(2,1)} %param.21) | copy-start | bytes 6291460
  0.0 16.4 %copy-start.5 = (s32[2]{0:T(128)S(1)}, s32[2]{0:T(128)}, u32[]{:S(2)}) copy-start(s32[2]{0:T(128)} %param.23) | copy-start | bytes 28
  0.0 16.5 %copy-start.3 = (s32[2,3,4096]{2,0,1:T(2,128)S(1)}, s32[2,3,4096]{2,0,1:T(2,128)}, u32[]{:S(2)}) copy-start(s32[2,3,4096]{2,0,1:T(2,128)} %param.22) | copy-start | bytes 294916
  4.5 25.2 %all-to-all-start = ((f32[32,2,1281]{2,1,0:T(2,128)}), f32[32,2,1281]{2,1,0:T(2,128)S(1)}, u32[]{:S(2)}, u32[]{:S(2)}) async-start(f32[32,2,1281]{2,1,0:T(2,128)} %pad_maximum_fusion), calls=%async_computation | async-start | bytes 720896 | tf_op jit(solution)/shard_map/all_to_all | solution.py:62
  17.0 12.1 %copy-start.4 = (bf16[1,10,128]{2,1,0:T(8,128)(2,1)S(1)}, bf16[1,10,128]{2,1,0:T(8,128)(2,1)}, u32[]{:S(2)}) copy-start(bf16[1,10,128]{2,1,0:T(8,128)(2,1)} %param.19) | copy-start | bytes 7684
  30.6 22.3 %copy-start.1 = (bf16[1024,256]{1,0:T(8,128)(2,1)S(1)}, bf16[1024,256]{1,0:T(8,128)(2,1)}, u32[]{:S(2)}) copy-start(bf16[1024,256]{1,0:T(8,128)(2,1)} %param.24) | copy-start | bytes 1572868
  30.6 30.6 %copy-start.6 = (bf16[256]{0:T(256)(128)(2,1)S(1)}, bf16[256]{0:T(256)(128)(2,1)}, u32[]{:S(2)}) copy-start(bf16[256]{0:T(256)(128)(2,1)} %param.25) | copy-start | bytes 1540
  30.6 33.4 %copy-start.2 = (bf16[64,256]{1,0:T(8,128)(2,1)S(1)}, bf16[64,256]{1,0:T(8,128)(2,1)}, u32[]{:S(2)}) copy-start(bf16[64,256]{1,0:T(8,128)(2,1)} %param.16) | copy-start | bytes 98308
  53.1 3.7 %collective-permute-start = (bf16[64,256]{1,0:T(8,128)(2,1)S(1)}, bf16[64,256]{1,0:T(8,128)(2,1)S(1)}, u32[]{:S(2)}, u32[]{:S(2)}) collective-permute-start(bf16[64,256]{1,0:T(8,128)(2,1)S(1)} %convolution_convert_fusion.1), channel_id=1, source_target_pairs={{0,1},{1,0},{2,3},{3,2},{4,5},{5,4},{6,7},{7,6},{8,9},{9,8},{10,11... | collective-permute-start | bytes 98312 | tf_op jit(solution)/shard_map/ppermute | solution.py:78
  56.8 5.1 %collective-permute-start.3 = (bf16[64,256]{1,0:T(8,128)(2,1)S(1)}, bf16[64,256]{1,0:T(8,128)(2,1)S(1)}, u32[]{:S(2)}, u32[]{:S(2)}) collective-permute-start(bf16[64,256]{1,0:T(8,128)(2,1)S(1)} %add_convert_fusion.1), channel_id=1, source_target_pairs={{0,6},{1,7},{2,0},{3,1},{4,2},{5,3},{6,4},{7,5},{8,14},{9,15},{10,... | collective-permute-start | bytes 98312 | tf_op jit(solution)/shard_map/ppermute | solution.py:78
  59.6 4.0 %collective-permute-start.2 = (bf16[64,256]{1,0:T(8,128)(2,1)S(1)}, bf16[64,256]{1,0:T(8,128)(2,1)S(1)}, u32[]{:S(2)}, u32[]{:S(2)}) collective-permute-start(bf16[64,256]{1,0:T(8,128)(2,1)S(1)} %add_convert_fusion.1), channel_id=1, source_target_pairs={{0,2},{1,3},{2,4},{3,5},{4,6},{5,7},{6,0},{7,1},{8,10},{9,11},{10,... | collective-permute-start | bytes 98312 | tf_op jit(solution)/shard_map/ppermute | solution.py:78
  59.6 4.4 %collective-permute-start.1 = (bf16[64,256]{1,0:T(8,128)(2,1)S(1)}, bf16[64,256]{1,0:T(8,128)(2,1)S(1)}, u32[]{:S(2)}, u32[]{:S(2)}) collective-permute-start(bf16[64,256]{1,0:T(8,128)(2,1)S(1)} %add_convert_fusion.1), channel_id=1, source_target_pairs={{0,4},{1,5},{2,6},{3,7},{4,0},{5,1},{6,2},{7,3},{8,12},{9,13},{10,... | collective-permute-start | bytes 98312 | tf_op jit(solution)/shard_map/ppermute | solution.py:78
  121.4 5.0 %collective-permute-start.4 = (bf16[64,256]{1,0:T(8,128)(2,1)S(1)}, bf16[64,256]{1,0:T(8,128)(2,1)S(1)}, u32[]{:S(2)}, u32[]{:S(2)}) collective-permute-start(bf16[64,256]{1,0:T(8,128)(2,1)S(1)} %convolution_convert_fusion.2), channel_id=1, source_target_pairs={{0,1},{1,0},{2,3},{3,2},{4,5},{5,4},{6,7},{7,6},{8,9},{9,8},{10,11... | collective-permute-start | bytes 98312 | tf_op jit(solution)/shard_map/ppermute | solution.py:78
  126.5 3.9 %collective-permute-start.7 = (bf16[64,256]{1,0:T(8,128)(2,1)S(1)}, bf16[64,256]{1,0:T(8,128)(2,1)S(1)}, u32[]{:S(2)}, u32[]{:S(2)}) collective-permute-start(bf16[64,256]{1,0:T(8,128)(2,1)S(1)} %add_convert_fusion), channel_id=1, source_target_pairs={{0,6},{1,7},{2,0},{3,1},{4,2},{5,3},{6,4},{7,5},{8,14},{9,15},{10,... | collective-permute-start | bytes 98312 | tf_op jit(solution)/shard_map/ppermute | solution.py:78
  129.1 4.0 %collective-permute-start.6 = (bf16[64,256]{1,0:T(8,128)(2,1)S(1)}, bf16[64,256]{1,0:T(8,128)(2,1)S(1)}, u32[]{:S(2)}, u32[]{:S(2)}) collective-permute-start(bf16[64,256]{1,0:T(8,128)(2,1)S(1)} %add_convert_fusion), channel_id=1, source_target_pairs={{0,2},{1,3},{2,4},{3,5},{4,6},{5,7},{6,0},{7,1},{8,10},{9,11},{10,... | collective-permute-start | bytes 98312 | tf_op jit(solution)/shard_map/ppermute | solution.py:78
  129.1 4.3 %collective-permute-start.5 = (bf16[64,256]{1,0:T(8,128)(2,1)S(1)}, bf16[64,256]{1,0:T(8,128)(2,1)S(1)}, u32[]{:S(2)}, u32[]{:S(2)}) collective-permute-start(bf16[64,256]{1,0:T(8,128)(2,1)S(1)} %add_convert_fusion), channel_id=1, source_target_pairs={{0,4},{1,5},{2,6},{3,7},{4,0},{5,1},{6,2},{7,3},{8,12},{9,13},{10,... | collective-permute-start | bytes 98312 | tf_op jit(solution)/shard_map/ppermute | solution.py:78
